TPU v7x, 512 devices: a whole 4x4x16 slice. The times are simulated.
512 devices in a mesh: len: 32 (over z, core), xa: 4 (over y), xb: 4 (over x).
Axes of the slice: x: 4, y: 4, z: 16, core: 2. Of those that a mesh axis runs over, the one named last changes fastest.
Arguments:
- displacement: float32 [3, 4096, 4096], P(None, ('xa', 'xb'), 'len'), may hold values from -3 to 3
- velocity: float32 [3, 4096, 4096], P(None, ('xa', 'xb'), 'len'), may hold values from -6 to 6
- anchors: float32 [3, 4096], P(None, ('xa', 'xb')), may hold values from -0.5 to 0.5
- seg_live: int32 [4096, 32], P(('xa', 'xb'), 'len'), may hold values from 1 to 128
- pair_blocks: int32 [32, 16, 16, 32, 2], P('len', ('xa', 'xb')), may hold values from 0 to 255
- pair_count: int32 [32, 16, 16], P('len', ('xa', 'xb')), may hold values from 1 to 32, as said below
Outputs:
- new_velocity: float32 [3, 4096, 4096], P(None, ('xa', 'xb'), 'len')
- new_displacement: float32 [3, 4096, 4096], P(None, ('xa', 'xb'), 'len')
Inputs may be any that keep to these rules, and one draw needn't show every extreme that they name: `seg_live`: the first that many segments of a block take part in contact. `pair_blocks`: block numbers local to the device that holds the block. `pair_count`: live pairs from a device to a peer stand in the first slots of that peer's row; slots at or beyond the count hold arbitrary block numbers and carry no pair; the count 32 is reached in every draw.
All inputs are finite; a program needn't handle non-finite values.
Results may differ from a plain program's by a relative error of at most 0.0003.
Values sent between devices are 32-bit elements; how exact they have to be, the bound alone decides.
No kernel may reach another device: no remote copies, remote signals or barrier semaphores. Data moves between devices by JAX's collectives and lax.ppermute only.
A program may use at most 64 MiB of HBM per device.

v0:
```python
import jax
import jax.numpy as jnp
from jax import lax
from jax.experimental import pallas as pl
from jax.experimental.pallas import tpu as pltpu
from jax.sharding import PartitionSpec as P

spacing = 1.0 / 128.0
axial_stiff = 1.0
bend_stiff = 0.25
contact_stiff = 1.0 / 16.0
time_step = 0.2
damping = 0.9
masked_far = 1.0e4
HIGHEST = lax.Precision.HIGHEST


def padded_2(block, sides, width):
    for axis, dim in sides:
        count = lax.axis_size(axis)
        forward = [(i, i + 1) for i in range(count - 1)]
        backward = [(target, source) for source, target in forward]
        low = lax.ppermute(
            lax.slice_in_dim(block, block.shape[dim] - width, None, axis=dim), axis, forward
        )
        high = lax.ppermute(lax.slice_in_dim(block, 0, width, axis=dim), axis, backward)
        block = jnp.concatenate([low, block, high], axis=dim)
    return block


def chain_force(padded):
    center = padded[:, :, 2:-2]
    next_one = padded[:, :, 3:-1]
    prev_one = padded[:, :, 1:-3]
    next_two = padded[:, :, 4:]
    prev_two = padded[:, :, :-4]
    axial = next_one - 2.0 * center + prev_one
    bending = next_two - 4.0 * next_one + 6.0 * center - 4.0 * prev_one + prev_two
    return axial_stiff * axial - bend_stiff * bending


def pair_kernel(cnt_ref, mine_ref, m_ref, rd_ref, rq_ref, f1_ref, f2_ref):
    f1_ref[...] = jnp.zeros(f1_ref.shape, f1_ref.dtype)
    f2_ref[...] = jnp.zeros(f2_ref.shape, f2_ref.dtype)
    peers = cnt_ref.shape[0]
    cap = rd_ref.shape[0] // peers
    blocks = m_ref.shape[0]

    def peer(d, carry):
        live = jnp.clip(cnt_ref[d], 0, cap)

        def one(c, carry):
            slot = d * cap + c
            b = jnp.clip(mine_ref[slot], 0, blocks - 1)
            m = m_ref[b]
            rd = rd_ref[slot]
            rq = rq_ref[slot]
            dist = lax.dot_general(
                rd, m, (((0,), (0,)), ((), ())), precision=HIGHEST,
                preferred_element_type=jnp.float32,
            )
            w = jnp.exp(-dist) * contact_stiff
            f1 = lax.dot_general(
                rq, w, (((1,), (0,)), ((), ())), precision=HIGHEST,
                preferred_element_type=jnp.float32,
            )
            f2 = lax.dot_general(
                m, w, (((1,), (1,)), ((), ())), precision=HIGHEST,
                preferred_element_type=jnp.float32,
            )
            on_first = m * f1[3:4, :] - f1
            on_second = rq * f2[3:4, :] - f2
            f1_ref[b] = f1_ref[b] + on_first
            f2_ref[slot] = on_second[0:3, :]
            return carry

        return lax.fori_loop(0, live, one, carry)

    lax.fori_loop(0, peers, peer, 0)


def back_kernel(req_ref, f1_ref, ret_ref, out_ref):
    out_ref[...] = f1_ref[...]
    blocks = out_ref.shape[0]

    def one(s, carry):
        b = jnp.clip(req_ref[s], 0, blocks - 1)
        out_ref[b, 0:3, :] = out_ref[b, 0:3, :] + ret_ref[s]
        return carry

    lax.fori_loop(0, ret_ref.shape[0], one, 0)


def local(displacement, velocity, anchors, seg_live, pair_blocks, pair_count):
    seg_len = displacement.shape[2]
    fibre_count = displacement.shape[1]
    per_fibre = seg_len // 128
    block_total = fibre_count * per_fibre
    peer_total = pair_blocks.shape[2]
    slot_cap = pair_blocks.shape[3]
    slot_total = peer_total * slot_cap
    padded = padded_2(displacement, (("len", 2),), 2)
    beam = chain_force(padded)

    height = jnp.arange(seg_len, dtype=jnp.int32).astype(jnp.float32) * spacing
    lift = jnp.stack([jnp.zeros_like(height), jnp.zeros_like(height), height])
    positions = displacement + anchors[:, :, None] + lift[:, None, :]
    blocks = positions.reshape(3, block_total, 128).transpose(1, 0, 2)
    lanes = jnp.arange(128, dtype=jnp.int32)
    live = (lanes[None, :] < seg_live.reshape(block_total)[:, None]).astype(jnp.float32)
    norm = jnp.sum(blocks * blocks, axis=1)
    ones = jnp.ones_like(live)
    zero = jnp.zeros_like(live)
    mine_rows = jnp.stack(
        [blocks[:, 0], blocks[:, 1], blocks[:, 2], ones, norm, masked_far * (1.0 - live), ones, zero],
        axis=1,
    )
    lend_rows = jnp.stack([blocks[:, 0], blocks[:, 1], blocks[:, 2], live], axis=1)

    mine_ids = pair_blocks[0, 0, :, :, 0].reshape(slot_total)
    their_ids = pair_blocks[0, 0, :, :, 1]
    requested = lax.all_to_all(their_ids, ("xa", "xb"), split_axis=0, concat_axis=0, tiled=True)
    requested_flat = requested.reshape(slot_total)
    lent = lend_rows[requested_flat].reshape(peer_total, slot_cap, 4, 128)
    remote = lax.all_to_all(lent, ("xa", "xb"), split_axis=0, concat_axis=0, tiled=True)
    remote = remote.reshape(slot_total, 4, 128)
    q = remote[:, 0:3]
    rnorm = jnp.sum(q * q, axis=1)
    rlive = remote[:, 3]
    rones = jnp.ones_like(rlive)
    rzero = jnp.zeros_like(rlive)
    rd = jnp.stack(
        [-2.0 * q[:, 0], -2.0 * q[:, 1], -2.0 * q[:, 2], rnorm, rones, rones,
         masked_far * (1.0 - rlive), rzero],
        axis=1,
    )
    rq = jnp.stack([q[:, 0], q[:, 1], q[:, 2], rones, rzero, rzero, rzero, rzero], axis=1)

    smem = pl.BlockSpec(memory_space=pltpu.SMEM)
    vmem = pl.BlockSpec(memory_space=pltpu.VMEM)
    f1, f2 = pl.pallas_call(
        pair_kernel,
        out_shape=(
            jax.ShapeDtypeStruct((block_total, 8, 128), jnp.float32),
            jax.ShapeDtypeStruct((slot_total, 3, 128), jnp.float32),
        ),
        in_specs=[smem, smem, vmem, vmem, vmem],
        out_specs=(vmem, vmem),
    )(pair_count[0, 0], mine_ids, mine_rows, rd, rq)

    returned = lax.all_to_all(
        f2.reshape(peer_total, slot_cap, 3, 128), ("xa", "xb"), split_axis=0, concat_axis=0, tiled=True
    )
    acc = pl.pallas_call(
        back_kernel,
        out_shape=jax.ShapeDtypeStruct((block_total, 8, 128), jnp.float32),
        in_specs=[smem, vmem, vmem],
        out_specs=vmem,
    )(requested_flat, f1, returned.reshape(slot_total, 3, 128))
    contact = acc[:, 0:3, :].transpose(1, 0, 2).reshape(3, fibre_count, seg_len)
    new_velocity = damping * velocity + time_step * (beam + contact)
    new_displacement = displacement + time_step * new_velocity
    return (new_velocity, new_displacement)


def solution(mesh):
    in_specs = (
        P(None, ("xa", "xb"), "len"),
        P(None, ("xa", "xb"), "len"),
        P(None, ("xa", "xb")),
        P(("xa", "xb"), "len"),
        P("len", ("xa", "xb"), None, None, None),
        P("len", ("xa", "xb"), None),
    )
    out_specs = (P(None, ("xa", "xb"), "len"), P(None, ("xa", "xb"), "len"))
    return jax.shard_map(local, mesh=mesh, in_specs=in_specs, out_specs=out_specs, check_vma=False)
```

profile of v0, /device:TPU:131, one launch (start us, length us, event | category | flops | bytes accessed | tf_op | source)
XLA Modules:
  0.0 310.2 jit_solution(12906319432600245617)
XLA Ops:
  0.6 1.4 slice_reduce_fusion
  2.0 6.9 %all-to-all-start = ((s32[16,1,32]{2,1,0:T(1,128)}), s32[16,1,32]{2,1,0:T(1,128)S(1)}, u32[]{:S(2)}, u32[]{:S(2)}) async-start(s32[16,1,32]{2,1,0:T(1,128)} %get-tuple-element.31), calls=%async_computation | async-start | bytes 16384 | tf_op jit(solution)/shard_map/all_to_all | solution.py:122
  9.0 0.8 copy.75
  9.8 1.0 compare_convert_fusion
  10.8 1.6 multiply_reduce_fusion.1
  12.4 0.2 pad_maximum_fusion.1
  12.7 1.6 all-to-all-done
  14.2 0.1 reshape.136
  14.3 0.0 copy-start.2
  14.3 2.6 gather_fusion
  16.9 5.1 %all-to-all-start.1 = ((f32[16,32,4,128]{3,2,1,0:T(4,128)}), f32[16,32,4,128]{3,2,1,0:T(4,128)S(1)}, u32[]{:S(2)}, u32[]{:S(2)}) async-start(f32[16,32,4,128]{3,2,1,0:T(4,128)} %bitcast.7), calls=%async_computation.1 | async-start | bytes 2097152 | tf_op jit(solution)/shard_map/all_to_all | solution.py:125
  22.1 0.7 reshape_squeeze.3.mine_ref
  22.7 0.1 pad.3.clone
  22.8 0.0 copy-done.2
  22.8 0.3 subtract_multiply_fusion
  23.2 0.1 stack_broadcast_in_dim.7
  23.2 2.3 stack.38.m_ref
  25.5 10.9 %all-to-all-done.1 = f32[16,32,4,128]{3,2,1,0:T(4,128)S(1)} async-done(((f32[16,32,4,128]{3,2,1,0:T(4,128)}), f32[16,32,4,128]{3,2,1,0:T(4,128)S(1)}, u32[]{:S(2)}, u32[]{:S(2)}) %all-to-all-start.1) | async-done | bytes 1048608 | tf_op jit(solution)/shard_map/all_to_all | solution.py:125
  36.4 0.9 fusion.9
  37.4 0.8 fusion.11
  38.1 0.1 sub.35
  38.3 1.7 maximum_maximum_fusion.rq_ref
  40.0 0.1 stack_broadcast_in_dim.8
  40.2 0.1 stack.41
  40.3 4.4 %stack.42.rd_ref = f32[512,8,128]{2,1,0:T(8,128)} concatenate(f32[512,1,128]{2,1,0:T(1,128)S(1)} %get-tuple-element.25, f32[512,1,128]{2,1,0:T(1,128)S(1)} %get-tuple-element.24, f32[512,1,128]{2,1,0:T(1,128)S(1)} %get-tuple-element.23, f32[512,1,128]{2,1,0:T(1,128)S(1)} %bitcast.33, f32[512,2,128]{2,1,0:T(2,128)S(1)} %stack.41, f32[512,1,128]{2,1,0:T(1,128)S(1)} %get-tuple-element.22, ...), dimensions={1} | concatenate | bytes 4194304 | tf_op jit(solution)/shard_map/stack | solution.py:132
  44.8 55.1 %shard_map.80 = (f32[256,8,128]{2,1,0:T(8,128)}, f32[512,3,128]{2,1,0:T(4,128)}) custom-call(s32[16]{0:T(128)} %bitcast.40, s32[512]{0:T(512)} %reshape_squeeze.3.mine_ref, f32[256,8,128]{2,1,0:T(8,128)} %stack.38.m_ref, f32[512,8,128]{2,1,0:T(8,128)} %stack.42.rd_ref, f32[512,8,128]{2,1,0:T(8,128)} %maximum_maximum_fusion.rq_ref), custom_call_target="tpu_custom_call" | custom-call | tf_op jit(solution)/shard_map/pallas_call | solution.py:141
  99.8 0.0 copy-start
  99.8 2.3 copy.80
  102.1 132.8 %all-to-all-start.2 = ((f32[16,32,3,128]{3,1,2,0:T(8,128)}), f32[16,32,3,128]{3,1,2,0:T(8,128)S(1)}, u32[]{:S(2)}, u32[]{:S(2)}) async-start(f32[16,32,3,128]{3,1,2,0:T(8,128)} %copy.80), calls=%async_computation.2 | async-start | bytes 1572864 | tf_op jit(solution)/shard_map/all_to_all | solution.py:151
  234.9 0.0 copy-done
  234.9 0.3 copy_dynamic-update-slice_fusion
  235.3 1.3 fusion.12
  236.6 10.7 %collective-permute-start = (f32[3,256,2]{2,0,1:T(4,128)}, f32[3,256,2]{2,0,1:T(4,128)}, u32[]{:S(2)}, u32[]{:S(2)}) collective-permute-start(f32[3,256,2]{2,0,1:T(4,128)} %get-tuple-element.26), channel_id=1, source_target_pairs={{16,0},{32,16},{48,32},{64,48},{80,64},{96,80},{112,96},{128,112},... | collective-permute-start | bytes 18440 | tf_op jit(solution)/shard_map/ppermute | solution.py:26
  247.4 43.6 %collective-permute-start.1 = (f32[3,256,2]{2,0,1:T(4,128)}, f32[3,256,2]{2,0,1:T(4,128)S(1)}, u32[]{:S(2)}, u32[]{:S(2)}) collective-permute-start(f32[3,256,2]{2,0,1:T(4,128)} %get-tuple-element.27), channel_id=1, source_target_pairs={{0,16},{16,32},{32,48},{48,64},{64,80},{80,96},{96,112},{112,128},... | collective-permute-start | bytes 18440 | tf_op jit(solution)/shard_map/ppermute | solution.py:23
  291.0 0.5 broadcast.119
  291.5 0.7 reduce.9
  292.2 0.7 reshape.135.req_ref
  292.8 3.4 %collective-permute-done = f32[3,256,2]{2,0,1:T(4,128)} collective-permute-done((f32[3,256,2]{2,0,1:T(4,128)}, f32[3,256,2]{2,0,1:T(4,128)}, u32[]{:S(2)}, u32[]{:S(2)}) %collective-permute-start) | collective-permute-done | bytes 6176 | tf_op jit(solution)/shard_map/ppermute | solution.py:26
  296.2 1.2 constant_dynamic-update-slice_fusion
  297.4 0.0 all-to-all-done.2
  297.4 1.6 copy.81
  299.0 0.0 copy-start.1
  299.0 6.9 %shard_map.81 = f32[256,8,128]{2,1,0:T(8,128)} custom-call(s32[512]{0:T(512)} %reshape.135.req_ref, f32[256,8,128]{2,1,0:T(8,128)} %get-tuple-element.4.f1_ref, f32[512,3,128]{2,1,0:T(4,128)} %bitcast.29), custom_call_target="tpu_custom_call" | custom-call | tf_op jit(solution)/shard_map/pallas_call | solution.py:154
  306.0 0.0 collective-permute-done.1
  306.0 0.0 copy-done.1
  306.0 2.6 multiply_add_fusion
  308.6 0.8 copy.84
  309.4 0.8 copy.83
  (6 shorter events, 0.0 us)
Async XLA Ops:
  2.0 12.2 %all-to-all-start = ((s32[16,1,32]{2,1,0:T(1,128)}), s32[16,1,32]{2,1,0:T(1,128)S(1)}, u32[]{:S(2)}, u32[]{:S(2)}) async-start(s32[16,1,32]{2,1,0:T(1,128)} %get-tuple-element.31), calls=%async_computation | async-start | bytes 16384 | tf_op jit(solution)/shard_map/all_to_all | solution.py:122
  14.3 8.5 %copy-start.2 = (s32[256,1]{0,1:T(1,128)S(1)}, s32[256,1]{0,1:T(1,128)}, u32[]{:S(2)}) copy-start(s32[256,1]{0,1:T(1,128)} %param.9) | copy-start | bytes 3076
  16.9 19.5 %all-to-all-start.1 = ((f32[16,32,4,128]{3,2,1,0:T(4,128)}), f32[16,32,4,128]{3,2,1,0:T(4,128)S(1)}, u32[]{:S(2)}, u32[]{:S(2)}) async-start(f32[16,32,4,128]{3,2,1,0:T(4,128)} %bitcast.7), calls=%async_computation.1 | async-start | bytes 2097152 | tf_op jit(solution)/shard_map/all_to_all | solution.py:125
  99.8 135.1 %copy-start = (f32[3,256,128]{2,1,0:T(8,128)S(1)}, f32[3,256,128]{2,1,0:T(8,128)}, u32[]{:S(2)}) copy-start(f32[3,256,128]{2,1,0:T(8,128)} %param.6) | copy-start | bytes 1179652
  102.1 195.3 %all-to-all-start.2 = ((f32[16,32,3,128]{3,1,2,0:T(8,128)}), f32[16,32,3,128]{3,1,2,0:T(8,128)S(1)}, u32[]{:S(2)}, u32[]{:S(2)}) async-start(f32[16,32,3,128]{3,1,2,0:T(8,128)} %copy.80), calls=%async_computation.2 | async-start | bytes 1572864 | tf_op jit(solution)/shard_map/all_to_all | solution.py:151
  236.6 59.6 %collective-permute-start = (f32[3,256,2]{2,0,1:T(4,128)}, f32[3,256,2]{2,0,1:T(4,128)}, u32[]{:S(2)}, u32[]{:S(2)}) collective-permute-start(f32[3,256,2]{2,0,1:T(4,128)} %get-tuple-element.26), channel_id=1, source_target_pairs={{16,0},{32,16},{48,32},{64,48},{80,64},{96,80},{112,96},{128,112},... | collective-permute-start | bytes 18440 | tf_op jit(solution)/shard_map/ppermute | solution.py:26
  247.4 58.6 %collective-permute-start.1 = (f32[3,256,2]{2,0,1:T(4,128)}, f32[3,256,2]{2,0,1:T(4,128)S(1)}, u32[]{:S(2)}, u32[]{:S(2)}) collective-permute-start(f32[3,256,2]{2,0,1:T(4,128)} %get-tuple-element.27), channel_id=1, source_target_pairs={{0,16},{16,32},{32,48},{48,64},{64,80},{80,96},{96,112},{112,128},... | collective-permute-start | bytes 18440 | tf_op jit(solution)/shard_map/ppermute | solution.py:23
  299.0 7.0 %copy-start.1 = (f32[3,256,128]{2,1,0:T(8,128)S(1)}, f32[3,256,128]{2,1,0:T(8,128)}, u32[]{:S(2)}) copy-start(f32[3,256,128]{2,1,0:T(8,128)} %param.7) | copy-start | bytes 1179652
where the time goes:
time: 311 us; the launch traced here: 310 us
  starting transfers between devices  199 us (64%)
  Pallas kernels  62 us (20%)
  local copies, waits for them, and re-layouts  22.4 us (7%)
  waiting for transfers between devices  15.9 us (5%)
  other arithmetic  9.94 us (3%)
    all_to_all x1, starting transfers between devices, local(): lax.all_to_all(f2.reshape(peer_total, slot_cap, 3, 128), ('xa', 'xb'), sp...  133 us
    pallas_call x1, Pallas kernels, local(): pl.pallas_call(pair_kernel, out_shape=(jax.ShapeDtypeStruct((block_total,...  55.1 us
    ppermute x1, starting transfers between devices, padded_2(): lax.ppermute(lax.slice_in_dim(block, block.shape[dim] - width, None, axis...  43.6 us
    all_to_all x1, waiting for transfers between devices, local(): lax.all_to_all(lent, ('xa', 'xb'), split_axis=0, concat_axis=0, tiled=True)  10.9 us
    ppermute x1, starting transfers between devices, padded_2(): lax.ppermute(lax.slice_in_dim(block, 0, width, axis=dim), axis, backward)  10.7 us
    pallas_call x1, Pallas kernels, local(): pl.pallas_call(back_kernel, out_shape=jax.ShapeDtypeStruct((block_total,...  6.94 us
    all_to_all x1, starting transfers between devices, local(): lax.all_to_all(their_ids, ('xa', 'xb'), split_axis=0, concat_axis=0, tile...  6.92 us
  transfers between devices with their start and end apart: 5, of which 3 were waited for; matrix products, arithmetic and copies ran while one was open for 4% of the time, Pallas kernels for 2%

commit v1 on v0

--- a/solution.py
+++ b/solution.py
@@ -13,6 +13,8 @@
 damping = 0.9
 masked_far = 1.0e4
 HIGHEST = lax.Precision.HIGHEST
+HIGH = lax.Precision.HIGH
+tile_group = 8
 
 
 def padded_2(block, sides, width):
@@ -39,6 +41,22 @@
     return axial_stiff * axial - bend_stiff * bending
 
 
+def tile_pair(m, rd, rq):
+    dist = lax.dot_general(
+        rd, m, (((0,), (0,)), ((), ())), precision=HIGHEST, preferred_element_type=jnp.float32
+    )
+    w = jnp.exp(-dist)
+    f1 = lax.dot_general(
+        rq, w, (((1,), (0,)), ((), ())), precision=HIGH, preferred_element_type=jnp.float32
+    )
+    f2 = lax.dot_general(
+        m, w, (((1,), (1,)), ((), ())), precision=HIGH, preferred_element_type=jnp.float32
+    )
+    f1 = f1 * contact_stiff
+    f2 = f2 * contact_stiff
+    return m * f1[3:4, :] - f1, (rq * f2[3:4, :] - f2)[0:3, :]
+
+
 def pair_kernel(cnt_ref, mine_ref, m_ref, rd_ref, rq_ref, f1_ref, f2_ref):
     f1_ref[...] = jnp.zeros(f1_ref.shape, f1_ref.dtype)
     f2_ref[...] = jnp.zeros(f2_ref.shape, f2_ref.dtype)
@@ -49,32 +67,21 @@
     def peer(d, carry):
         live = jnp.clip(cnt_ref[d], 0, cap)
 
-        def one(c, carry):
-            slot = d * cap + c
-            b = jnp.clip(mine_ref[slot], 0, blocks - 1)
-            m = m_ref[b]
-            rd = rd_ref[slot]
-            rq = rq_ref[slot]
-            dist = lax.dot_general(
-                rd, m, (((0,), (0,)), ((), ())), precision=HIGHEST,
-                preferred_element_type=jnp.float32,
-            )
-            w = jnp.exp(-dist) * contact_stiff
-            f1 = lax.dot_general(
-                rq, w, (((1,), (0,)), ((), ())), precision=HIGHEST,
-                preferred_element_type=jnp.float32,
-            )
-            f2 = lax.dot_general(
-                m, w, (((1,), (1,)), ((), ())), precision=HIGHEST,
-                preferred_element_type=jnp.float32,
-            )
-            on_first = m * f1[3:4, :] - f1
-            on_second = rq * f2[3:4, :] - f2
-            f1_ref[b] = f1_ref[b] + on_first
-            f2_ref[slot] = on_second[0:3, :]
+        def group(g, carry):
+            done = []
+            for k in range(tile_group):
+                c = g * tile_group + k
+                slot = d * cap + c
+                b = jnp.clip(mine_ref[slot], 0, blocks - 1)
+                on_first, on_second = tile_pair(m_ref[b], rd_ref[slot], rq_ref[slot])
+                ok = c < live
+                done.append((b, slot, jnp.where(ok, on_first, 0.0), jnp.where(ok, on_second, 0.0)))
+            for b, slot, on_first, on_second in done:
+                f1_ref[b] = f1_ref[b] + on_first
+                f2_ref[slot] = on_second
             return carry
 
-        return lax.fori_loop(0, live, one, carry)
+        return lax.fori_loop(0, (live + tile_group - 1) // tile_group, group, carry)
 
     lax.fori_loop(0, peers, peer, 0)
 

time: 311 us -> 200 us (0.64)
  the two profiles are of different devices: /device:TPU:131 before, /device:TPU:227 now
where the time goes in v1:
time: 200 us; the launch traced here: 199 us
  Pallas kernels  105 us (52%)
  starting transfers between devices  45.1 us (23%)
  local copies, waits for them, and re-layouts  22.4 us (11%)
  waiting for transfers between devices  15.9 us (8%)
  other arithmetic  9.94 us (5%)
    pallas_call x1, Pallas kernels, local(): pl.pallas_call(pair_kernel, out_shape=(jax.ShapeDtypeStruct((block_total,...  98.4 us
    ppermute x1, starting transfers between devices, padded_2(): lax.ppermute(lax.slice_in_dim(block, block.shape[dim] - width, None, axis...  17.5 us
    all_to_all x1, waiting for transfers between devices, local(): lax.all_to_all(lent, ('xa', 'xb'), split_axis=0, concat_axis=0, tiled=True)  10.9 us
    ppermute x1, starting transfers between devices, padded_2(): lax.ppermute(lax.slice_in_dim(block, 0, width, axis=dim), axis, backward)  9.87 us
    pallas_call x1, Pallas kernels, local(): pl.pallas_call(back_kernel, out_shape=jax.ShapeDtypeStruct((block_total,...  6.94 us
    all_to_all x1, starting transfers between devices, local(): lax.all_to_all(their_ids, ('xa', 'xb'), split_axis=0, concat_axis=0, tile...  6.92 us
    all_to_all x1, starting transfers between devices, local(): lax.all_to_all(f2.reshape(peer_total, slot_cap, 3, 128), ('xa', 'xb'), sp...  5.7 us
    all_to_all x1, starting transfers between devices, local(): lax.all_to_all(lent, ('xa', 'xb'), split_axis=0, concat_axis=0, tiled=True)  5.12 us
  transfers between devices with their start and end apart: 5, of which 3 were waited for; matrix products, arithmetic and copies ran while one was open for 7% of the time, Pallas kernels for 3%

profile of v1, /device:TPU:227, one launch (start us, length us, event | category | flops | bytes accessed | tf_op | source)
XLA Modules:
  0.0 199.4 jit_solution(14967144535861536787)
XLA Ops:
  0.6 1.4 slice_reduce_fusion
  2.0 6.9 %all-to-all-start = ((s32[16,1,32]{2,1,0:T(1,128)}), s32[16,1,32]{2,1,0:T(1,128)S(1)}, u32[]{:S(2)}, u32[]{:S(2)}) async-start(s32[16,1,32]{2,1,0:T(1,128)} %get-tuple-element.31), calls=%async_computation | async-start | bytes 16384 | tf_op jit(solution)/shard_map/all_to_all | solution.py:129
  9.0 0.8 copy.75
  9.8 1.0 compare_convert_fusion
  10.8 1.6 multiply_reduce_fusion.1
  12.4 0.2 pad_maximum_fusion.1
  12.7 1.6 all-to-all-done
  14.2 0.1 reshape.136
  14.3 0.0 copy-start.2
  14.3 2.6 %gather_fusion = f32[512,4,128]{2,1,0:T(4,128)} fusion(f32[256,4,128]{2,1,0:T(4,128)S(1)} %pad_maximum_fusion.1, s32[1024]{0:T(1024)S(1)} %pad_clamp_fusion), kind=kCustom, calls=%fused_computation | custom fusion | bytes 2099200 | tf_op jit(solution)/shard_map/gather | solution.py:131
  16.9 5.1 %all-to-all-start.1 = ((f32[16,32,4,128]{3,2,1,0:T(4,128)}), f32[16,32,4,128]{3,2,1,0:T(4,128)S(1)}, u32[]{:S(2)}, u32[]{:S(2)}) async-start(f32[16,32,4,128]{3,2,1,0:T(4,128)} %bitcast.7), calls=%async_computation.1 | async-start | bytes 2097152 | tf_op jit(solution)/shard_map/all_to_all | solution.py:132
  22.1 0.7 reshape_squeeze.3.mine_ref
  22.7 0.1 pad.3.clone
  22.8 0.0 copy-done.2
  22.8 0.3 subtract_multiply_fusion
  23.2 0.1 stack_broadcast_in_dim.7
  23.2 2.3 %stack.38.m_ref = f32[256,8,128]{2,1,0:T(8,128)} concatenate(f32[256,3,128]{2,1,0:T(4,128)S(1)} %get-tuple-element.19, f32[256,1,128]{2,1,0:T(1,128)S(1)} %bitcast.31, f32[256,1,128]{2,1,0:T(1,128)S(1)} %bitcast.35, f32[256,1,128]{2,1,0:T(1,128)S(1)} %subtract_multiply_fusion, f32[256,1,128]{2,1,0:T(1,128)S(1)} %bitcast.32, f32[256,1,128]{2,1,0:T(1,128)S(1)} %stack_broadcast_in_dim.7), dimensions={1} | concatenate | bytes 2097152 | tf_op jit(solution)/shard_map/stack | solution.py:121
  25.5 10.9 %all-to-all-done.1 = f32[16,32,4,128]{3,2,1,0:T(4,128)S(1)} async-done(((f32[16,32,4,128]{3,2,1,0:T(4,128)}), f32[16,32,4,128]{3,2,1,0:T(4,128)S(1)}, u32[]{:S(2)}, u32[]{:S(2)}) %all-to-all-start.1) | async-done | bytes 1048608 | tf_op jit(solution)/shard_map/all_to_all | solution.py:132
  36.4 0.9 fusion.9
  37.4 0.8 fusion.11
  38.1 0.1 sub.35
  38.3 1.7 maximum_maximum_fusion.rq_ref
  40.0 0.1 stack_broadcast_in_dim.8
  40.2 0.1 stack.41
  40.3 4.4 %stack.42.rd_ref = f32[512,8,128]{2,1,0:T(8,128)} concatenate(f32[512,1,128]{2,1,0:T(1,128)S(1)} %get-tuple-element.25, f32[512,1,128]{2,1,0:T(1,128)S(1)} %get-tuple-element.24, f32[512,1,128]{2,1,0:T(1,128)S(1)} %get-tuple-element.23, f32[512,1,128]{2,1,0:T(1,128)S(1)} %bitcast.33, f32[512,2,128]{2,1,0:T(2,128)S(1)} %stack.41, f32[512,1,128]{2,1,0:T(1,128)S(1)} %get-tuple-element.22, ...), dimensions={1} | concatenate | bytes 4194304 | tf_op jit(solution)/shard_map/stack | solution.py:139
  44.8 98.4 %shard_map.80 = (f32[256,8,128]{2,1,0:T(8,128)}, f32[512,3,128]{2,1,0:T(4,128)}) custom-call(s32[16]{0:T(128)} %bitcast.40, s32[512]{0:T(512)} %reshape_squeeze.3.mine_ref, f32[256,8,128]{2,1,0:T(8,128)} %stack.38.m_ref, f32[512,8,128]{2,1,0:T(8,128)} %stack.42.rd_ref, f32[512,8,128]{2,1,0:T(8,128)} %maximum_maximum_fusion.rq_ref), custom_call_target="tpu_custom_call" | custom-call | tf_op jit(solution)/shard_map/pallas_call | solution.py:148
  143.2 0.0 copy-start
  143.2 2.3 %copy.80 = f32[16,32,3,128]{3,1,2,0:T(8,128)} copy(f32[16,32,3,128]{3,2,1,0:T(4,128)} %bitcast.34) | data formatting | bytes 1572864 | tf_op jit(solution)/shard_map/reshape | solution.py:159
  145.5 5.7 %all-to-all-start.2 = ((f32[16,32,3,128]{3,1,2,0:T(8,128)}), f32[16,32,3,128]{3,1,2,0:T(8,128)S(1)}, u32[]{:S(2)}, u32[]{:S(2)}) async-start(f32[16,32,3,128]{3,1,2,0:T(8,128)} %copy.80), calls=%async_computation.2 | async-start | bytes 1572864 | tf_op jit(solution)/shard_map/all_to_all | solution.py:158
  151.2 0.0 copy-done
  151.2 0.3 copy_dynamic-update-slice_fusion
  151.5 1.3 fusion.12
  152.9 9.9 %collective-permute-start = (f32[3,256,2]{2,0,1:T(4,128)}, f32[3,256,2]{2,0,1:T(4,128)}, u32[]{:S(2)}, u32[]{:S(2)}) collective-permute-start(f32[3,256,2]{2,0,1:T(4,128)} %get-tuple-element.26), channel_id=1, source_target_pairs={{16,0},{32,16},{48,32},{64,48},{80,64},{96,80},{112,96},{128,112},... | collective-permute-start | bytes 18440 | tf_op jit(solution)/shard_map/ppermute | solution.py:28
  162.7 17.5 %collective-permute-start.1 = (f32[3,256,2]{2,0,1:T(4,128)}, f32[3,256,2]{2,0,1:T(4,128)S(1)}, u32[]{:S(2)}, u32[]{:S(2)}) collective-permute-start(f32[3,256,2]{2,0,1:T(4,128)} %get-tuple-element.27), channel_id=1, source_target_pairs={{0,16},{16,32},{32,48},{48,64},{64,80},{80,96},{96,112},{112,128},... | collective-permute-start | bytes 18440 | tf_op jit(solution)/shard_map/ppermute | solution.py:25
  180.2 0.5 broadcast.119
  180.7 0.7 reduce.9
  181.4 0.7 reshape.135.req_ref
  182.1 3.4 %collective-permute-done = f32[3,256,2]{2,0,1:T(4,128)} collective-permute-done((f32[3,256,2]{2,0,1:T(4,128)}, f32[3,256,2]{2,0,1:T(4,128)}, u32[]{:S(2)}, u32[]{:S(2)}) %collective-permute-start) | collective-permute-done | bytes 6176 | tf_op jit(solution)/shard_map/ppermute | solution.py:28
  185.4 1.2 constant_dynamic-update-slice_fusion
  186.7 0.0 all-to-all-done.2
  186.7 1.6 copy.81
  188.3 0.0 copy-start.1
  188.3 6.9 %shard_map.81 = f32[256,8,128]{2,1,0:T(8,128)} custom-call(s32[512]{0:T(512)} %reshape.135.req_ref, f32[256,8,128]{2,1,0:T(8,128)} %get-tuple-element.4.f1_ref, f32[512,3,128]{2,1,0:T(4,128)} %bitcast.29), custom_call_target="tpu_custom_call" | custom-call | tf_op jit(solution)/shard_map/pallas_call | solution.py:161
  195.2 0.0 collective-permute-done.1
  195.2 0.0 copy-done.1
  195.2 2.6 %multiply_add_fusion = (f32[3,256,128]{2,0,1:T(4,128)S(1)}, f32[3,256,128]{2,0,1:T(4,128)S(1)}) fusion(f32[3,256,128]{2,1,0:T(8,128)S(1)} %copy-done, f32[256,8,128]{2,1,0:T(8,128)} %shard_map.81, f32[3,256,128]{2,0,1:T(4,128)S(1)} %get-tuple-element.29, f32[3,256,2]{2,0,1:T(4,128)S(1)} %collective-permute-done.1, ...), kind=kLoop, calls=%fused_computation.19 | loop fusion | flops 1966080 | bytes 3151872 | tf_op jit(solution)/shard_map/add | solution.py:169
  197.9 0.8 copy.84
  198.6 0.8 copy.83
  (6 shorter events, 0.0 us)
Async XLA Ops:
  2.0 12.2 %all-to-all-start = ((s32[16,1,32]{2,1,0:T(1,128)}), s32[16,1,32]{2,1,0:T(1,128)S(1)}, u32[]{:S(2)}, u32[]{:S(2)}) async-start(s32[16,1,32]{2,1,0:T(1,128)} %get-tuple-element.31), calls=%async_computation | async-start | bytes 16384 | tf_op jit(solution)/shard_map/all_to_all | solution.py:129
  14.3 8.5 %copy-start.2 = (s32[256,1]{0,1:T(1,128)S(1)}, s32[256,1]{0,1:T(1,128)}, u32[]{:S(2)}) copy-start(s32[256,1]{0,1:T(1,128)} %param.9) | copy-start | bytes 3076
  16.9 19.5 %all-to-all-start.1 = ((f32[16,32,4,128]{3,2,1,0:T(4,128)}), f32[16,32,4,128]{3,2,1,0:T(4,128)S(1)}, u32[]{:S(2)}, u32[]{:S(2)}) async-start(f32[16,32,4,128]{3,2,1,0:T(4,128)} %bitcast.7), calls=%async_computation.1 | async-start | bytes 2097152 | tf_op jit(solution)/shard_map/all_to_all | solution.py:132
  143.2 8.0 %copy-start = (f32[3,256,128]{2,1,0:T(8,128)S(1)}, f32[3,256,128]{2,1,0:T(8,128)}, u32[]{:S(2)}) copy-start(f32[3,256,128]{2,1,0:T(8,128)} %param.6) | copy-start | bytes 1179652
  145.5 41.2 %all-to-all-start.2 = ((f32[16,32,3,128]{3,1,2,0:T(8,128)}), f32[16,32,3,128]{3,1,2,0:T(8,128)S(1)}, u32[]{:S(2)}, u32[]{:S(2)}) async-start(f32[16,32,3,128]{3,1,2,0:T(8,128)} %copy.80), calls=%async_computation.2 | async-start | bytes 1572864 | tf_op jit(solution)/shard_map/all_to_all | solution.py:158
  152.9 32.6 %collective-permute-start = (f32[3,256,2]{2,0,1:T(4,128)}, f32[3,256,2]{2,0,1:T(4,128)}, u32[]{:S(2)}, u32[]{:S(2)}) collective-permute-start(f32[3,256,2]{2,0,1:T(4,128)} %get-tuple-element.26), channel_id=1, source_target_pairs={{16,0},{32,16},{48,32},{64,48},{80,64},{96,80},{112,96},{128,112},... | collective-permute-start | bytes 18440 | tf_op jit(solution)/shard_map/ppermute | solution.py:28
  162.7 32.5 %collective-permute-start.1 = (f32[3,256,2]{2,0,1:T(4,128)}, f32[3,256,2]{2,0,1:T(4,128)S(1)}, u32[]{:S(2)}, u32[]{:S(2)}) collective-permute-start(f32[3,256,2]{2,0,1:T(4,128)} %get-tuple-element.27), channel_id=1, source_target_pairs={{0,16},{16,32},{32,48},{48,64},{64,80},{80,96},{96,112},{112,128},... | collective-permute-start | bytes 18440 | tf_op jit(solution)/shard_map/ppermute | solution.py:25
  188.3 7.0 %copy-start.1 = (f32[3,256,128]{2,1,0:T(8,128)S(1)}, f32[3,256,128]{2,1,0:T(8,128)}, u32[]{:S(2)}) copy-start(f32[3,256,128]{2,1,0:T(8,128)} %param.7) | copy-start | bytes 1179652

commit v2 on v1

--- a/solution.py
+++ b/solution.py
@@ -15,6 +15,7 @@
 HIGHEST = lax.Precision.HIGHEST
 HIGH = lax.Precision.HIGH
 tile_group = 8
+balance_rounds = 3
 
 
 def padded_2(block, sides, width):
@@ -57,33 +58,68 @@
     return m * f1[3:4, :] - f1, (rq * f2[3:4, :] - f2)[0:3, :]
 
 
-def pair_kernel(cnt_ref, mine_ref, m_ref, rd_ref, rq_ref, f1_ref, f2_ref):
+def pair_kernel(
+    ka_ref, hl_ref, hh_ref, mine_ref, req_ref, m_ref, rd_ref, rq_ref, f1_ref, f2_ref, lb_ref, ls_ref
+):
     f1_ref[...] = jnp.zeros(f1_ref.shape, f1_ref.dtype)
     f2_ref[...] = jnp.zeros(f2_ref.shape, f2_ref.dtype)
-    peers = cnt_ref.shape[0]
-    cap = rd_ref.shape[0] // peers
+    peers = ka_ref.shape[0]
+    cap = mine_ref.shape[0] // peers
     blocks = m_ref.shape[0]
 
-    def peer(d, carry):
-        live = jnp.clip(cnt_ref[d], 0, cap)
-
-        def group(g, carry):
-            done = []
-            for k in range(tile_group):
-                c = g * tile_group + k
-                slot = d * cap + c
-                b = jnp.clip(mine_ref[slot], 0, blocks - 1)
-                on_first, on_second = tile_pair(m_ref[b], rd_ref[slot], rq_ref[slot])
-                ok = c < live
-                done.append((b, slot, jnp.where(ok, on_first, 0.0), jnp.where(ok, on_second, 0.0)))
-            for b, slot, on_first, on_second in done:
-                f1_ref[b] = f1_ref[b] + on_first
-                f2_ref[slot] = on_second
-            return carry
-
-        return lax.fori_loop(0, (live + tile_group - 1) // tile_group, group, carry)
-
-    lax.fori_loop(0, peers, peer, 0)
+    def listed(d, n):
+        def asked(c, n):
+            lb_ref[n] = jnp.clip(mine_ref[d * cap + c], 0, blocks - 1)
+            ls_ref[n] = d * 2 * cap + c
+            return n + 1
+
+        def held(c, n):
+            lb_ref[n] = jnp.clip(req_ref[d * cap + c], 0, blocks - 1)
+            ls_ref[n] = d * 2 * cap + cap + c
+            return n + 1
+
+        n = lax.fori_loop(0, jnp.clip(ka_ref[d], 0, cap), asked, n)
+        low = jnp.clip(hl_ref[d], 0, cap)
+        return lax.fori_loop(low, jnp.clip(hh_ref[d], low, cap), held, n)
+
+    total = lax.fori_loop(0, peers, listed, 0)
+    last = jnp.maximum(total - 1, 0)
+
+    def group(g, carry):
+        done = []
+        for k in range(tile_group):
+            t = g * tile_group + k
+            at = jnp.minimum(t, last)
+            b = lb_ref[at]
+            slot = ls_ref[at]
+            on_first, on_second = tile_pair(m_ref[b], rd_ref[slot], rq_ref[slot])
+            done.append((b, slot, jnp.where(t < total, on_first, 0.0), on_second))
+        for b, slot, on_first, on_second in done:
+            f1_ref[b] = f1_ref[b] + on_first
+            f2_ref[slot] = on_second
+        return carry
+
+    lax.fori_loop(0, (total + tile_group - 1) // tile_group, group, 0)
+
+
+def split_pairs(counts, cap):
+    peers = counts.shape[0]
+    whole = jnp.clip(counts, 0, cap)
+    share = whole.astype(jnp.float32)
+    eye = jnp.eye(peers, dtype=jnp.float32)
+    off = share * (1.0 - eye)
+    own = jnp.sum(share * eye, axis=1)
+    off_row = jnp.sum(off, axis=1)
+    level = jnp.sum(share) / peers
+    keep = jnp.ones((peers,), jnp.float32)
+    for _ in range(balance_rounds):
+        incoming = jnp.sum((1.0 - keep)[:, None] * off, axis=0)
+        target = jnp.maximum(level - incoming, 0.0)
+        keep = jnp.clip((target - own) / jnp.maximum(off_row, 1.0), 0.0, 1.0)
+    split = jnp.floor(keep[:, None] * share + 0.5).astype(jnp.int32)
+    split = jnp.clip(split, 0, whole)
+    diag = jnp.eye(peers, dtype=jnp.bool_)
+    return jnp.where(diag, whole, split), whole
 
 
 def back_kernel(req_ref, f1_ref, ret_ref, out_ref):
@@ -124,13 +160,13 @@
     )
     lend_rows = jnp.stack([blocks[:, 0], blocks[:, 1], blocks[:, 2], live], axis=1)
 
-    mine_ids = pair_blocks[0, 0, :, :, 0].reshape(slot_total)
+    mine_ids = pair_blocks[0, 0, :, :, 0]
     their_ids = pair_blocks[0, 0, :, :, 1]
     requested = lax.all_to_all(their_ids, ("xa", "xb"), split_axis=0, concat_axis=0, tiled=True)
-    requested_flat = requested.reshape(slot_total)
-    lent = lend_rows[requested_flat].reshape(peer_total, slot_cap, 4, 128)
+    lend_ids = jnp.concatenate([requested, mine_ids], axis=1).reshape(2 * slot_total)
+    lent = lend_rows[lend_ids].reshape(peer_total, 2 * slot_cap, 4, 128)
     remote = lax.all_to_all(lent, ("xa", "xb"), split_axis=0, concat_axis=0, tiled=True)
-    remote = remote.reshape(slot_total, 4, 128)
+    remote = remote.reshape(2 * slot_total, 4, 128)
     q = remote[:, 0:3]
     rnorm = jnp.sum(q * q, axis=1)
     rlive = remote[:, 3]
@@ -143,27 +179,37 @@
     )
     rq = jnp.stack([q[:, 0], q[:, 1], q[:, 2], rones, rzero, rzero, rzero, rzero], axis=1)
 
+    counts = lax.all_gather(pair_count[0, 0], ("xa", "xb"), axis=0, tiled=False)
+    split, whole = split_pairs(counts, slot_cap)
+    me = lax.axis_index(("xa", "xb"))
+    ask_keep = split[me]
+    hold_low = split[:, me]
+    hold_high = whole[:, me]
+
     smem = pl.BlockSpec(memory_space=pltpu.SMEM)
     vmem = pl.BlockSpec(memory_space=pltpu.VMEM)
     f1, f2 = pl.pallas_call(
         pair_kernel,
         out_shape=(
             jax.ShapeDtypeStruct((block_total, 8, 128), jnp.float32),
-            jax.ShapeDtypeStruct((slot_total, 3, 128), jnp.float32),
+            jax.ShapeDtypeStruct((2 * slot_total, 3, 128), jnp.float32),
         ),
-        in_specs=[smem, smem, vmem, vmem, vmem],
+        in_specs=[smem, smem, smem, smem, smem, vmem, vmem, vmem],
         out_specs=(vmem, vmem),
-    )(pair_count[0, 0], mine_ids, mine_rows, rd, rq)
+        scratch_shapes=[pltpu.SMEM((2 * slot_total,), jnp.int32), pltpu.SMEM((2 * slot_total,), jnp.int32)],
+    )(ask_keep, hold_low, hold_high, mine_ids.reshape(slot_total), requested.reshape(slot_total),
+      mine_rows, rd, rq)
 
     returned = lax.all_to_all(
-        f2.reshape(peer_total, slot_cap, 3, 128), ("xa", "xb"), split_axis=0, concat_axis=0, tiled=True
+        f2.reshape(peer_total, 2 * slot_cap, 3, 128), ("xa", "xb"), split_axis=0, concat_axis=0,
+        tiled=True,
     )
     acc = pl.pallas_call(
         back_kernel,
         out_shape=jax.ShapeDtypeStruct((block_total, 8, 128), jnp.float32),
         in_specs=[smem, vmem, vmem],
         out_specs=vmem,
-    )(requested_flat, f1, returned.reshape(slot_total, 3, 128))
+    )(lend_ids, f1, returned.reshape(2 * slot_total, 3, 128))
     contact = acc[:, 0:3, :].transpose(1, 0, 2).reshape(3, fibre_count, seg_len)
     new_velocity = damping * velocity + time_step * (beam + contact)
     new_displacement = displacement + time_step * new_velocity

time: 200 us -> 211 us (1.055)
  the two profiles are of different devices: /device:TPU:227 before, /device:TPU:321 now
where the time goes in v2:
time: 211 us; the launch traced here: 209 us
  Pallas kernels  85 us (40%)
  local copies, waits for them, and re-layouts  39 us (18%)
  blocking collectives  36.8 us (17%)
  starting transfers between devices  22.5 us (11%)
  other arithmetic  15 us (7%)
  waiting for transfers between devices  9.5 us (5%)
    pallas_call x1, Pallas kernels, local(): pl.pallas_call(pair_kernel, out_shape=(jax.ShapeDtypeStruct((block_total,...  73.3 us
    all_gather x1, blocking collectives, local(): counts = lax.all_gather(pair_count[0, 0], ('xa', 'xb'), axis=0, tiled=False)  36.8 us
    pallas_call x1, Pallas kernels, local(): pl.pallas_call(back_kernel, out_shape=jax.ShapeDtypeStruct((block_total,...  11.6 us
    another operation x3, local copies, waits for them, and re-layouts, local(): jnp.stack([-2.0 * q[:, 0], -2.0 * q[:, 1], -2.0 * q[:, 2], rnorm, rones,...  11.3 us
    gather x1, local copies, waits for them, and re-layouts, local(): lent = lend_rows[lend_ids].reshape(peer_total, 2 * slot_cap, 4, 128)  7.96 us
    all_to_all x1, starting transfers between devices, local(): lax.all_to_all(their_ids, ('xa', 'xb'), split_axis=0, concat_axis=0, tile...  6.75 us
    all_to_all x1, starting transfers between devices, local(): lax.all_to_all(f2.reshape(peer_total, 2 * slot_cap, 3, 128), ('xa', 'xb')...  5.87 us
    ppermute x1, waiting for transfers between devices, padded_2(): lax.ppermute(lax.slice_in_dim(block, 0, width, axis=dim), axis, backward)  4.39 us
  transfers between devices with their start and end apart: 5, of which 3 were waited for; matrix products, arithmetic and copies ran while one was open for 9% of the time, Pallas kernels for 6%

profile of v2, /device:TPU:321, one launch (start us, length us, event | category | flops | bytes accessed | tf_op | source)
XLA Modules:
  0.0 209.3 jit_solution(1429106193113233783)
XLA Ops:
  0.6 1.4 slice_bitcast_fusion.1
  2.0 6.8 %all-to-all-start = ((s32[16,1,32]{2,1,0:T(1,128)}), s32[16,1,32]{2,1,0:T(1,128)S(1)}, u32[]{:S(2)}, u32[]{:S(2)}) async-start(s32[16,1,32]{2,1,0:T(1,128)} %get-tuple-element.34), calls=%async_computation | async-start | bytes 16384 | tf_op jit(solution)/shard_map/all_to_all | solution.py:165
  8.8 0.8 copy.80
  9.6 1.0 compare_convert_fusion
  10.7 1.6 multiply_reduce_fusion.1
  12.3 0.2 pad_maximum_fusion.1
  12.5 2.6 %all-to-all-done = s32[16,1,32]{2,1,0:T(1,128)S(1)} async-done(((s32[16,1,32]{2,1,0:T(1,128)}), s32[16,1,32]{2,1,0:T(1,128)S(1)}, u32[]{:S(2)}, u32[]{:S(2)}) %all-to-all-start) | async-done | bytes 2080 | tf_op jit(solution)/shard_map/all_to_all | solution.py:165
  15.1 0.1 pad_add_fusion
  15.2 0.1 reshape.175
  15.3 8.0 %gather_fusion = f32[1024,4,128]{2,1,0:T(4,128)} fusion(f32[256,4,128]{2,1,0:T(4,128)S(1)} %pad_maximum_fusion.1, s32[1024]{0:T(1024)S(1)} %broadcast_clamp_fusion.1), kind=kCustom, calls=%fused_computation | custom fusion | bytes 4198400 | tf_op jit(solution)/shard_map/gather | solution.py:167
  23.3 0.0 copy-start.4
  23.3 0.0 copy-start.3
  23.3 4.2 %all-to-all-start.1 = ((f32[16,64,4,128]{3,2,1,0:T(4,128)}), f32[16,64,4,128]{3,2,1,0:T(4,128)S(1)}, u32[]{:S(2)}, u32[]{:S(2)}) async-start(f32[16,64,4,128]{3,2,1,0:T(4,128)} %bitcast.39), calls=%async_computation.1 | async-start | bytes 4194304 | tf_op jit(solution)/shard_map/all_to_all | solution.py:168
  27.5 0.7 reshape_squeeze.3.mine_ref
  28.1 0.0 copy-done.4
  28.1 36.8 %all-gather = s32[16,1,16]{2,1,0:T(1,128)S(1)} all-gather(s32[1,1,16]{2,1,0:T(1,128)S(1)} %copy-done.4), channel_id=2, replica_groups=mesh['len'=32,'xa'=4,'xb'=4] {'xa','xb'}, dimensions={0}, use_global_device_ids=true | all-gather | bytes 1088 | tf_op jit(solution)/shard_map/all_gather | solution.py:182
  64.9 0.7 fusion.10
  66.2 0.1 pad.3.clone
  66.3 0.0 copy-done.3
  66.3 0.3 subtract_multiply_fusion
  66.7 0.1 stack_broadcast_in_dim.7
  66.7 2.3 %stack.38.m_ref = f32[256,8,128]{2,1,0:T(8,128)} concatenate(f32[256,3,128]{2,1,0:T(4,128)S(1)} %get-tuple-element.23, f32[256,1,128]{2,1,0:T(1,128)S(1)} %bitcast.43, f32[256,1,128]{2,1,0:T(1,128)S(1)} %bitcast.45, f32[256,1,128]{2,1,0:T(1,128)S(1)} %subtract_multiply_fusion, f32[256,1,128]{2,1,0:T(1,128)S(1)} %bitcast.44, f32[256,1,128]{2,1,0:T(1,128)S(1)} %stack_broadcast_in_dim.7), dimensions={1} | concatenate | bytes 2097152 | tf_op jit(solution)/shard_map/stack | solution.py:157
  69.0 0.1 multiply_reduce_fusion.3
  69.1 0.1 multiply_reduce_fusion.2
  69.2 0.1 minimum_select_fusion
  69.3 0.8 dynamic-slice_reduce_fusion.1.hl_ref
  70.1 1.0 dynamic-slice_reduce_fusion.hh_ref
  71.1 0.5 fusion.11.ka_ref
  71.7 0.5 broadcast.191
  72.2 0.7 reduce.7
  72.9 0.7 reshape.174.req_ref
  73.5 0.0 all-to-all-done.1
  73.5 2.9 %fusion.4 = (f32[1024,1,128]{2,1,0:T(1,128)S(1)}, f32[1024,1,128]{2,1,0:T(1,128)}, f32[1024,1,128]{2,1,0:T(1,128)}, f32[1024,1,128]{2,1,0:T(1,128)}) fusion(f32[1024,4,128]{2,1,0:T(4,128)S(1)} %bitcast.36), kind=kLoop, calls=%fused_computation.11 | loop fusion | flops 655360 | bytes 4194304 | tf_op jit(solution)/shard_map/mul | solution.py:177
  76.5 1.5 fusion.14
  78.0 0.3 sub.113
  78.2 0.0 copy-start.1
  78.3 2.8 %maximum_maximum_fusion.rq_ref = f32[1024,8,128]{2,1,0:T(8,128)} fusion(f32[1024,1,128]{2,1,0:T(1,128)S(1)} %sub.113, f32[1024,3,128]{2,1,0:T(4,128)S(1)} %get-tuple-element.24, f32[8]{0:T(128)S(1)} %pad.3.clone), kind=kLoop, calls=%fused_computation.1 | loop fusion | flops 2097152 | bytes 6291488 | tf_op jit(solution)/shard_map/stack | solution.py:180
  81.0 0.3 stack.41
  81.3 0.3 stack_broadcast_in_dim.8
  81.6 0.0 copy-done.1
  81.6 10.8 %stack.42.rd_ref = f32[1024,8,128]{2,1,0:T(8,128)} concatenate(f32[1024,1,128]{2,1,0:T(1,128)} %get-tuple-element.29, f32[1024,1,128]{2,1,0:T(1,128)} %get-tuple-element.28, f32[1024,1,128]{2,1,0:T(1,128)S(1)} %copy-done.1, f32[1024,1,128]{2,1,0:T(1,128)S(1)} %bitcast.40, f32[1024,2,128]{2,1,0:T(2,128)S(1)} %stack.41, f32[1024,1,128]{2,1,0:T(1,128)S(1)} %get-tuple-element.26, ...), dimensions={1} | concatenate | bytes 8388608 | tf_op jit(solution)/shard_map/stack | solution.py:175
  92.3 73.3 %shard_map.80 = (f32[256,8,128]{2,1,0:T(8,128)}, f32[1024,3,128]{2,1,0:T(4,128)}) custom-call(s32[16]{0:T(128)} %fusion.11.ka_ref, s32[16]{0:T(128)} %dynamic-slice_reduce_fusion.1.hl_ref, s32[16]{0:T(128)} %dynamic-slice_reduce_fusion.hh_ref, s32[512]{0:T(512)} %reshape_squeeze.3.mine_ref, s32[512]{0:T(512)} %reshape.174.req_ref, ...), custom_call_target="tpu_custom_call" | custom-call | tf_op jit(solution)/shard_map/pallas_call | solution.py:191
  165.7 3.0 %copy.85 = f32[16,64,3,128]{3,1,2,0:T(8,128)} copy(f32[16,64,3,128]{3,2,1,0:T(4,128)} %bitcast.41) | data formatting | bytes 3145728 | tf_op jit(solution)/shard_map/reshape | solution.py:204
  168.6 0.0 copy-start
  168.6 5.9 %all-to-all-start.2 = ((f32[16,64,3,128]{3,1,2,0:T(8,128)}), f32[16,64,3,128]{3,1,2,0:T(8,128)S(1)}, u32[]{:S(2)}, u32[]{:S(2)}) async-start(f32[16,64,3,128]{3,1,2,0:T(8,128)} %copy.85), calls=%async_computation.2 | async-start | bytes 3145728 | tf_op jit(solution)/shard_map/all_to_all | solution.py:203
  174.5 0.0 copy-done
  174.5 0.3 copy_dynamic-update-slice_fusion
  174.9 1.3 fusion.15
  176.2 1.9 collective-permute-start
  178.1 3.8 %collective-permute-start.1 = (f32[3,256,2]{2,0,1:T(4,128)}, f32[3,256,2]{2,0,1:T(4,128)}, u32[]{:S(2)}, u32[]{:S(2)}) collective-permute-start(f32[3,256,2]{2,0,1:T(4,128)} %get-tuple-element.31), channel_id=1, source_target_pairs={{0,16},{16,32},{32,48},{48,64},{64,80},{80,96},{96,112},{112,128},... | collective-permute-start | bytes 18440 | tf_op jit(solution)/shard_map/ppermute | solution.py:26
  181.9 0.7 reshape.173.req_ref
  182.6 4.4 %collective-permute-done = f32[3,256,2]{2,0,1:T(4,128)} collective-permute-done((f32[3,256,2]{2,0,1:T(4,128)}, f32[3,256,2]{2,0,1:T(4,128)}, u32[]{:S(2)}, u32[]{:S(2)}) %collective-permute-start) | collective-permute-done | bytes 6176 | tf_op jit(solution)/shard_map/ppermute | solution.py:29
  187.0 1.2 constant_dynamic-update-slice_fusion
  188.2 2.5 %all-to-all-done.2 = f32[16,64,3,128]{3,1,2,0:T(8,128)S(1)} async-done(((f32[16,64,3,128]{3,1,2,0:T(8,128)}), f32[16,64,3,128]{3,1,2,0:T(8,128)S(1)}, u32[]{:S(2)}, u32[]{:S(2)}) %all-to-all-start.2) | async-done | bytes 1572896 | tf_op jit(solution)/shard_map/all_to_all | solution.py:203
  190.7 2.4 %copy.86 = f32[16,64,3,128]{3,2,1,0:T(4,128)} copy(f32[16,64,3,128]{3,1,2,0:T(8,128)S(1)} %all-to-all-done.2) | data formatting | bytes 3145728 | tf_op jit(solution)/shard_map/all_to_all | solution.py:203
  193.1 0.0 copy-start.2
  193.1 11.6 %shard_map.81 = f32[256,8,128]{2,1,0:T(8,128)} custom-call(s32[1024]{0:T(1024)} %reshape.173.req_ref, f32[256,8,128]{2,1,0:T(8,128)} %get-tuple-element.4.f1_ref, f32[1024,3,128]{2,1,0:T(4,128)} %bitcast.38), custom_call_target="tpu_custom_call" | custom-call | tf_op jit(solution)/shard_map/pallas_call | solution.py:207
  204.8 0.0 collective-permute-done.1
  204.8 0.0 copy-done.2
  204.8 2.9 %multiply_add_fusion = (f32[3,256,128]{2,0,1:T(4,128)S(1)}, f32[3,256,128]{2,0,1:T(4,128)S(1)}) fusion(f32[3,256,128]{2,1,0:T(8,128)S(1)} %copy-done, f32[256,8,128]{2,1,0:T(8,128)} %shard_map.81, f32[3,256,128]{2,0,1:T(4,128)S(1)} %get-tuple-element.33, f32[3,256,2]{2,0,1:T(4,128)} %collective-permute-done.1, ...), kind=kLoop, calls=%fused_computation.24 | loop fusion | flops 1966080 | bytes 3151872 | tf_op jit(solution)/shard_map/add | solution.py:215
  207.7 0.8 copy.88
  208.5 0.8 copy.89
  (10 shorter events, 0.1 us)
Async XLA Ops:
  2.0 13.1 %all-to-all-start = ((s32[16,1,32]{2,1,0:T(1,128)}), s32[16,1,32]{2,1,0:T(1,128)S(1)}, u32[]{:S(2)}, u32[]{:S(2)}) async-start(s32[16,1,32]{2,1,0:T(1,128)} %get-tuple-element.34), calls=%async_computation | async-start | bytes 16384 | tf_op jit(solution)/shard_map/all_to_all | solution.py:165
  23.3 4.8 %copy-start.4 = (s32[1,1,16]{2,1,0:T(1,128)S(1)}, s32[1,1,16]{2,1,0:T(1,128)}, u32[]{:S(2)}) copy-start(s32[1,1,16]{2,1,0:T(1,128)} %param.11) | copy-start | bytes 196
  23.3 43.0 %copy-start.3 = (s32[256,1]{0,1:T(1,128)S(1)}, s32[256,1]{0,1:T(1,128)}, u32[]{:S(2)}) copy-start(s32[256,1]{0,1:T(1,128)} %param.9) | copy-start | bytes 3076
  23.3 50.2 %all-to-all-start.1 = ((f32[16,64,4,128]{3,2,1,0:T(4,128)}), f32[16,64,4,128]{3,2,1,0:T(4,128)S(1)}, u32[]{:S(2)}, u32[]{:S(2)}) async-start(f32[16,64,4,128]{3,2,1,0:T(4,128)} %bitcast.39), calls=%async_computation.1 | async-start | bytes 4194304 | tf_op jit(solution)/shard_map/all_to_all | solution.py:168
  78.2 3.3 %copy-start.1 = (f32[1024,1,128]{2,1,0:T(1,128)S(1)}, f32[1024,1,128]{2,1,0:T(1,128)}, u32[]{:S(2)}) copy-start(f32[1024,1,128]{2,1,0:T(1,128)} %get-tuple-element.27) | copy-start | bytes 1572868
  168.6 5.9 %copy-start = (f32[3,256,128]{2,1,0:T(8,128)S(1)}, f32[3,256,128]{2,1,0:T(8,128)}, u32[]{:S(2)}) copy-start(f32[3,256,128]{2,1,0:T(8,128)} %param.6) | copy-start | bytes 1179652
  168.6 22.0 %all-to-all-start.2 = ((f32[16,64,3,128]{3,1,2,0:T(8,128)}), f32[16,64,3,128]{3,1,2,0:T(8,128)S(1)}, u32[]{:S(2)}, u32[]{:S(2)}) async-start(f32[16,64,3,128]{3,1,2,0:T(8,128)} %copy.85), calls=%async_computation.2 | async-start | bytes 3145728 | tf_op jit(solution)/shard_map/all_to_all | solution.py:203
  176.2 10.8 %collective-permute-start = (f32[3,256,2]{2,0,1:T(4,128)}, f32[3,256,2]{2,0,1:T(4,128)}, u32[]{:S(2)}, u32[]{:S(2)}) collective-permute-start(f32[3,256,2]{2,0,1:T(4,128)} %get-tuple-element.30), channel_id=1, source_target_pairs={{16,0},{32,16},{48,32},{64,48},{80,64},{96,80},{112,96},{128,112},... | collective-permute-start | bytes 18440 | tf_op jit(solution)/shard_map/ppermute | solution.py:29
  178.1 26.7 %collective-permute-start.1 = (f32[3,256,2]{2,0,1:T(4,128)}, f32[3,256,2]{2,0,1:T(4,128)}, u32[]{:S(2)}, u32[]{:S(2)}) collective-permute-start(f32[3,256,2]{2,0,1:T(4,128)} %get-tuple-element.31), channel_id=1, source_target_pairs={{0,16},{16,32},{32,48},{48,64},{64,80},{80,96},{96,112},{112,128},... | collective-permute-start | bytes 18440 | tf_op jit(solution)/shard_map/ppermute | solution.py:26
  193.1 11.6 %copy-start.2 = (f32[3,256,128]{2,1,0:T(8,128)S(1)}, f32[3,256,128]{2,1,0:T(8,128)}, u32[]{:S(2)}) copy-start(f32[3,256,128]{2,1,0:T(8,128)} %param.7) | copy-start | bytes 1179652

commit v3 on v2

--- a/solution.py
+++ b/solution.py
@@ -18,17 +18,15 @@
 balance_rounds = 3
 
 
-def padded_2(block, sides, width):
-    for axis, dim in sides:
-        count = lax.axis_size(axis)
-        forward = [(i, i + 1) for i in range(count - 1)]
-        backward = [(target, source) for source, target in forward]
-        low = lax.ppermute(
-            lax.slice_in_dim(block, block.shape[dim] - width, None, axis=dim), axis, forward
-        )
-        high = lax.ppermute(lax.slice_in_dim(block, 0, width, axis=dim), axis, backward)
-        block = jnp.concatenate([low, block, high], axis=dim)
-    return block
+def halos(block, axis, dim, width):
+    count = lax.axis_size(axis)
+    forward = [(i, i + 1) for i in range(count - 1)]
+    backward = [(target, source) for source, target in forward]
+    low = lax.ppermute(
+        lax.slice_in_dim(block, block.shape[dim] - width, None, axis=dim), axis, forward
+    )
+    high = lax.ppermute(lax.slice_in_dim(block, 0, width, axis=dim), axis, backward)
+    return low, high
 
 
 def chain_force(padded):
@@ -42,6 +40,21 @@
     return axial_stiff * axial - bend_stiff * bending
 
 
+def rows_of(x, near):
+    row = lax.broadcasted_iota(jnp.int32, (8, 128), 0)
+    v0, v1, v2, on = x[0:1], x[1:2], x[2:3], x[3:4]
+    norm = v0 * v0 + v1 * v1 + v2 * v2
+    far = masked_far * (1.0 - on)
+    pick = lambda r, v: jnp.where(row == r, jnp.broadcast_to(v, (8, 128)), 0.0)
+    if near:
+        return (pick(0, v0) + pick(1, v1) + pick(2, v2) + jnp.where((row == 3) | (row == 6), 1.0, 0.0)
+                + pick(4, norm) + pick(5, far))
+    rd = (pick(0, -2.0 * v0) + pick(1, -2.0 * v1) + pick(2, -2.0 * v2) + pick(3, norm)
+          + jnp.where((row == 4) | (row == 5), 1.0, 0.0) + pick(6, far))
+    rq = pick(0, v0) + pick(1, v1) + pick(2, v2) + jnp.where(row == 3, 1.0, 0.0)
+    return rd, rq
+
+
 def tile_pair(m, rd, rq):
     dist = lax.dot_general(
         rd, m, (((0,), (0,)), ((), ())), precision=HIGHEST, preferred_element_type=jnp.float32
@@ -59,7 +72,8 @@
 
 
 def pair_kernel(
-    ka_ref, hl_ref, hh_ref, mine_ref, req_ref, m_ref, rd_ref, rq_ref, f1_ref, f2_ref, lb_ref, ls_ref
+    ka_ref, hl_ref, hh_ref, mine_ref, req_ref, m_ref, rem_ref, low_ref, high_ref, f1_ref, f2_ref, lb_ref,
+    ls_ref,
 ):
     f1_ref[...] = jnp.zeros(f1_ref.shape, f1_ref.dtype)
     f2_ref[...] = jnp.zeros(f2_ref.shape, f2_ref.dtype)
@@ -92,7 +106,8 @@
             at = jnp.minimum(t, last)
             b = lb_ref[at]
             slot = ls_ref[at]
-            on_first, on_second = tile_pair(m_ref[b], rd_ref[slot], rq_ref[slot])
+            rd, rq = rows_of(rem_ref[slot], False)
+            on_first, on_second = tile_pair(rows_of(m_ref[b], True), rd, rq)
             done.append((b, slot, jnp.where(t < total, on_first, 0.0), on_second))
         for b, slot, on_first, on_second in done:
             f1_ref[b] = f1_ref[b] + on_first
@@ -131,7 +146,7 @@
         out_ref[b, 0:3, :] = out_ref[b, 0:3, :] + ret_ref[s]
         return carry
 
-    lax.fori_loop(0, ret_ref.shape[0], one, 0)
+    lax.fori_loop(0, ret_ref.shape[0], one, 0, unroll=8)
 
 
 def local(displacement, velocity, anchors, seg_live, pair_blocks, pair_count):
@@ -142,8 +157,8 @@
     peer_total = pair_blocks.shape[2]
     slot_cap = pair_blocks.shape[3]
     slot_total = peer_total * slot_cap
-    padded = padded_2(displacement, (("len", 2),), 2)
-    beam = chain_force(padded)
+    halo_low, halo_high = halos(displacement, "len", 2, 2)
+    beam = chain_force(jnp.concatenate([halo_low, displacement, halo_high], axis=2))
 
     height = jnp.arange(seg_len, dtype=jnp.int32).astype(jnp.float32) * spacing
     lift = jnp.stack([jnp.zeros_like(height), jnp.zeros_like(height), height])
@@ -151,35 +166,21 @@
     blocks = positions.reshape(3, block_total, 128).transpose(1, 0, 2)
     lanes = jnp.arange(128, dtype=jnp.int32)
     live = (lanes[None, :] < seg_live.reshape(block_total)[:, None]).astype(jnp.float32)
-    norm = jnp.sum(blocks * blocks, axis=1)
-    ones = jnp.ones_like(live)
-    zero = jnp.zeros_like(live)
-    mine_rows = jnp.stack(
-        [blocks[:, 0], blocks[:, 1], blocks[:, 2], ones, norm, masked_far * (1.0 - live), ones, zero],
-        axis=1,
-    )
     lend_rows = jnp.stack([blocks[:, 0], blocks[:, 1], blocks[:, 2], live], axis=1)
 
     mine_ids = pair_blocks[0, 0, :, :, 0]
     their_ids = pair_blocks[0, 0, :, :, 1]
-    requested = lax.all_to_all(their_ids, ("xa", "xb"), split_axis=0, concat_axis=0, tiled=True)
+    own_counts = jnp.broadcast_to(pair_count[0, 0][None, :], (peer_total, peer_total))
+    asked = lax.all_to_all(
+        jnp.concatenate([their_ids, own_counts], axis=1), ("xa", "xb"), split_axis=0, concat_axis=0,
+        tiled=True,
+    )
+    requested = asked[:, :slot_cap]
+    counts = asked[:, slot_cap:]
     lend_ids = jnp.concatenate([requested, mine_ids], axis=1).reshape(2 * slot_total)
     lent = lend_rows[lend_ids].reshape(peer_total, 2 * slot_cap, 4, 128)
     remote = lax.all_to_all(lent, ("xa", "xb"), split_axis=0, concat_axis=0, tiled=True)
     remote = remote.reshape(2 * slot_total, 4, 128)
-    q = remote[:, 0:3]
-    rnorm = jnp.sum(q * q, axis=1)
-    rlive = remote[:, 3]
-    rones = jnp.ones_like(rlive)
-    rzero = jnp.zeros_like(rlive)
-    rd = jnp.stack(
-        [-2.0 * q[:, 0], -2.0 * q[:, 1], -2.0 * q[:, 2], rnorm, rones, rones,
-         masked_far * (1.0 - rlive), rzero],
-        axis=1,
-    )
-    rq = jnp.stack([q[:, 0], q[:, 1], q[:, 2], rones, rzero, rzero, rzero, rzero], axis=1)
-
-    counts = lax.all_gather(pair_count[0, 0], ("xa", "xb"), axis=0, tiled=False)
     split, whole = split_pairs(counts, slot_cap)
     me = lax.axis_index(("xa", "xb"))
     ask_keep = split[me]
@@ -194,11 +195,11 @@
             jax.ShapeDtypeStruct((block_total, 8, 128), jnp.float32),
             jax.ShapeDtypeStruct((2 * slot_total, 3, 128), jnp.float32),
         ),
-        in_specs=[smem, smem, smem, smem, smem, vmem, vmem, vmem],
+        in_specs=[smem, smem, smem, smem, smem, vmem, vmem, vmem, vmem],
         out_specs=(vmem, vmem),
         scratch_shapes=[pltpu.SMEM((2 * slot_total,), jnp.int32), pltpu.SMEM((2 * slot_total,), jnp.int32)],
     )(ask_keep, hold_low, hold_high, mine_ids.reshape(slot_total), requested.reshape(slot_total),
-      mine_rows, rd, rq)
+      lend_rows, remote, halo_low, halo_high)
 
     returned = lax.all_to_all(
         f2.reshape(peer_total, 2 * slot_cap, 3, 128), ("xa", "xb"), split_axis=0, concat_axis=0,

time: 211 us -> 162 us (0.77)
  the two profiles are of different devices: /device:TPU:321 before, /device:TPU:320 now
where the time goes in v3:
time: 162 us; the launch traced here: 161 us
  Pallas kernels  53 us (33%)
  waiting for transfers between devices  39.6 us (24%)
  starting transfers between devices  31.9 us (20%)
  local copies, waits for them, and re-layouts  27.1 us (17%)
  other arithmetic  7.9 us (5%)
    pallas_call x1, Pallas kernels, local(): pl.pallas_call(pair_kernel, out_shape=(jax.ShapeDtypeStruct((block_total,...  46.2 us
    all_to_all x1, waiting for transfers between devices, local(): lax.all_to_all(f2.reshape(peer_total, 2 * slot_cap, 3, 128), ('xa', 'xb')...  18.8 us
    all_to_all x1, starting transfers between devices, local(): lax.all_to_all(f2.reshape(peer_total, 2 * slot_cap, 3, 128), ('xa', 'xb')...  16.4 us
    all_to_all x1, waiting for transfers between devices, local(): lax.all_to_all(lent, ('xa', 'xb'), split_axis=0, concat_axis=0, tiled=True)  15.5 us
    gather x1, local copies, waits for them, and re-layouts, local(): lent = lend_rows[lend_ids].reshape(peer_total, 2 * slot_cap, 4, 128)  7.96 us
    all_to_all x1, starting transfers between devices, local(): lax.all_to_all(jnp.concatenate([their_ids, own_counts], axis=1), ('xa', '...  7.03 us
    pallas_call x1, Pallas kernels, local(): pl.pallas_call(back_kernel, out_shape=jax.ShapeDtypeStruct((block_total,...  6.84 us
    all_to_all x1, starting transfers between devices, local(): lax.all_to_all(lent, ('xa', 'xb'), split_axis=0, concat_axis=0, tiled=True)  4.15 us
  transfers between devices with their start and end apart: 5, of which 5 were waited for; matrix products, arithmetic and copies ran while one was open for 9% of the time, Pallas kernels for 0%

profile of v3, /device:TPU:320, one launch (start us, length us, event | category | flops | bytes accessed | tf_op | source)
XLA Modules:
  0.0 160.9 jit_solution(16954698747714107014)
XLA Ops:
  0.6 0.8 fusion.14
  1.4 0.7 pad.6.clone
  2.2 0.6 pad_add_fusion
  2.8 7.0 %all-to-all-start = ((s32[16,1,48]{2,1,0:T(1,128)}), s32[16,1,48]{2,1,0:T(1,128)S(1)}, u32[]{:S(2)}, u32[]{:S(2)}) async-start(s32[16,1,48]{2,1,0:T(1,128)} %bitcast.2), calls=%async_computation | async-start | bytes 16384 | tf_op jit(solution)/shard_map/all_to_all | solution.py:174
  9.8 0.8 copy.86
  10.7 1.0 compare_convert_fusion
  11.7 2.3 %copy_dynamic-update-slice_fusion = (f32[3,256,130]{2,0,1:T(4,128)}, f32[256,3,128]{2,1,0:T(4,128)S(1)}, f32[3,256,128]{2,0,1:T(4,128)S(1)}) fusion(f32[3,256,128]{2,1,0:T(8,128)} %param.6, f32[3,128]{1,0:T(4,128)S(1)} %stack.4, f32[3,256]{0,1:T(8,128)S(1)} %copy.86), kind=kLoop, calls=%fused_computation.22 | loop fusion | flops 196607 | bytes 1708544
  14.0 0.2 pad_maximum_fusion.1.m_ref
  14.2 0.0 copy-start
  14.2 3.1 %all-to-all-done = s32[16,1,48]{2,1,0:T(1,128)S(1)} async-done(((s32[16,1,48]{2,1,0:T(1,128)}), s32[16,1,48]{2,1,0:T(1,128)S(1)}, u32[]{:S(2)}, u32[]{:S(2)}) %all-to-all-start) | async-done | bytes 3104 | tf_op jit(solution)/shard_map/all_to_all | solution.py:174
  17.3 0.1 pad_add_fusion.1
  17.4 0.1 reshape.141
  17.5 8.0 %gather_fusion = f32[1024,4,128]{2,1,0:T(4,128)} fusion(f32[256,4,128]{2,1,0:T(4,128)S(1)} %pad_maximum_fusion.1.m_ref, s32[1024]{0:T(1024)S(1)} %broadcast_clamp_fusion), kind=kCustom, calls=%fused_computation | custom fusion | bytes 4198400 | tf_op jit(solution)/shard_map/gather | solution.py:181
  25.4 0.0 copy-done
  25.4 4.1 %all-to-all-start.1 = ((f32[16,64,4,128]{3,2,1,0:T(4,128)}), f32[16,64,4,128]{3,2,1,0:T(4,128)S(1)}, u32[]{:S(2)}, u32[]{:S(2)}) async-start(f32[16,64,4,128]{3,2,1,0:T(4,128)} %bitcast.9), calls=%async_computation.1 | async-start | bytes 4194304 | tf_op jit(solution)/shard_map/all_to_all | solution.py:182
  29.6 1.3 fusion.13
  30.9 1.9 %collective-permute-start = (f32[3,256,2]{2,0,1:T(4,128)}, f32[3,256,2]{2,0,1:T(4,128)}, u32[]{:S(2)}, u32[]{:S(2)}) collective-permute-start(f32[3,256,2]{2,0,1:T(4,128)} %get-tuple-element.22), channel_id=1, source_target_pairs={{16,0},{32,16},{48,32},{64,48},{80,64},{96,80},{112,96},{128,112},... | collective-permute-start | bytes 18440 | tf_op jit(solution)/shard_map/ppermute | solution.py:28
  32.8 2.4 %collective-permute-start.1 = (f32[3,256,2]{2,0,1:T(4,128)}, f32[3,256,2]{2,0,1:T(4,128)S(1)}, u32[]{:S(2)}, u32[]{:S(2)}) collective-permute-start(f32[3,256,2]{2,0,1:T(4,128)} %get-tuple-element.23), channel_id=1, source_target_pairs={{0,16},{16,32},{32,48},{48,64},{64,80},{80,96},{96,112},{112,128},... | collective-permute-start | bytes 18440 | tf_op jit(solution)/shard_map/ppermute | solution.py:25
  35.3 0.7 reshape_squeeze.3.mine_ref
  35.9 0.7 fusion.9
  37.3 0.1 multiply_reduce_fusion.1
  37.4 0.1 multiply_reduce_fusion
  37.5 0.1 slice_clamp_fusion
  37.6 0.5 fusion.10.ka_ref
  38.1 0.7 reshape.140.req_ref
  38.8 0.8 dynamic-slice_reduce_fusion
  39.5 0.3 collective-permute-done
  39.8 1.8 %copy.89.high_ref = f32[3,256,2]{2,1,0:T(8,128)} copy(f32[3,256,2]{2,0,1:T(4,128)} %collective-permute-done) | data formatting | bytes 12288 | tf_op jit(solution)/shard_map/ppermute | solution.py:28
  41.6 1.9 %collective-permute-done.1 = f32[3,256,2]{2,0,1:T(4,128)S(1)} collective-permute-done((f32[3,256,2]{2,0,1:T(4,128)}, f32[3,256,2]{2,0,1:T(4,128)S(1)}, u32[]{:S(2)}, u32[]{:S(2)}) %collective-permute-start.1) | collective-permute-done | bytes 6176 | tf_op jit(solution)/shard_map/ppermute | solution.py:25
  43.5 0.0 copy-start.3
  43.5 0.8 copy.88.low_ref
  44.4 15.5 %all-to-all-done.1 = f32[16,64,4,128]{3,2,1,0:T(4,128)S(1)} async-done(((f32[16,64,4,128]{3,2,1,0:T(4,128)}), f32[16,64,4,128]{3,2,1,0:T(4,128)S(1)}, u32[]{:S(2)}, u32[]{:S(2)}) %all-to-all-start.1) | async-done | bytes 2097184 | tf_op jit(solution)/shard_map/all_to_all | solution.py:182
  59.9 0.0 copy-start.1
  59.9 1.3 copy-done.1
  61.2 46.2 %shard_map.80 = (f32[256,8,128]{2,1,0:T(8,128)}, f32[1024,3,128]{2,1,0:T(4,128)}) custom-call(s32[16]{0:T(128)} %fusion.10.ka_ref, s32[16]{0:T(128)} %get-tuple-element.32.hl_ref, s32[16]{0:T(128)} %get-tuple-element.31.hh_ref, s32[512]{0:T(512)} %reshape_squeeze.3.mine_ref, s32[512]{0:T(512)} %reshape.140.req_ref, f32[256,4,128]{2,1,0:T(4,128)} %copy-done, ...), custom_call_target="tpu_custom_call" | custom-call | tf_op jit(solution)/shard_map/pallas_call | solution.py:192
  107.4 0.0 copy-done.3
  107.4 3.0 %copy.90 = f32[16,64,3,128]{3,1,2,0:T(8,128)} copy(f32[16,64,3,128]{3,2,1,0:T(4,128)} %bitcast.35) | data formatting | bytes 3145728 | tf_op jit(solution)/shard_map/reshape | solution.py:205
  110.3 0.0 copy-start.2
  110.3 16.4 %all-to-all-start.2 = ((f32[16,64,3,128]{3,1,2,0:T(8,128)}), f32[16,64,3,128]{3,1,2,0:T(8,128)S(1)}, u32[]{:S(2)}, u32[]{:S(2)}) async-start(f32[16,64,3,128]{3,1,2,0:T(8,128)} %copy.90), calls=%async_computation.2 | async-start | bytes 3145728 | tf_op jit(solution)/shard_map/all_to_all | solution.py:204
  126.7 0.7 reshape.139.req_ref
  127.3 0.0 copy-done.2
  127.3 1.2 constant_dynamic-update-slice_fusion
  128.6 18.8 %all-to-all-done.2 = f32[16,64,3,128]{3,1,2,0:T(8,128)S(1)} async-done(((f32[16,64,3,128]{3,1,2,0:T(8,128)}), f32[16,64,3,128]{3,1,2,0:T(8,128)S(1)}, u32[]{:S(2)}, u32[]{:S(2)}) %all-to-all-start.2) | async-done | bytes 1572896 | tf_op jit(solution)/shard_map/all_to_all | solution.py:204
  147.4 2.4 %copy.91 = f32[16,64,3,128]{3,2,1,0:T(4,128)} copy(f32[16,64,3,128]{3,1,2,0:T(8,128)S(1)} %all-to-all-done.2) | data formatting | bytes 3145728 | tf_op jit(solution)/shard_map/all_to_all | solution.py:204
  149.8 0.0 copy-start.4
  149.8 0.0 copy-start.5
  149.8 0.0 copy-start.6
  149.8 6.8 %shard_map.81 = f32[256,8,128]{2,1,0:T(8,128)} custom-call(s32[1024]{0:T(1024)} %reshape.139.req_ref, f32[256,8,128]{2,1,0:T(8,128)} %get-tuple-element.4.f1_ref, f32[1024,3,128]{2,1,0:T(4,128)} %bitcast.33), custom_call_target="tpu_custom_call" | custom-call | tf_op jit(solution)/shard_map/pallas_call | solution.py:208
  156.7 0.0 copy-done.4
  156.7 0.0 copy-done.5
  156.7 0.0 copy-done.6
  156.7 2.7 %multiply_add_fusion = (f32[3,256,128]{2,0,1:T(4,128)S(1)}, f32[3,256,128]{2,0,1:T(4,128)S(1)}) fusion(f32[3,256,128]{2,1,0:T(8,128)S(1)} %copy-done.5, f32[256,8,128]{2,1,0:T(8,128)} %shard_map.81, f32[3,256,128]{2,0,1:T(4,128)S(1)} %get-tuple-element.26, f32[3,256,2]{2,0,1:T(4,128)S(1)} %copy-done.4, ...), kind=kLoop, calls=%fused_computation.17 | loop fusion | flops 1966080 | bytes 3151872 | tf_op jit(solution)/shard_map/add | solution.py:216
  159.3 0.8 copy.94
  160.1 0.8 copy.93
  (7 shorter events, 0.1 us)
Async XLA Ops:
  2.8 14.5 %all-to-all-start = ((s32[16,1,48]{2,1,0:T(1,128)}), s32[16,1,48]{2,1,0:T(1,128)S(1)}, u32[]{:S(2)}, u32[]{:S(2)}) async-start(s32[16,1,48]{2,1,0:T(1,128)} %bitcast.2), calls=%async_computation | async-start | bytes 16384 | tf_op jit(solution)/shard_map/all_to_all | solution.py:174
  14.2 11.2 %copy-start = (f32[256,4,128]{2,1,0:T(4,128)}, f32[256,4,128]{2,1,0:T(4,128)S(1)}, u32[]{:S(2)}) copy-start(f32[256,4,128]{2,1,0:T(4,128)S(1)} %pad_maximum_fusion.1.m_ref) | copy-start | bytes 1572868
  25.4 34.4 %all-to-all-start.1 = ((f32[16,64,4,128]{3,2,1,0:T(4,128)}), f32[16,64,4,128]{3,2,1,0:T(4,128)S(1)}, u32[]{:S(2)}, u32[]{:S(2)}) async-start(f32[16,64,4,128]{3,2,1,0:T(4,128)} %bitcast.9), calls=%async_computation.1 | async-start | bytes 4194304 | tf_op jit(solution)/shard_map/all_to_all | solution.py:182
  30.9 8.9 %collective-permute-start = (f32[3,256,2]{2,0,1:T(4,128)}, f32[3,256,2]{2,0,1:T(4,128)}, u32[]{:S(2)}, u32[]{:S(2)}) collective-permute-start(f32[3,256,2]{2,0,1:T(4,128)} %get-tuple-element.22), channel_id=1, source_target_pairs={{16,0},{32,16},{48,32},{64,48},{80,64},{96,80},{112,96},{128,112},... | collective-permute-start | bytes 18440 | tf_op jit(solution)/shard_map/ppermute | solution.py:28
  32.8 10.7 %collective-permute-start.1 = (f32[3,256,2]{2,0,1:T(4,128)}, f32[3,256,2]{2,0,1:T(4,128)S(1)}, u32[]{:S(2)}, u32[]{:S(2)}) collective-permute-start(f32[3,256,2]{2,0,1:T(4,128)} %get-tuple-element.23), channel_id=1, source_target_pairs={{0,16},{16,32},{32,48},{48,64},{64,80},{80,96},{96,112},{112,128},... | collective-permute-start | bytes 18440 | tf_op jit(solution)/shard_map/ppermute | solution.py:25
  43.5 63.8 %copy-start.3 = (f32[3,256,2]{2,0,1:T(4,128)}, f32[3,256,2]{2,0,1:T(4,128)S(1)}, u32[]{:S(2)}) copy-start(f32[3,256,2]{2,0,1:T(4,128)S(1)} %collective-permute-done.1) | copy-start | bytes 18436
  59.9 1.3 copy-start.1
  110.3 17.0 %copy-start.2 = (f32[3,256,130]{2,0,1:T(4,128)S(1)}, f32[3,256,130]{2,0,1:T(4,128)}, u32[]{:S(2)}) copy-start(f32[3,256,130]{2,0,1:T(4,128)} %get-tuple-element.24) | copy-start | bytes 1198084
  110.3 37.0 %all-to-all-start.2 = ((f32[16,64,3,128]{3,1,2,0:T(8,128)}), f32[16,64,3,128]{3,1,2,0:T(8,128)S(1)}, u32[]{:S(2)}, u32[]{:S(2)}) async-start(f32[16,64,3,128]{3,1,2,0:T(8,128)} %copy.90), calls=%async_computation.2 | async-start | bytes 3145728 | tf_op jit(solution)/shard_map/all_to_all | solution.py:204
  149.8 6.9 %copy-start.4 = (f32[3,256,2]{2,0,1:T(4,128)S(1)}, f32[3,256,2]{2,0,1:T(4,128)}, u32[]{:S(2)}) copy-start(f32[3,256,2]{2,0,1:T(4,128)} %copy-done.3) | copy-start | bytes 18436
  149.8 6.9 %copy-start.5 = (f32[3,256,128]{2,1,0:T(8,128)S(1)}, f32[3,256,128]{2,1,0:T(8,128)}, u32[]{:S(2)}) copy-start(f32[3,256,128]{2,1,0:T(8,128)} %param.6) | copy-start | bytes 1179652
  149.8 6.9 %copy-start.6 = (f32[3,256,128]{2,1,0:T(8,128)S(1)}, f32[3,256,128]{2,1,0:T(8,128)}, u32[]{:S(2)}) copy-start(f32[3,256,128]{2,1,0:T(8,128)} %param.7) | copy-start | bytes 1179652

commit v4 on v3

--- a/solution.py
+++ b/solution.py
@@ -15,7 +15,6 @@
 HIGHEST = lax.Precision.HIGHEST
 HIGH = lax.Precision.HIGH
 tile_group = 8
-balance_rounds = 3
 
 
 def halos(block, axis, dim, width):
@@ -42,7 +41,9 @@
 
 def rows_of(x, near):
     row = lax.broadcasted_iota(jnp.int32, (8, 128), 0)
-    v0, v1, v2, on = x[0:1], x[1:2], x[2:3], x[3:4]
+    lane = lax.broadcasted_iota(jnp.int32, (1, 128), 1).astype(jnp.float32)
+    v0, v1, v2 = x[0:1], x[1:2], x[2:3]
+    on = jnp.where(lane < x[3:4, 0:1], 1.0, 0.0)
     norm = v0 * v0 + v1 * v1 + v2 * v2
     far = masked_far * (1.0 - on)
     pick = lambda r, v: jnp.where(row == r, jnp.broadcast_to(v, (8, 128)), 0.0)
@@ -71,30 +72,20 @@
     return m * f1[3:4, :] - f1, (rq * f2[3:4, :] - f2)[0:3, :]
 
 
-def pair_kernel(
-    ka_ref, hl_ref, hh_ref, mine_ref, req_ref, m_ref, rem_ref, low_ref, high_ref, f1_ref, f2_ref, lb_ref,
-    ls_ref,
-):
+def pair_kernel(cnt_ref, req_ref, m_ref, rem_ref, low_ref, high_ref, f1_ref, f2_ref, lb_ref, ls_ref):
     f1_ref[...] = jnp.zeros(f1_ref.shape, f1_ref.dtype)
     f2_ref[...] = jnp.zeros(f2_ref.shape, f2_ref.dtype)
-    peers = ka_ref.shape[0]
-    cap = mine_ref.shape[0] // peers
+    peers = cnt_ref.shape[0]
+    cap = req_ref.shape[0] // peers
     blocks = m_ref.shape[0]
 
     def listed(d, n):
-        def asked(c, n):
-            lb_ref[n] = jnp.clip(mine_ref[d * cap + c], 0, blocks - 1)
-            ls_ref[n] = d * 2 * cap + c
+        def held(c, n):
+            lb_ref[n] = jnp.clip(req_ref[d * cap + c], 0, blocks - 1)
+            ls_ref[n] = d * cap + c
             return n + 1
 
-        def held(c, n):
-            lb_ref[n] = jnp.clip(req_ref[d * cap + c], 0, blocks - 1)
-            ls_ref[n] = d * 2 * cap + cap + c
-            return n + 1
-
-        n = lax.fori_loop(0, jnp.clip(ka_ref[d], 0, cap), asked, n)
-        low = jnp.clip(hl_ref[d], 0, cap)
-        return lax.fori_loop(low, jnp.clip(hh_ref[d], low, cap), held, n)
+        return lax.fori_loop(0, jnp.clip(cnt_ref[d], 0, cap), held, n)
 
     total = lax.fori_loop(0, peers, listed, 0)
     last = jnp.maximum(total - 1, 0)
@@ -115,26 +106,6 @@
         return carry
 
     lax.fori_loop(0, (total + tile_group - 1) // tile_group, group, 0)
-
-
-def split_pairs(counts, cap):
-    peers = counts.shape[0]
-    whole = jnp.clip(counts, 0, cap)
-    share = whole.astype(jnp.float32)
-    eye = jnp.eye(peers, dtype=jnp.float32)
-    off = share * (1.0 - eye)
-    own = jnp.sum(share * eye, axis=1)
-    off_row = jnp.sum(off, axis=1)
-    level = jnp.sum(share) / peers
-    keep = jnp.ones((peers,), jnp.float32)
-    for _ in range(balance_rounds):
-        incoming = jnp.sum((1.0 - keep)[:, None] * off, axis=0)
-        target = jnp.maximum(level - incoming, 0.0)
-        keep = jnp.clip((target - own) / jnp.maximum(off_row, 1.0), 0.0, 1.0)
-    split = jnp.floor(keep[:, None] * share + 0.5).astype(jnp.int32)
-    split = jnp.clip(split, 0, whole)
-    diag = jnp.eye(peers, dtype=jnp.bool_)
-    return jnp.where(diag, whole, split), whole
 
 
 def back_kernel(req_ref, f1_ref, ret_ref, out_ref):
@@ -165,27 +136,25 @@
     positions = displacement + anchors[:, :, None] + lift[:, None, :]
     blocks = positions.reshape(3, block_total, 128).transpose(1, 0, 2)
     lanes = jnp.arange(128, dtype=jnp.int32)
-    live = (lanes[None, :] < seg_live.reshape(block_total)[:, None]).astype(jnp.float32)
-    lend_rows = jnp.stack([blocks[:, 0], blocks[:, 1], blocks[:, 2], live], axis=1)
+    seg_count = seg_live.reshape(block_total).astype(jnp.float32)
+    meta = jnp.where(lanes[None, :] == 0, seg_count[:, None], 0.0)
+    my_rows = jnp.concatenate([blocks, meta[:, None, :]], axis=1)
 
     mine_ids = pair_blocks[0, 0, :, :, 0]
-    their_ids = pair_blocks[0, 0, :, :, 1]
-    own_counts = jnp.broadcast_to(pair_count[0, 0][None, :], (peer_total, peer_total))
-    asked = lax.all_to_all(
-        jnp.concatenate([their_ids, own_counts], axis=1), ("xa", "xb"), split_axis=0, concat_axis=0,
-        tiled=True,
+    their_ids = pair_blocks[0, 0, :, :, 1].astype(jnp.float32)
+    live_to = jnp.broadcast_to(pair_count[0, 0].astype(jnp.float32)[:, None], their_ids.shape)
+    mine_flat = mine_ids.reshape(slot_total)
+    sent_meta = jnp.where(
+        lanes == 0, seg_count[mine_flat][:, None],
+        jnp.where(lanes == 1, their_ids.reshape(slot_total)[:, None],
+                  jnp.where(lanes == 2, live_to.reshape(slot_total)[:, None], 0.0)),
     )
-    requested = asked[:, :slot_cap]
-    counts = asked[:, slot_cap:]
-    lend_ids = jnp.concatenate([requested, mine_ids], axis=1).reshape(2 * slot_total)
-    lent = lend_rows[lend_ids].reshape(peer_total, 2 * slot_cap, 4, 128)
-    remote = lax.all_to_all(lent, ("xa", "xb"), split_axis=0, concat_axis=0, tiled=True)
-    remote = remote.reshape(2 * slot_total, 4, 128)
-    split, whole = split_pairs(counts, slot_cap)
-    me = lax.axis_index(("xa", "xb"))
-    ask_keep = split[me]
-    hold_low = split[:, me]
-    hold_high = whole[:, me]
+    lent = jnp.concatenate([blocks[mine_flat], sent_meta[:, None, :]], axis=1)
+    remote = lax.all_to_all(
+        lent.reshape(peer_total, slot_cap, 4, 128), ("xa", "xb"), split_axis=0, concat_axis=0, tiled=True
+    )
+    req_ids = remote[:, :, 3, 1].astype(jnp.int32).reshape(slot_total)
+    live_from = remote[:, 0, 3, 2].astype(jnp.int32)
 
     smem = pl.BlockSpec(memory_space=pltpu.SMEM)
     vmem = pl.BlockSpec(memory_space=pltpu.VMEM)
@@ -193,24 +162,22 @@
         pair_kernel,
         out_shape=(
             jax.ShapeDtypeStruct((block_total, 8, 128), jnp.float32),
-            jax.ShapeDtypeStruct((2 * slot_total, 3, 128), jnp.float32),
+            jax.ShapeDtypeStruct((slot_total, 3, 128), jnp.float32),
         ),
-        in_specs=[smem, smem, smem, smem, smem, vmem, vmem, vmem, vmem],
+        in_specs=[smem, smem, vmem, vmem, vmem, vmem],
         out_specs=(vmem, vmem),
-        scratch_shapes=[pltpu.SMEM((2 * slot_total,), jnp.int32), pltpu.SMEM((2 * slot_total,), jnp.int32)],
-    )(ask_keep, hold_low, hold_high, mine_ids.reshape(slot_total), requested.reshape(slot_total),
-      lend_rows, remote, halo_low, halo_high)
+        scratch_shapes=[pltpu.SMEM((slot_total,), jnp.int32), pltpu.SMEM((slot_total,), jnp.int32)],
+    )(live_from, req_ids, my_rows, remote.reshape(slot_total, 4, 128), halo_low, halo_high)
 
     returned = lax.all_to_all(
-        f2.reshape(peer_total, 2 * slot_cap, 3, 128), ("xa", "xb"), split_axis=0, concat_axis=0,
-        tiled=True,
+        f2.reshape(peer_total, slot_cap, 3, 128), ("xa", "xb"), split_axis=0, concat_axis=0, tiled=True
     )
     acc = pl.pallas_call(
         back_kernel,
         out_shape=jax.ShapeDtypeStruct((block_total, 8, 128), jnp.float32),
         in_specs=[smem, vmem, vmem],
         out_specs=vmem,
-    )(lend_ids, f1, returned.reshape(2 * slot_total, 3, 128))
+    )(mine_flat, f1, returned.reshape(slot_total, 3, 128))
     contact = acc[:, 0:3, :].transpose(1, 0, 2).reshape(3, fibre_count, seg_len)
     new_velocity = damping * velocity + time_step * (beam + contact)
     new_displacement = displacement + time_step * new_velocity

time: 162 us -> 145 us (0.90)
  the two profiles are of different devices: /device:TPU:320 before, /device:TPU:480 now
where the time goes in v4:
time: 145 us; the launch traced here: 144 us
  Pallas kernels  65.1 us (45%)
  starting transfers between devices  24.7 us (17%)
  waiting for transfers between devices  24.4 us (17%)
  local copies, waits for them, and re-layouts  18.7 us (13%)
  other arithmetic  10.4 us (7%)
    pallas_call x1, Pallas kernels, local(): pl.pallas_call(pair_kernel, out_shape=(jax.ShapeDtypeStruct((block_total,...  60.6 us
    all_to_all x1, waiting for transfers between devices, local(): lax.all_to_all(f2.reshape(peer_total, slot_cap, 3, 128), ('xa', 'xb'), sp...  15.3 us
    all_to_all x1, starting transfers between devices, local(): lax.all_to_all(f2.reshape(peer_total, slot_cap, 3, 128), ('xa', 'xb'), sp...  13.3 us
    all_to_all x1, starting transfers between devices, local(): lax.all_to_all(lent.reshape(peer_total, slot_cap, 4, 128), ('xa', 'xb'),...  7.03 us
    pallas_call x1, Pallas kernels, local(): pl.pallas_call(back_kernel, out_shape=jax.ShapeDtypeStruct((block_total,...  4.58 us
    gather x1, local copies, waits for them, and re-layouts, local(): seg_count[mine_flat][:, None]  3.51 us
    unnamed x33, local copies, waits for them, and re-layouts  3.39 us
    all_to_all x1, waiting for transfers between devices, local(): lax.all_to_all(lent.reshape(peer_total, slot_cap, 4, 128), ('xa', 'xb'),...  3.14 us
  transfers between devices with their start and end apart: 4, of which 4 were waited for; matrix products, arithmetic and copies ran while one was open for 3% of the time, Pallas kernels for 0%

profile of v4, /device:TPU:480, one launch (start us, length us, event | category | flops | bytes accessed | tf_op | source)
XLA Modules:
  0.0 144.1 jit_solution(14255262556020561356)
XLA Ops:
  0.6 0.5 iota_compare_fusion.2
  1.1 0.0 copy-start.14
  1.2 0.6 iota_compare_fusion
  1.7 0.1 copy-done.14
  1.8 0.0 copy-start.10
  1.8 0.5 convert_bitcast_fusion
  2.3 0.2 copy-done.10
  2.5 1.4 fusion.13
  3.9 0.1 reshape_squeeze.6
  4.0 0.0 copy-start.4
  4.0 3.5 %gather_fusion.1 = f32[512]{0:T(512)S(1)} fusion(f32[256]{0:T(256)S(1)} %bitcast.21, s32[1024]{0:T(1024)S(1)} %pad_clamp_fusion), kind=kCustom, calls=%fused_computation.1 | custom fusion | bytes 6144 | tf_op jit(solution)/shard_map/gather | solution.py:148
  7.5 0.0 copy-start.8
  7.5 0.7 broadcast_in_dim.72
  8.2 0.0 copy-done.8
  8.2 0.1 copy.103
  8.4 0.0 copy-done.4
  8.4 0.5 copy_dynamic-update-slice_fusion
  8.9 2.1 %gather_fusion = f32[512,3,128]{2,1,0:T(4,128)S(1)} fusion(f32[256,3,128]{2,1,0:T(4,128)S(1)} %get-tuple-element.23, s32[1024]{0:T(1024)S(1)} %pad_clamp_fusion), kind=kCustom, calls=%fused_computation | custom fusion | bytes 1574912 | tf_op jit(solution)/shard_map/gather | solution.py:152
  11.0 0.0 copy-start.6
  11.0 0.0 copy-start.7
  11.0 0.0 copy-start.13
  11.0 0.1 copy.105
  11.1 0.0 copy-start.9
  11.1 0.0 copy-start.11
  11.1 0.0 copy-start.12
  11.1 0.5 copy-done.6
  11.7 0.0 copy-done.7
  11.7 0.0 copy-done.13
  11.7 0.0 copy-done.9
  11.7 0.1 copy-done.11
  11.8 0.0 copy-done.12
  11.8 0.2 select_select_fusion
  12.0 1.1 pad_maximum_fusion
  13.1 7.0 %all-to-all-start = ((f32[16,32,4,128]{3,1,2,0:T(8,128)}), f32[16,32,4,128]{3,1,2,0:T(8,128)S(1)}, u32[]{:S(2)}, u32[]{:S(2)}) async-start(f32[16,32,4,128]{3,1,2,0:T(8,128)} %pad_maximum_fusion), calls=%async_computation | async-start | bytes 2097152 | tf_op jit(solution)/shard_map/all_to_all | solution.py:153
  20.1 0.3 fusion.12
  20.5 2.1 %collective-permute-start = (f32[3,256,2]{2,0,1:T(4,128)S(1)}, f32[3,256,2]{2,0,1:T(4,128)S(1)}, u32[]{:S(2)}, u32[]{:S(2)}) collective-permute-start(f32[3,256,2]{2,0,1:T(4,128)S(1)} %get-tuple-element.20), channel_id=1, source_target_pairs={{16,0},{32,16},{48,32},{64,48},{80,64},{96,80},{112,96},{128,112},... | collective-permute-start | bytes 18440 | tf_op jit(solution)/shard_map/ppermute | solution.py:27
  22.6 2.3 %collective-permute-start.1 = (f32[3,256,2]{2,0,1:T(4,128)S(1)}, f32[3,256,2]{2,0,1:T(4,128)S(1)}, u32[]{:S(2)}, u32[]{:S(2)}) collective-permute-start(f32[3,256,2]{2,0,1:T(4,128)S(1)} %get-tuple-element.21), channel_id=1, source_target_pairs={{0,16},{16,32},{32,48},{48,64},{64,80},{80,96},{96,112},{112,128},... | collective-permute-start | bytes 18440 | tf_op jit(solution)/shard_map/ppermute | solution.py:24
  24.9 0.3 broadcast_select_fusion
  25.2 1.0 pad_maximum_fusion.2.m_ref
  26.2 3.0 %collective-permute-done = f32[3,256,2]{2,0,1:T(4,128)S(1)} collective-permute-done((f32[3,256,2]{2,0,1:T(4,128)S(1)}, f32[3,256,2]{2,0,1:T(4,128)S(1)}, u32[]{:S(2)}, u32[]{:S(2)}) %collective-permute-start) | collective-permute-done | bytes 6176 | tf_op jit(solution)/shard_map/ppermute | solution.py:27
  29.2 0.9 copy.108.high_ref
  30.1 3.0 %collective-permute-done.1 = f32[3,256,2]{2,0,1:T(4,128)S(1)} collective-permute-done((f32[3,256,2]{2,0,1:T(4,128)S(1)}, f32[3,256,2]{2,0,1:T(4,128)S(1)}, u32[]{:S(2)}, u32[]{:S(2)}) %collective-permute-start.1) | collective-permute-done | bytes 6176 | tf_op jit(solution)/shard_map/ppermute | solution.py:24
  33.1 0.0 copy-done.2
  33.1 0.8 copy-done
  33.9 0.8 copy.107.low_ref
  34.6 3.1 %all-to-all-done = f32[16,32,4,128]{3,1,2,0:T(8,128)S(1)} async-done(((f32[16,32,4,128]{3,1,2,0:T(8,128)}), f32[16,32,4,128]{3,1,2,0:T(8,128)S(1)}, u32[]{:S(2)}, u32[]{:S(2)}) %all-to-all-start) | async-done | bytes 1048608 | tf_op jit(solution)/shard_map/all_to_all | solution.py:153
  37.8 0.5 fusion.9
  38.2 0.7 convert_element_type.59.req_ref
  38.9 1.0 fusion.10.cnt_ref
  40.0 1.7 %copy.106 = f32[16,32,4,128]{3,2,1,0:T(4,128)} copy(f32[16,32,4,128]{3,1,2,0:T(8,128)S(1)} %all-to-all-done) | data formatting | bytes 2097152 | tf_op jit(solution)/shard_map/all_to_all | solution.py:153
  41.6 60.6 %shard_map.77 = (f32[256,8,128]{2,1,0:T(8,128)}, f32[512,3,128]{2,1,0:T(4,128)}) custom-call(s32[16]{0:T(128)} %fusion.10.cnt_ref, s32[512]{0:T(512)} %convert_element_type.59.req_ref, f32[256,4,128]{2,1,0:T(4,128)} %pad_maximum_fusion.2.m_ref, f32[512,4,128]{2,1,0:T(4,128)} %bitcast.24, f32[3,256,2]{2,1,0:T(8,128)} %copy.107.low_ref, ...), custom_call_target="tpu_custom_call" | custom-call | tf_op jit(solution)/shard_map/pallas_call | solution.py:161
  102.2 2.2 %copy.109 = f32[16,32,3,128]{3,1,2,0:T(8,128)} copy(f32[16,32,3,128]{3,2,1,0:T(4,128)} %bitcast.26) | data formatting | bytes 1572864 | tf_op jit(solution)/shard_map/reshape | solution.py:173
  104.4 13.3 %all-to-all-start.1 = ((f32[16,32,3,128]{3,1,2,0:T(8,128)}), f32[16,32,3,128]{3,1,2,0:T(8,128)S(1)}, u32[]{:S(2)}, u32[]{:S(2)}) async-start(f32[16,32,3,128]{3,1,2,0:T(8,128)} %copy.109), calls=%async_computation.1 | async-start | bytes 1572864 | tf_op jit(solution)/shard_map/all_to_all | solution.py:172
  117.7 0.7 reshape_squeeze.5.req_ref
  118.4 0.0 copy-done.3
  118.4 0.2 constant_dynamic-update-slice_fusion
  118.5 15.3 %all-to-all-done.1 = f32[16,32,3,128]{3,1,2,0:T(8,128)S(1)} async-done(((f32[16,32,3,128]{3,1,2,0:T(8,128)}), f32[16,32,3,128]{3,1,2,0:T(8,128)S(1)}, u32[]{:S(2)}, u32[]{:S(2)}) %all-to-all-start.1) | async-done | bytes 786464 | tf_op jit(solution)/shard_map/all_to_all | solution.py:172
  133.8 1.5 %copy.110 = f32[16,32,3,128]{3,2,1,0:T(4,128)} copy(f32[16,32,3,128]{3,1,2,0:T(8,128)S(1)} %all-to-all-done.1) | data formatting | bytes 1572864 | tf_op jit(solution)/shard_map/all_to_all | solution.py:172
  135.3 4.6 %shard_map.78 = f32[256,8,128]{2,1,0:T(8,128)} custom-call(s32[512]{0:T(512)} %reshape_squeeze.5.req_ref, f32[256,8,128]{2,1,0:T(8,128)} %get-tuple-element.4.f1_ref, f32[512,3,128]{2,1,0:T(4,128)} %bitcast.25), custom_call_target="tpu_custom_call" | custom-call | tf_op jit(solution)/shard_map/pallas_call | solution.py:175
  139.9 0.0 copy-done.1
  139.9 0.0 copy-done.5
  139.9 2.7 %multiply_add_fusion = (f32[3,256,128]{2,0,1:T(4,128)S(1)}, f32[3,256,128]{2,0,1:T(4,128)S(1)}) fusion(f32[3,256,128]{2,1,0:T(8,128)S(1)} %copy-done.4, f32[256,8,128]{2,1,0:T(8,128)} %shard_map.78, f32[3,256,128]{2,0,1:T(4,128)S(1)} %get-tuple-element.24, f32[3,256,2]{2,0,1:T(4,128)S(1)} %copy-done.1, ...), kind=kLoop, calls=%fused_computation.19 | loop fusion | flops 1966080 | bytes 3151872 | tf_op jit(solution)/shard_map/add | solution.py:183
  142.6 0.8 copy.113
  143.4 0.8 copy.112
  (10 shorter events, 0.0 us)
Async XLA Ops:
  1.1 0.7 copy-start.14
  1.8 0.7 copy-start.10
  4.0 4.4 %copy-start.4 = (f32[3,256,128]{2,1,0:T(8,128)S(1)}, f32[3,256,128]{2,1,0:T(8,128)}, u32[]{:S(2)}) copy-start(f32[3,256,128]{2,1,0:T(8,128)} %param.6) | copy-start | bytes 1179652
  7.5 0.7 copy-start.8
  11.0 0.7 copy-start.6
  11.0 0.7 copy-start.7
  11.0 0.7 copy-start.13
  11.1 0.6 copy-start.9
  11.1 0.7 copy-start.11
  11.1 0.7 copy-start.12
  13.1 24.7 %all-to-all-start = ((f32[16,32,4,128]{3,1,2,0:T(8,128)}), f32[16,32,4,128]{3,1,2,0:T(8,128)S(1)}, u32[]{:S(2)}, u32[]{:S(2)}) async-start(f32[16,32,4,128]{3,1,2,0:T(8,128)} %pad_maximum_fusion), calls=%async_computation | async-start | bytes 2097152 | tf_op jit(solution)/shard_map/all_to_all | solution.py:153
  20.5 8.8 %collective-permute-start = (f32[3,256,2]{2,0,1:T(4,128)S(1)}, f32[3,256,2]{2,0,1:T(4,128)S(1)}, u32[]{:S(2)}, u32[]{:S(2)}) collective-permute-start(f32[3,256,2]{2,0,1:T(4,128)S(1)} %get-tuple-element.20), channel_id=1, source_target_pairs={{16,0},{32,16},{48,32},{64,48},{80,64},{96,80},{112,96},{128,112},... | collective-permute-start | bytes 18440 | tf_op jit(solution)/shard_map/ppermute | solution.py:27
  22.6 10.5 %collective-permute-start.1 = (f32[3,256,2]{2,0,1:T(4,128)S(1)}, f32[3,256,2]{2,0,1:T(4,128)S(1)}, u32[]{:S(2)}, u32[]{:S(2)}) collective-permute-start(f32[3,256,2]{2,0,1:T(4,128)S(1)} %get-tuple-element.21), channel_id=1, source_target_pairs={{0,16},{16,32},{32,48},{48,64},{64,80},{80,96},{96,112},{112,128},... | collective-permute-start | bytes 18440 | tf_op jit(solution)/shard_map/ppermute | solution.py:24
  29.2 3.8 %copy-start.2 = (f32[3,256,2]{2,0,1:T(4,128)}, f32[3,256,2]{2,0,1:T(4,128)S(1)}, u32[]{:S(2)}) copy-start(f32[3,256,2]{2,0,1:T(4,128)S(1)} %collective-permute-done) | copy-start | bytes 18436
  33.1 0.8 copy-start
  104.4 13.9 %copy-start.3 = (f32[3,256,2]{2,0,1:T(4,128)S(1)}, f32[3,256,2]{2,0,1:T(4,128)}, u32[]{:S(2)}) copy-start(f32[3,256,2]{2,0,1:T(4,128)} %copy-done.2) | copy-start | bytes 18436
  104.4 29.4 %all-to-all-start.1 = ((f32[16,32,3,128]{3,1,2,0:T(8,128)}), f32[16,32,3,128]{3,1,2,0:T(8,128)S(1)}, u32[]{:S(2)}, u32[]{:S(2)}) async-start(f32[16,32,3,128]{3,1,2,0:T(8,128)} %copy.109), calls=%async_computation.1 | async-start | bytes 1572864 | tf_op jit(solution)/shard_map/all_to_all | solution.py:172
  135.3 4.6 %copy-start.1 = (f32[3,256,2]{2,0,1:T(4,128)S(1)}, f32[3,256,2]{2,0,1:T(4,128)}, u32[]{:S(2)}) copy-start(f32[3,256,2]{2,0,1:T(4,128)} %copy-done) | copy-start | bytes 18436
  135.3 4.6 %copy-start.5 = (f32[3,256,128]{2,1,0:T(8,128)S(1)}, f32[3,256,128]{2,1,0:T(8,128)}, u32[]{:S(2)}) copy-start(f32[3,256,128]{2,1,0:T(8,128)} %param.7) | copy-start | bytes 1179652

commit v5 on v4

--- a/solution.py
+++ b/solution.py
@@ -12,7 +12,6 @@
 time_step = 0.2
 damping = 0.9
 masked_far = 1.0e4
-HIGHEST = lax.Precision.HIGHEST
 HIGH = lax.Precision.HIGH
 tile_group = 8
 
@@ -56,20 +55,29 @@
     return rd, rq
 
 
-def tile_pair(m, rd, rq):
+def tile_two(m_a, m_b, rd_a, rd_b, rq_a, rq_b):
+    zero = jnp.zeros((8, 128), jnp.float32)
+    mine = jnp.concatenate(
+        [jnp.concatenate([m_a, zero], axis=1), jnp.concatenate([zero, m_b], axis=1)], axis=0
+    )
     dist = lax.dot_general(
-        rd, m, (((0,), (0,)), ((), ())), precision=HIGHEST, preferred_element_type=jnp.float32
+        jnp.concatenate([rd_a, rd_b], axis=0), mine, (((0,), (0,)), ((), ())), precision=HIGH,
+        preferred_element_type=jnp.float32,
     )
     w = jnp.exp(-dist)
     f1 = lax.dot_general(
-        rq, w, (((1,), (0,)), ((), ())), precision=HIGH, preferred_element_type=jnp.float32
+        jnp.concatenate([rq_a, rq_b], axis=0), w, (((1,), (0,)), ((), ())), precision=HIGH,
+        preferred_element_type=jnp.float32,
     )
     f2 = lax.dot_general(
-        m, w, (((1,), (1,)), ((), ())), precision=HIGH, preferred_element_type=jnp.float32
+        mine, w, (((1,), (1,)), ((), ())), precision=HIGH, preferred_element_type=jnp.float32
     )
     f1 = f1 * contact_stiff
     f2 = f2 * contact_stiff
-    return m * f1[3:4, :] - f1, (rq * f2[3:4, :] - f2)[0:3, :]
+    out = []
+    for m, rq, g1, g2 in ((m_a, rq_a, f1[0:8, 0:128], f2[0:8]), (m_b, rq_b, f1[8:16, 128:256], f2[8:16])):
+        out.append((m * g1[3:4, :] - g1, (rq * g2[3:4, :] - g2)[0:3, :]))
+    return out
 
 
 def pair_kernel(cnt_ref, req_ref, m_ref, rem_ref, low_ref, high_ref, f1_ref, f2_ref, lb_ref, ls_ref):
@@ -92,14 +100,17 @@
 
     def group(g, carry):
         done = []
-        for k in range(tile_group):
-            t = g * tile_group + k
-            at = jnp.minimum(t, last)
-            b = lb_ref[at]
-            slot = ls_ref[at]
-            rd, rq = rows_of(rem_ref[slot], False)
-            on_first, on_second = tile_pair(rows_of(m_ref[b], True), rd, rq)
-            done.append((b, slot, jnp.where(t < total, on_first, 0.0), on_second))
+        for k in range(0, tile_group, 2):
+            picked = []
+            for t in (g * tile_group + k, g * tile_group + k + 1):
+                at = jnp.minimum(t, last)
+                picked.append((t, lb_ref[at], ls_ref[at]))
+            (t_a, b_a, s_a), (t_b, b_b, s_b) = picked
+            rd_a, rq_a = rows_of(rem_ref[s_a], False)
+            rd_b, rq_b = rows_of(rem_ref[s_b], False)
+            pair = tile_two(rows_of(m_ref[b_a], True), rows_of(m_ref[b_b], True), rd_a, rd_b, rq_a, rq_b)
+            for (t, b, slot), (on_first, on_second) in zip(picked, pair):
+                done.append((b, slot, jnp.where(t < total, on_first, 0.0), on_second))
         for b, slot, on_first, on_second in done:
             f1_ref[b] = f1_ref[b] + on_first
             f2_ref[slot] = on_second

time: 145 us -> 111 us (0.77)
  the two profiles are of different devices: /device:TPU:480 before, /device:TPU:256 now
where the time goes in v5:
time: 111 us; the launch traced here: 110 us
  Pallas kernels  33.6 us (30%)
  starting transfers between devices  26.9 us (24%)
  waiting for transfers between devices  19.9 us (18%)
  local copies, waits for them, and re-layouts  18.7 us (17%)
  other arithmetic  10.4 us (9%)
    pallas_call x1, Pallas kernels, local(): pl.pallas_call(pair_kernel, out_shape=(jax.ShapeDtypeStruct((block_total,...  29.1 us
    all_to_all x1, starting transfers between devices, local(): lax.all_to_all(f2.reshape(peer_total, slot_cap, 3, 128), ('xa', 'xb'), sp...  15.6 us
    all_to_all x1, waiting for transfers between devices, local(): lax.all_to_all(f2.reshape(peer_total, slot_cap, 3, 128), ('xa', 'xb'), sp...  10.7 us
    all_to_all x1, starting transfers between devices, local(): lax.all_to_all(lent.reshape(peer_total, slot_cap, 4, 128), ('xa', 'xb'),...  7.03 us
    pallas_call x1, Pallas kernels, local(): pl.pallas_call(back_kernel, out_shape=jax.ShapeDtypeStruct((block_total,...  4.58 us
    ppermute x1, waiting for transfers between devices, halos(): lax.ppermute(lax.slice_in_dim(block, block.shape[dim] - width, None, axis...  4.18 us
    gather x1, local copies, waits for them, and re-layouts, local(): seg_count[mine_flat][:, None]  3.51 us
    unnamed x33, local copies, waits for them, and re-layouts  3.39 us
  transfers between devices with their start and end apart: 4, of which 4 were waited for; matrix products, arithmetic and copies ran while one was open for 4% of the time, Pallas kernels for 0%

profile of v5, /device:TPU:256, one launch (start us, length us, event | category | flops | bytes accessed | tf_op | source)
XLA Modules:
  0.0 110.4 jit_solution(330958160894187614)
XLA Ops:
  0.6 0.5 iota_compare_fusion.2
  1.1 0.0 copy-start.14
  1.2 0.6 iota_compare_fusion
  1.7 0.1 copy-done.14
  1.8 0.0 copy-start.10
  1.8 0.5 convert_bitcast_fusion
  2.3 0.2 copy-done.10
  2.5 1.4 %fusion.13 = (s32[1,1,16,32,1]{3,4,2,1,0:T(1,128)S(1)}, s32[16,32]{1,0:T(8,128)S(1)}, f32[1,1,16,32,1]{3,4,2,1,0:T(1,128)}) fusion(s32[1,1,16,32,2]{3,4,2,1,0:T(2,128)} %param.10), kind=kLoop, calls=%fused_computation.39 | loop fusion | flops 512 | bytes 10240 | tf_op jit(solution)/shard_map/slice | solution.py:154
  3.9 0.1 reshape_squeeze.6
  4.0 0.0 copy-start.4
  4.0 3.5 %gather_fusion.1 = f32[512]{0:T(512)S(1)} fusion(f32[256]{0:T(256)S(1)} %bitcast.21, s32[1024]{0:T(1024)S(1)} %pad_clamp_fusion), kind=kCustom, calls=%fused_computation.1 | custom fusion | bytes 6144 | tf_op jit(solution)/shard_map/gather | solution.py:159
  7.5 0.0 copy-start.8
  7.5 0.7 broadcast_in_dim.72
  8.2 0.0 copy-done.8
  8.2 0.1 copy.103
  8.4 0.0 copy-done.4
  8.4 0.5 copy_dynamic-update-slice_fusion
  8.9 2.1 %gather_fusion = f32[512,3,128]{2,1,0:T(4,128)S(1)} fusion(f32[256,3,128]{2,1,0:T(4,128)S(1)} %get-tuple-element.23, s32[1024]{0:T(1024)S(1)} %pad_clamp_fusion), kind=kCustom, calls=%fused_computation | custom fusion | bytes 1574912 | tf_op jit(solution)/shard_map/gather | solution.py:163
  11.0 0.0 copy-start.6
  11.0 0.0 copy-start.7
  11.0 0.0 copy-start.13
  11.0 0.1 copy.105
  11.1 0.0 copy-start.9
  11.1 0.0 copy-start.11
  11.1 0.0 copy-start.12
  11.1 0.5 copy-done.6
  11.7 0.0 copy-done.7
  11.7 0.0 copy-done.13
  11.7 0.0 copy-done.9
  11.7 0.1 copy-done.11
  11.8 0.0 copy-done.12
  11.8 0.2 select_select_fusion
  12.0 1.1 pad_maximum_fusion
  13.1 7.0 %all-to-all-start = ((f32[16,32,4,128]{3,1,2,0:T(8,128)}), f32[16,32,4,128]{3,1,2,0:T(8,128)S(1)}, u32[]{:S(2)}, u32[]{:S(2)}) async-start(f32[16,32,4,128]{3,1,2,0:T(8,128)} %pad_maximum_fusion), calls=%async_computation | async-start | bytes 2097152 | tf_op jit(solution)/shard_map/all_to_all | solution.py:164
  20.1 0.3 fusion.12
  20.5 1.9 %collective-permute-start = (f32[3,256,2]{2,0,1:T(4,128)S(1)}, f32[3,256,2]{2,0,1:T(4,128)S(1)}, u32[]{:S(2)}, u32[]{:S(2)}) collective-permute-start(f32[3,256,2]{2,0,1:T(4,128)S(1)} %get-tuple-element.20), channel_id=1, source_target_pairs={{16,0},{32,16},{48,32},{64,48},{80,64},{96,80},{112,96},{128,112},... | collective-permute-start | bytes 18440 | tf_op jit(solution)/shard_map/ppermute | solution.py:26
  22.4 2.4 %collective-permute-start.1 = (f32[3,256,2]{2,0,1:T(4,128)S(1)}, f32[3,256,2]{2,0,1:T(4,128)S(1)}, u32[]{:S(2)}, u32[]{:S(2)}) collective-permute-start(f32[3,256,2]{2,0,1:T(4,128)S(1)} %get-tuple-element.21), channel_id=1, source_target_pairs={{0,16},{16,32},{32,48},{48,64},{64,80},{80,96},{96,112},{112,128},... | collective-permute-start | bytes 18440 | tf_op jit(solution)/shard_map/ppermute | solution.py:23
  24.8 0.3 broadcast_select_fusion
  25.2 1.0 pad_maximum_fusion.2.m_ref
  26.2 2.9 %collective-permute-done = f32[3,256,2]{2,0,1:T(4,128)S(1)} collective-permute-done((f32[3,256,2]{2,0,1:T(4,128)S(1)}, f32[3,256,2]{2,0,1:T(4,128)S(1)}, u32[]{:S(2)}, u32[]{:S(2)}) %collective-permute-start) | collective-permute-done | bytes 6176 | tf_op jit(solution)/shard_map/ppermute | solution.py:26
  29.1 0.9 copy.108.high_ref
  29.9 4.2 %collective-permute-done.1 = f32[3,256,2]{2,0,1:T(4,128)S(1)} collective-permute-done((f32[3,256,2]{2,0,1:T(4,128)S(1)}, f32[3,256,2]{2,0,1:T(4,128)S(1)}, u32[]{:S(2)}, u32[]{:S(2)}) %collective-permute-start.1) | collective-permute-done | bytes 6176 | tf_op jit(solution)/shard_map/ppermute | solution.py:23
  34.1 0.0 copy-done.2
  34.1 0.8 copy-done
  34.9 0.8 copy.107.low_ref
  35.7 2.1 %all-to-all-done = f32[16,32,4,128]{3,1,2,0:T(8,128)S(1)} async-done(((f32[16,32,4,128]{3,1,2,0:T(8,128)}), f32[16,32,4,128]{3,1,2,0:T(8,128)S(1)}, u32[]{:S(2)}, u32[]{:S(2)}) %all-to-all-start) | async-done | bytes 1048608 | tf_op jit(solution)/shard_map/all_to_all | solution.py:164
  37.8 0.5 fusion.9
  38.2 0.7 convert_element_type.59.req_ref
  38.9 1.0 fusion.10.cnt_ref
  40.0 1.7 %copy.106 = f32[16,32,4,128]{3,2,1,0:T(4,128)} copy(f32[16,32,4,128]{3,1,2,0:T(8,128)S(1)} %all-to-all-done) | data formatting | bytes 2097152 | tf_op jit(solution)/shard_map/all_to_all | solution.py:164
  41.6 29.1 %shard_map.77 = (f32[256,8,128]{2,1,0:T(8,128)}, f32[512,3,128]{2,1,0:T(4,128)}) custom-call(s32[16]{0:T(128)} %fusion.10.cnt_ref, s32[512]{0:T(512)} %convert_element_type.59.req_ref, f32[256,4,128]{2,1,0:T(4,128)} %pad_maximum_fusion.2.m_ref, f32[512,4,128]{2,1,0:T(4,128)} %bitcast.24, f32[3,256,2]{2,1,0:T(8,128)} %copy.107.low_ref, ...), custom_call_target="tpu_custom_call" | custom-call | tf_op jit(solution)/shard_map/pallas_call | solution.py:172
  70.7 2.2 %copy.109 = f32[16,32,3,128]{3,1,2,0:T(8,128)} copy(f32[16,32,3,128]{3,2,1,0:T(4,128)} %bitcast.26) | data formatting | bytes 1572864 | tf_op jit(solution)/shard_map/reshape | solution.py:184
  72.9 15.6 %all-to-all-start.1 = ((f32[16,32,3,128]{3,1,2,0:T(8,128)}), f32[16,32,3,128]{3,1,2,0:T(8,128)S(1)}, u32[]{:S(2)}, u32[]{:S(2)}) async-start(f32[16,32,3,128]{3,1,2,0:T(8,128)} %copy.109), calls=%async_computation.1 | async-start | bytes 1572864 | tf_op jit(solution)/shard_map/all_to_all | solution.py:183
  88.5 0.7 reshape_squeeze.5.req_ref
  89.1 0.0 copy-done.3
  89.1 0.2 constant_dynamic-update-slice_fusion
  89.3 10.7 %all-to-all-done.1 = f32[16,32,3,128]{3,1,2,0:T(8,128)S(1)} async-done(((f32[16,32,3,128]{3,1,2,0:T(8,128)}), f32[16,32,3,128]{3,1,2,0:T(8,128)S(1)}, u32[]{:S(2)}, u32[]{:S(2)}) %all-to-all-start.1) | async-done | bytes 786464 | tf_op jit(solution)/shard_map/all_to_all | solution.py:183
  100.1 1.5 %copy.110 = f32[16,32,3,128]{3,2,1,0:T(4,128)} copy(f32[16,32,3,128]{3,1,2,0:T(8,128)S(1)} %all-to-all-done.1) | data formatting | bytes 1572864 | tf_op jit(solution)/shard_map/all_to_all | solution.py:183
  101.6 4.6 %shard_map.78 = f32[256,8,128]{2,1,0:T(8,128)} custom-call(s32[512]{0:T(512)} %reshape_squeeze.5.req_ref, f32[256,8,128]{2,1,0:T(8,128)} %get-tuple-element.4.f1_ref, f32[512,3,128]{2,1,0:T(4,128)} %bitcast.25), custom_call_target="tpu_custom_call" | custom-call | tf_op jit(solution)/shard_map/pallas_call | solution.py:186
  106.2 0.0 copy-done.1
  106.2 0.0 copy-done.5
  106.2 2.7 %multiply_add_fusion = (f32[3,256,128]{2,0,1:T(4,128)S(1)}, f32[3,256,128]{2,0,1:T(4,128)S(1)}) fusion(f32[3,256,128]{2,1,0:T(8,128)S(1)} %copy-done.4, f32[256,8,128]{2,1,0:T(8,128)} %shard_map.78, f32[3,256,128]{2,0,1:T(4,128)S(1)} %get-tuple-element.24, f32[3,256,2]{2,0,1:T(4,128)S(1)} %copy-done.1, ...), kind=kLoop, calls=%fused_computation.19 | loop fusion | flops 1966080 | bytes 3151872 | tf_op jit(solution)/shard_map/add | solution.py:194
  108.9 0.8 copy.113
  109.6 0.8 copy.112
  (10 shorter events, 0.0 us)
Async XLA Ops:
  1.1 0.7 copy-start.14
  1.8 0.7 copy-start.10
  4.0 4.4 %copy-start.4 = (f32[3,256,128]{2,1,0:T(8,128)S(1)}, f32[3,256,128]{2,1,0:T(8,128)}, u32[]{:S(2)}) copy-start(f32[3,256,128]{2,1,0:T(8,128)} %param.6) | copy-start | bytes 1179652
  7.5 0.7 copy-start.8
  11.0 0.7 copy-start.6
  11.0 0.7 copy-start.7
  11.0 0.7 copy-start.13
  11.1 0.6 copy-start.9
  11.1 0.7 copy-start.11
  11.1 0.7 copy-start.12
  13.1 24.7 %all-to-all-start = ((f32[16,32,4,128]{3,1,2,0:T(8,128)}), f32[16,32,4,128]{3,1,2,0:T(8,128)S(1)}, u32[]{:S(2)}, u32[]{:S(2)}) async-start(f32[16,32,4,128]{3,1,2,0:T(8,128)} %pad_maximum_fusion), calls=%async_computation | async-start | bytes 2097152 | tf_op jit(solution)/shard_map/all_to_all | solution.py:164
  20.5 8.6 %collective-permute-start = (f32[3,256,2]{2,0,1:T(4,128)S(1)}, f32[3,256,2]{2,0,1:T(4,128)S(1)}, u32[]{:S(2)}, u32[]{:S(2)}) collective-permute-start(f32[3,256,2]{2,0,1:T(4,128)S(1)} %get-tuple-element.20), channel_id=1, source_target_pairs={{16,0},{32,16},{48,32},{64,48},{80,64},{96,80},{112,96},{128,112},... | collective-permute-start | bytes 18440 | tf_op jit(solution)/shard_map/ppermute | solution.py:26
  22.4 11.7 %collective-permute-start.1 = (f32[3,256,2]{2,0,1:T(4,128)S(1)}, f32[3,256,2]{2,0,1:T(4,128)S(1)}, u32[]{:S(2)}, u32[]{:S(2)}) collective-permute-start(f32[3,256,2]{2,0,1:T(4,128)S(1)} %get-tuple-element.21), channel_id=1, source_target_pairs={{0,16},{16,32},{32,48},{48,64},{64,80},{80,96},{96,112},{112,128},... | collective-permute-start | bytes 18440 | tf_op jit(solution)/shard_map/ppermute | solution.py:23
  29.1 5.0 %copy-start.2 = (f32[3,256,2]{2,0,1:T(4,128)}, f32[3,256,2]{2,0,1:T(4,128)S(1)}, u32[]{:S(2)}) copy-start(f32[3,256,2]{2,0,1:T(4,128)S(1)} %collective-permute-done) | copy-start | bytes 18436
  34.1 0.8 copy-start
  72.9 16.2 %copy-start.3 = (f32[3,256,2]{2,0,1:T(4,128)S(1)}, f32[3,256,2]{2,0,1:T(4,128)}, u32[]{:S(2)}) copy-start(f32[3,256,2]{2,0,1:T(4,128)} %copy-done.2) | copy-start | bytes 18436
  72.9 27.2 %all-to-all-start.1 = ((f32[16,32,3,128]{3,1,2,0:T(8,128)}), f32[16,32,3,128]{3,1,2,0:T(8,128)S(1)}, u32[]{:S(2)}, u32[]{:S(2)}) async-start(f32[16,32,3,128]{3,1,2,0:T(8,128)} %copy.109), calls=%async_computation.1 | async-start | bytes 1572864 | tf_op jit(solution)/shard_map/all_to_all | solution.py:183
  101.6 4.6 %copy-start.1 = (f32[3,256,2]{2,0,1:T(4,128)S(1)}, f32[3,256,2]{2,0,1:T(4,128)}, u32[]{:S(2)}) copy-start(f32[3,256,2]{2,0,1:T(4,128)} %copy-done) | copy-start | bytes 18436
  101.6 4.6 %copy-start.5 = (f32[3,256,128]{2,1,0:T(8,128)S(1)}, f32[3,256,128]{2,1,0:T(8,128)}, u32[]{:S(2)}) copy-start(f32[3,256,128]{2,1,0:T(8,128)} %param.7) | copy-start | bytes 1179652

commit v6 on v5

--- a/solution.py
+++ b/solution.py
@@ -1,3 +1,5 @@
+import functools
+
 import jax
 import jax.numpy as jnp
 from jax import lax
@@ -80,6 +82,29 @@
     return out
 
 
+def peer_row(slot, rows, cap):
+    return (slot // cap) * rows * cap + slot % cap
+
+
+def pack_kernel(mine_ref, their_ref, cnt_ref, rows_ref, lent_ref):
+    peers = cnt_ref.shape[0]
+    cap = mine_ref.shape[0] // peers
+    blocks = rows_ref.shape[0]
+    row = lax.broadcasted_iota(jnp.int32, (4, 128), 0)
+    lane = lax.broadcasted_iota(jnp.int32, (4, 128), 1)
+
+    def one(s, carry):
+        x = rows_ref[jnp.clip(mine_ref[s], 0, blocks - 1)]
+        theirs = their_ref[s].astype(jnp.float32)
+        live = cnt_ref[s // cap].astype(jnp.float32)
+        x = jnp.where((row == 3) & (lane == 1), theirs, x)
+        x = jnp.where((row == 3) & (lane == 2), live, x)
+        lent_ref[pl.ds(peer_row(s, 4, cap), 4, stride=cap), :] = x
+        return carry
+
+    lax.fori_loop(0, mine_ref.shape[0], one, 0, unroll=8)
+
+
 def pair_kernel(cnt_ref, req_ref, m_ref, rem_ref, low_ref, high_ref, f1_ref, f2_ref, lb_ref, ls_ref):
     f1_ref[...] = jnp.zeros(f1_ref.shape, f1_ref.dtype)
     f2_ref[...] = jnp.zeros(f2_ref.shape, f2_ref.dtype)
@@ -106,29 +131,35 @@
                 at = jnp.minimum(t, last)
                 picked.append((t, lb_ref[at], ls_ref[at]))
             (t_a, b_a, s_a), (t_b, b_b, s_b) = picked
-            rd_a, rq_a = rows_of(rem_ref[s_a], False)
-            rd_b, rq_b = rows_of(rem_ref[s_b], False)
+            rd_a, rq_a = rows_of(rem_ref[pl.ds(peer_row(s_a, 4, cap), 4, stride=cap), :], False)
+            rd_b, rq_b = rows_of(rem_ref[pl.ds(peer_row(s_b, 4, cap), 4, stride=cap), :], False)
             pair = tile_two(rows_of(m_ref[b_a], True), rows_of(m_ref[b_b], True), rd_a, rd_b, rq_a, rq_b)
             for (t, b, slot), (on_first, on_second) in zip(picked, pair):
                 done.append((b, slot, jnp.where(t < total, on_first, 0.0), on_second))
         for b, slot, on_first, on_second in done:
             f1_ref[b] = f1_ref[b] + on_first
-            f2_ref[slot] = on_second
+            f2_ref[pl.ds(peer_row(slot, 3, cap), 3, stride=cap), :] = on_second
         return carry
 
     lax.fori_loop(0, (total + tile_group - 1) // tile_group, group, 0)
 
 
-def back_kernel(req_ref, f1_ref, ret_ref, out_ref):
-    out_ref[...] = f1_ref[...]
-    blocks = out_ref.shape[0]
+def back_kernel(cap, mine_ref, f1_ref, ret_ref, vel_ref, disp_ref, beam_ref, nv_ref, nd_ref, acc_ref):
+    acc_ref[...] = f1_ref[...]
+    blocks = vel_ref.shape[1]
 
     def one(s, carry):
-        b = jnp.clip(req_ref[s], 0, blocks - 1)
-        out_ref[b, 0:3, :] = out_ref[b, 0:3, :] + ret_ref[s]
+        b = jnp.clip(mine_ref[s], 0, blocks - 1)
+        start = pl.multiple_of(b * 8, 8)
+        acc_ref[pl.ds(start, 3), :] = acc_ref[pl.ds(start, 3), :] + ret_ref[pl.ds(peer_row(s, 3, cap), 3, stride=cap), :]
         return carry
 
-    lax.fori_loop(0, ret_ref.shape[0], one, 0, unroll=8)
+    lax.fori_loop(0, mine_ref.shape[0], one, 0, unroll=8)
+    for c in range(3):
+        contact = acc_ref[pl.ds(c, blocks, stride=8), :]
+        new_velocity = damping * vel_ref[c] + time_step * (beam_ref[c] + contact)
+        nv_ref[c] = new_velocity
+        nd_ref[c] = disp_ref[c] + time_step * new_velocity
 
 
 def local(displacement, velocity, anchors, seg_live, pair_blocks, pair_count):
@@ -151,47 +182,47 @@
     meta = jnp.where(lanes[None, :] == 0, seg_count[:, None], 0.0)
     my_rows = jnp.concatenate([blocks, meta[:, None, :]], axis=1)
 
-    mine_ids = pair_blocks[0, 0, :, :, 0]
-    their_ids = pair_blocks[0, 0, :, :, 1].astype(jnp.float32)
-    live_to = jnp.broadcast_to(pair_count[0, 0].astype(jnp.float32)[:, None], their_ids.shape)
-    mine_flat = mine_ids.reshape(slot_total)
-    sent_meta = jnp.where(
-        lanes == 0, seg_count[mine_flat][:, None],
-        jnp.where(lanes == 1, their_ids.reshape(slot_total)[:, None],
-                  jnp.where(lanes == 2, live_to.reshape(slot_total)[:, None], 0.0)),
-    )
-    lent = jnp.concatenate([blocks[mine_flat], sent_meta[:, None, :]], axis=1)
-    remote = lax.all_to_all(
-        lent.reshape(peer_total, slot_cap, 4, 128), ("xa", "xb"), split_axis=0, concat_axis=0, tiled=True
-    )
-    req_ids = remote[:, :, 3, 1].astype(jnp.int32).reshape(slot_total)
-    live_from = remote[:, 0, 3, 2].astype(jnp.int32)
-
+    mine_flat = pair_blocks[0, 0, :, :, 0].reshape(slot_total)
+    their_flat = pair_blocks[0, 0, :, :, 1].reshape(slot_total)
     smem = pl.BlockSpec(memory_space=pltpu.SMEM)
     vmem = pl.BlockSpec(memory_space=pltpu.VMEM)
+    lent = pl.pallas_call(
+        pack_kernel,
+        out_shape=jax.ShapeDtypeStruct((peer_total * 4 * slot_cap, 128), jnp.float32),
+        in_specs=[smem, smem, smem, vmem],
+        out_specs=vmem,
+    )(mine_flat, their_flat, pair_count[0, 0], my_rows)
+    remote = lax.all_to_all(
+        lent.reshape(peer_total, 4, slot_cap, 128), ("xa", "xb"), split_axis=0, concat_axis=0, tiled=True
+    )
+    req_ids = remote[:, 3, :, 1].astype(jnp.int32).reshape(slot_total)
+    live_from = remote[:, 3, 0, 2].astype(jnp.int32)
+
     f1, f2 = pl.pallas_call(
         pair_kernel,
         out_shape=(
             jax.ShapeDtypeStruct((block_total, 8, 128), jnp.float32),
-            jax.ShapeDtypeStruct((slot_total, 3, 128), jnp.float32),
+            jax.ShapeDtypeStruct((peer_total * 3 * slot_cap, 128), jnp.float32),
         ),
         in_specs=[smem, smem, vmem, vmem, vmem, vmem],
         out_specs=(vmem, vmem),
         scratch_shapes=[pltpu.SMEM((slot_total,), jnp.int32), pltpu.SMEM((slot_total,), jnp.int32)],
-    )(live_from, req_ids, my_rows, remote.reshape(slot_total, 4, 128), halo_low, halo_high)
+    )(live_from, req_ids, my_rows, remote.reshape(peer_total * 4 * slot_cap, 128), halo_low, halo_high)
 
     returned = lax.all_to_all(
-        f2.reshape(peer_total, slot_cap, 3, 128), ("xa", "xb"), split_axis=0, concat_axis=0, tiled=True
-    )
-    acc = pl.pallas_call(
-        back_kernel,
-        out_shape=jax.ShapeDtypeStruct((block_total, 8, 128), jnp.float32),
-        in_specs=[smem, vmem, vmem],
-        out_specs=vmem,
-    )(mine_flat, f1, returned.reshape(slot_total, 3, 128))
-    contact = acc[:, 0:3, :].transpose(1, 0, 2).reshape(3, fibre_count, seg_len)
-    new_velocity = damping * velocity + time_step * (beam + contact)
-    new_displacement = displacement + time_step * new_velocity
+        f2.reshape(peer_total, 3, slot_cap, 128), ("xa", "xb"), split_axis=0, concat_axis=0, tiled=True
+    )
+    new_velocity, new_displacement = pl.pallas_call(
+        functools.partial(back_kernel, slot_cap),
+        out_shape=(
+            jax.ShapeDtypeStruct(velocity.shape, jnp.float32),
+            jax.ShapeDtypeStruct(displacement.shape, jnp.float32),
+        ),
+        in_specs=[smem, vmem, vmem, vmem, vmem, vmem],
+        out_specs=(vmem, vmem),
+        scratch_shapes=[pltpu.VMEM((block_total * 8, 128), jnp.float32)],
+    )(mine_flat, f1.reshape(block_total * 8, 128), returned.reshape(peer_total * 3 * slot_cap, 128),
+      velocity, displacement, beam)
     return (new_velocity, new_displacement)
 
 

time: 111 us -> 104 us (0.937)
  the two profiles are of different devices: /device:TPU:256 before, /device:TPU:1 now
where the time goes in v6:
time: 104 us
  Pallas kernels  40.6 us (39%)
  starting transfers between devices  30.9 us (30%)
  waiting for transfers between devices  18.3 us (18%)
  local copies, waits for them, and re-layouts  7.44 us (7%)
  other arithmetic  5.5 us (5%)
    pallas_call x1, Pallas kernels, local(): pl.pallas_call(pair_kernel, out_shape=(jax.ShapeDtypeStruct((block_total,...  25.5 us
    all_to_all x1, starting transfers between devices, local(): lax.all_to_all(f2.reshape(peer_total, 3, slot_cap, 128), ('xa', 'xb'), sp...  16.9 us
    all_to_all x1, waiting for transfers between devices, local(): lax.all_to_all(f2.reshape(peer_total, 3, slot_cap, 128), ('xa', 'xb'), sp...  10.4 us
    all_to_all x1, waiting for transfers between devices, local(): lax.all_to_all(lent.reshape(peer_total, 4, slot_cap, 128), ('xa', 'xb'),...  7.97 us
    all_to_all x1, starting transfers between devices, local(): lax.all_to_all(lent.reshape(peer_total, 4, slot_cap, 128), ('xa', 'xb'),...  7.72 us
    pallas_call x1, Pallas kernels, local(): pl.pallas_call(pack_kernel, out_shape=jax.ShapeDtypeStruct((peer_total *...  7.68 us
    pallas_call x1, Pallas kernels, local(): pl.pallas_call(functools.partial(back_kernel, slot_cap), out_shape=(jax.S...  7.42 us
    unnamed x20, local copies, waits for them, and re-layouts  4.41 us
  transfers between devices with their start and end apart: 4, of which 2 were waited for; matrix products, arithmetic and copies ran while one was open for 4% of the time, Pallas kernels for 0%

profile of v6, /device:TPU:1, one launch (start us, length us, event | category | flops | bytes accessed | tf_op | source)
XLA Modules:
  0.0 103.5 jit_solution(14805757245171819797)
XLA Ops:
  0.7 0.8 slice_reduce_fusion
  1.5 0.0 copy-start.7
  1.5 0.7 reshape_squeeze.6.mine_ref
  2.2 0.0 copy-done.7
  2.2 0.0 copy-start.8
  2.2 0.1 copy.20
  2.3 0.5 copy-done.8
  2.9 0.7 reshape_squeeze.7.their_ref
  3.5 0.3 broadcast_select_fusion
  3.9 1.4 %fusion.1 = f32[256,3,128]{2,1,0:T(4,128)S(1)} fusion(f32[3,256,128]{2,1,0:T(8,128)} %disp_ref.1, f32[3,128]{1,0:T(4,128)S(1)} %stack.2, f32[3,256]{0,1:T(8,128)S(1)} %copy.20), kind=kLoop, calls=%fused_computation.5 | loop fusion | flops 196608 | bytes 791040 | tf_op jit(solution)/shard_map/transpose | solution.py:179
  5.2 1.0 %pad_maximum_fusion.rows_ref.m_ref = f32[256,4,128]{2,1,0:T(4,128)} fusion(f32[256,1,128]{2,1,0:T(1,128)S(1)} %broadcast_select_fusion, f32[256,3,128]{2,1,0:T(4,128)S(1)} %fusion.1), kind=kLoop, calls=%fused_computation.2 | loop fusion | flops 131072 | bytes 1048576 | tf_op jit(solution)/shard_map/concatenate | solution.py:183
  6.3 7.7 %shard_map.77 = f32[2048,128]{1,0:T(8,128)} custom-call(s32[512]{0:T(512)} %reshape_squeeze.6.mine_ref, s32[512]{0:T(512)} %reshape_squeeze.7.their_ref, s32[16]{0:T(128)} %bitcast.15, f32[256,4,128]{2,1,0:T(4,128)} %pad_maximum_fusion.rows_ref.m_ref), custom_call_target="tpu_custom_call" | custom-call | tf_op jit(solution)/shard_map/pallas_call | solution.py:189
  14.0 0.0 copy-start
  14.0 7.7 %all-to-all-start = ((f32[16,4,32,128]{3,2,1,0:T(8,128)}), f32[16,4,32,128]{3,2,1,0:T(8,128)S(1)}, u32[]{:S(2)}, u32[]{:S(2)}) async-start(f32[16,4,32,128]{3,2,1,0:T(8,128)} %bitcast.10), calls=%async_computation | async-start | bytes 2097152 | tf_op jit(solution)/shard_map/all_to_all | solution.py:195
  21.7 0.0 copy-done
  21.7 0.2 fusion.10
  21.9 4.4 %collective-permute-start = (f32[3,256,2]{2,1,0:T(8,128)S(1)}, f32[3,256,2]{2,1,0:T(8,128)S(1)}, u32[]{:S(2)}, u32[]{:S(2)}) collective-permute-start(f32[3,256,2]{2,1,0:T(8,128)S(1)} %get-tuple-element.9), channel_id=1, source_target_pairs={{0,16},{16,32},{32,48},{48,64},{64,80},{80,96},{96,112},{112,128},... | collective-permute-start | bytes 18440 | tf_op jit(solution)/shard_map/ppermute | solution.py:25
  26.3 1.9 %collective-permute-start.1 = (f32[3,256,2]{2,1,0:T(8,128)S(1)}, f32[3,256,2]{2,1,0:T(8,128)S(1)}, u32[]{:S(2)}, u32[]{:S(2)}) collective-permute-start(f32[3,256,2]{2,1,0:T(8,128)S(1)} %get-tuple-element.8), channel_id=1, source_target_pairs={{16,0},{32,16},{48,32},{64,48},{80,64},{96,80},{112,96},{128,112},... | collective-permute-start | bytes 18440 | tf_op jit(solution)/shard_map/ppermute | solution.py:28
  28.2 8.0 %all-to-all-done = f32[16,4,32,128]{3,2,1,0:T(8,128)S(1)} async-done(((f32[16,4,32,128]{3,2,1,0:T(8,128)}), f32[16,4,32,128]{3,2,1,0:T(8,128)S(1)}, u32[]{:S(2)}, u32[]{:S(2)}) %all-to-all-start) | async-done | bytes 1048608 | tf_op jit(solution)/shard_map/all_to_all | solution.py:195
  36.2 0.0 copy-start.1
  36.2 0.5 fusion.8
  36.6 0.9 fusion.9.cnt_ref
  37.6 0.7 convert_element_type.34.req_ref
  38.3 0.0 collective-permute-done.low_ref
  38.3 0.0 copy-start.5
  38.3 0.0 collective-permute-done.1.high_ref
  38.3 0.0 copy-start.3
  38.3 0.0 copy-done.1
  38.3 0.7 copy-done.5
  39.0 0.1 copy-done.3
  39.1 25.5 %shard_map.78 = (f32[256,8,128]{2,1,0:T(8,128)}, f32[1536,128]{1,0:T(8,128)}) custom-call(s32[16]{0:T(128)} %fusion.9.cnt_ref, s32[512]{0:T(512)} %convert_element_type.34.req_ref, f32[256,4,128]{2,1,0:T(4,128)} %pad_maximum_fusion.rows_ref.m_ref, f32[2048,128]{1,0:T(8,128)} %bitcast.9, f32[3,256,2]{2,1,0:T(8,128)} %copy-done.5, f32[3,256,2]{2,1,0:T(8,128)} %copy-done.3), custom_call_target="tpu_custom_call" | custom-call | tf_op jit(solution)/shard_map/pallas_call | solution.py:201
  64.6 16.9 %all-to-all-start.1 = ((f32[16,3,32,128]{3,2,1,0:T(8,128)}), f32[16,3,32,128]{3,2,1,0:T(8,128)S(1)}, u32[]{:S(2)}, u32[]{:S(2)}) async-start(f32[16,3,32,128]{3,2,1,0:T(8,128)} %bitcast.13), calls=%async_computation.1 | async-start | bytes 1572864 | tf_op jit(solution)/shard_map/all_to_all | solution.py:212
  81.5 0.0 copy-start.4
  81.6 1.0 copy-done.4
  82.5 0.0 copy-start.6
  82.5 1.0 copy-done.6
  83.5 1.3 %fusion.5.beam_ref = f32[3,256,128]{2,1,0:T(8,128)} fusion(f32[3,256,128]{2,1,0:T(8,128)S(1)} %copy-done, f32[3,256,2]{2,1,0:T(8,128)S(1)} %copy-done.6, f32[3,256,130]{2,1,0:T(8,128)S(1)} %constant_dynamic-update-slice_fusion), kind=kLoop, calls=%fused_computation.10 | loop fusion | flops 1376256 | bytes 1579008 | tf_op jit(solution)/shard_map/sub | solution.py:40
  84.8 10.4 %all-to-all-done.1 = f32[16,3,32,128]{3,2,1,0:T(8,128)S(1)} async-done(((f32[16,3,32,128]{3,2,1,0:T(8,128)}), f32[16,3,32,128]{3,2,1,0:T(8,128)S(1)}, u32[]{:S(2)}, u32[]{:S(2)}) %all-to-all-start.1) | async-done | bytes 786464 | tf_op jit(solution)/shard_map/all_to_all | solution.py:212
  95.2 0.0 copy-start.2
  95.2 0.9 copy-done.2
  96.1 7.4 %shard_map.79 = (f32[3,256,128]{2,1,0:T(8,128)}, f32[3,256,128]{2,1,0:T(8,128)}) custom-call(s32[512]{0:T(512)} %reshape_squeeze.6.mine_ref, f32[2048,128]{1,0:T(8,128)} %bitcast.12, f32[1536,128]{1,0:T(8,128)} %bitcast.11, f32[3,256,128]{2,1,0:T(8,128)} %vel_ref.1, f32[3,256,128]{2,1,0:T(8,128)} %disp_ref.1, f32[3,256,128]{2,1,0:T(8,128)} %fusion.5.beam_ref), custom_call_target="tpu_custom_call" | custom-call | tf_op jit(solution)/shard_map/pallas_call | solution.py:215
  (6 shorter events, 0.1 us)
Async XLA Ops:
  1.5 0.7 copy-start.7
  2.2 0.7 copy-start.8
  14.0 7.7 %copy-start = (f32[3,256,128]{2,1,0:T(8,128)S(1)}, f32[3,256,128]{2,1,0:T(8,128)}, u32[]{:S(2)}) copy-start(f32[3,256,128]{2,1,0:T(8,128)} %disp_ref.1) | copy-start | bytes 1179652
  14.0 22.2 %all-to-all-start = ((f32[16,4,32,128]{3,2,1,0:T(8,128)}), f32[16,4,32,128]{3,2,1,0:T(8,128)S(1)}, u32[]{:S(2)}, u32[]{:S(2)}) async-start(f32[16,4,32,128]{3,2,1,0:T(8,128)} %bitcast.10), calls=%async_computation | async-start | bytes 2097152 | tf_op jit(solution)/shard_map/all_to_all | solution.py:195
  21.9 16.4 %collective-permute-start = (f32[3,256,2]{2,1,0:T(8,128)S(1)}, f32[3,256,2]{2,1,0:T(8,128)S(1)}, u32[]{:S(2)}, u32[]{:S(2)}) collective-permute-start(f32[3,256,2]{2,1,0:T(8,128)S(1)} %get-tuple-element.9), channel_id=1, source_target_pairs={{0,16},{16,32},{32,48},{48,64},{64,80},{80,96},{96,112},{112,128},... | collective-permute-start | bytes 18440 | tf_op jit(solution)/shard_map/ppermute | solution.py:25
  26.3 12.0 %collective-permute-start.1 = (f32[3,256,2]{2,1,0:T(8,128)S(1)}, f32[3,256,2]{2,1,0:T(8,128)S(1)}, u32[]{:S(2)}, u32[]{:S(2)}) collective-permute-start(f32[3,256,2]{2,1,0:T(8,128)S(1)} %get-tuple-element.8), channel_id=1, source_target_pairs={{16,0},{32,16},{48,32},{64,48},{80,64},{96,80},{112,96},{128,112},... | collective-permute-start | bytes 18440 | tf_op jit(solution)/shard_map/ppermute | solution.py:28
  36.2 2.1 %copy-start.1 = (f32[16,4,32,128]{3,2,1,0:T(8,128)}, f32[16,4,32,128]{3,2,1,0:T(8,128)S(1)}, u32[]{:S(2)}) copy-start(f32[16,4,32,128]{3,2,1,0:T(8,128)S(1)} %all-to-all-done) | copy-start | bytes 3145732
  38.3 0.7 copy-start.5
  38.3 0.9 copy-start.3
  64.6 30.6 %all-to-all-start.1 = ((f32[16,3,32,128]{3,2,1,0:T(8,128)}), f32[16,3,32,128]{3,2,1,0:T(8,128)S(1)}, u32[]{:S(2)}, u32[]{:S(2)}) async-start(f32[16,3,32,128]{3,2,1,0:T(8,128)} %bitcast.13), calls=%async_computation.1 | async-start | bytes 1572864 | tf_op jit(solution)/shard_map/all_to_all | solution.py:212
  81.5 1.0 copy-start.4
  82.5 1.0 copy-start.6
  95.2 0.9 copy-start.2

commit v7 on v6

--- a/solution.py
+++ b/solution.py
@@ -93,16 +93,22 @@
     row = lax.broadcasted_iota(jnp.int32, (4, 128), 0)
     lane = lax.broadcasted_iota(jnp.int32, (4, 128), 1)
 
-    def one(s, carry):
-        x = rows_ref[jnp.clip(mine_ref[s], 0, blocks - 1)]
-        theirs = their_ref[s].astype(jnp.float32)
-        live = cnt_ref[s // cap].astype(jnp.float32)
-        x = jnp.where((row == 3) & (lane == 1), theirs, x)
-        x = jnp.where((row == 3) & (lane == 2), live, x)
-        lent_ref[pl.ds(peer_row(s, 4, cap), 4, stride=cap), :] = x
-        return carry
-
-    lax.fori_loop(0, mine_ref.shape[0], one, 0, unroll=8)
+    lent_ref[...] = jnp.zeros(lent_ref.shape, lent_ref.dtype)
+
+    def peer(d, carry):
+        live = cnt_ref[d]
+
+        def one(c, carry):
+            s = d * cap + c
+            x = rows_ref[jnp.clip(mine_ref[s], 0, blocks - 1)]
+            x = jnp.where((row == 3) & (lane == 1), their_ref[s].astype(jnp.float32), x)
+            x = jnp.where((row == 3) & (lane == 2), live.astype(jnp.float32), x)
+            lent_ref[pl.ds(d * 4 * cap + c, 4, stride=cap), :] = x
+            return carry
+
+        return lax.fori_loop(0, jnp.clip(live, 1, cap), one, carry)
+
+    lax.fori_loop(0, peers, peer, 0)
 
 
 def pair_kernel(cnt_ref, req_ref, m_ref, rem_ref, low_ref, high_ref, f1_ref, f2_ref, lb_ref, ls_ref):
@@ -144,17 +150,23 @@
     lax.fori_loop(0, (total + tile_group - 1) // tile_group, group, 0)
 
 
-def back_kernel(cap, mine_ref, f1_ref, ret_ref, vel_ref, disp_ref, beam_ref, nv_ref, nd_ref, acc_ref):
+def back_kernel(cap, mine_ref, cnt_ref, f1_ref, ret_ref, vel_ref, disp_ref, beam_ref, nv_ref, nd_ref, acc_ref):
     acc_ref[...] = f1_ref[...]
     blocks = vel_ref.shape[1]
 
-    def one(s, carry):
-        b = jnp.clip(mine_ref[s], 0, blocks - 1)
-        start = pl.multiple_of(b * 8, 8)
-        acc_ref[pl.ds(start, 3), :] = acc_ref[pl.ds(start, 3), :] + ret_ref[pl.ds(peer_row(s, 3, cap), 3, stride=cap), :]
-        return carry
-
-    lax.fori_loop(0, mine_ref.shape[0], one, 0, unroll=8)
+    def peer(d, carry):
+        def one(c, carry):
+            s = d * cap + c
+            b = jnp.clip(mine_ref[s], 0, blocks - 1)
+            start = pl.multiple_of(b * 8, 8)
+            acc_ref[pl.ds(start, 3), :] = (
+                acc_ref[pl.ds(start, 3), :] + ret_ref[pl.ds(d * 3 * cap + c, 3, stride=cap), :]
+            )
+            return carry
+
+        return lax.fori_loop(0, jnp.clip(cnt_ref[d], 0, cap), one, carry)
+
+    lax.fori_loop(0, cnt_ref.shape[0], peer, 0)
     for c in range(3):
         contact = acc_ref[pl.ds(c, blocks, stride=8), :]
         new_velocity = damping * vel_ref[c] + time_step * (beam_ref[c] + contact)
@@ -218,10 +230,10 @@
             jax.ShapeDtypeStruct(velocity.shape, jnp.float32),
             jax.ShapeDtypeStruct(displacement.shape, jnp.float32),
         ),
-        in_specs=[smem, vmem, vmem, vmem, vmem, vmem],
+        in_specs=[smem, smem, vmem, vmem, vmem, vmem, vmem],
         out_specs=(vmem, vmem),
         scratch_shapes=[pltpu.VMEM((block_total * 8, 128), jnp.float32)],
-    )(mine_flat, f1.reshape(block_total * 8, 128), returned.reshape(peer_total * 3 * slot_cap, 128),
+    )(mine_flat, pair_count[0, 0], f1.reshape(block_total * 8, 128), returned.reshape(peer_total * 3 * slot_cap, 128),
       velocity, displacement, beam)
     return (new_velocity, new_displacement)
 

time: 104 us -> 106 us (1.019)
  the two profiles are of different devices: /device:TPU:1 before, /device:TPU:96 now
where the time goes in v7:
time: 106 us
  Pallas kernels  46.6 us (44%)
  starting transfers between devices  25.3 us (24%)
  waiting for transfers between devices  20 us (19%)
  local copies, waits for them, and re-layouts  7.44 us (7%)
  other arithmetic  5.5 us (5%)
    pallas_call x1, Pallas kernels, local(): pl.pallas_call(pair_kernel, out_shape=(jax.ShapeDtypeStruct((block_total,...  34.6 us
    all_to_all x1, starting transfers between devices, local(): lax.all_to_all(f2.reshape(peer_total, 3, slot_cap, 128), ('xa', 'xb'), sp...  12.6 us
    all_to_all x1, waiting for transfers between devices, local(): lax.all_to_all(lent.reshape(peer_total, 4, slot_cap, 128), ('xa', 'xb'),...  11.7 us
    all_to_all x1, waiting for transfers between devices, local(): lax.all_to_all(f2.reshape(peer_total, 3, slot_cap, 128), ('xa', 'xb'), sp...  8.25 us
    all_to_all x1, starting transfers between devices, local(): lax.all_to_all(lent.reshape(peer_total, 4, slot_cap, 128), ('xa', 'xb'),...  7.17 us
    pallas_call x1, Pallas kernels, local(): pl.pallas_call(functools.partial(back_kernel, slot_cap), out_shape=(jax.S...  6.11 us
    pallas_call x1, Pallas kernels, local(): pl.pallas_call(pack_kernel, out_shape=jax.ShapeDtypeStruct((peer_total *...  5.8 us
    unnamed x20, local copies, waits for them, and re-layouts  4.41 us
  transfers between devices with their start and end apart: 4, of which 2 were waited for; matrix products, arithmetic and copies ran while one was open for 3% of the time, Pallas kernels for 0%

profile of v7, /device:TPU:96, one launch (start us, length us, event | category | flops | bytes accessed | tf_op | source)
XLA Modules:
  0.0 105.6 jit_solution(10741938346688726024)
XLA Ops:
  0.7 0.8 slice_reduce_fusion
  1.5 0.0 copy-start.7
  1.5 0.7 reshape_squeeze.6.mine_ref
  2.2 0.0 copy-done.7
  2.2 0.0 copy-start.8
  2.2 0.1 copy.20
  2.3 0.5 copy-done.8
  2.9 0.7 reshape_squeeze.7.their_ref
  3.5 0.3 broadcast_select_fusion
  3.9 1.4 %fusion.1 = f32[256,3,128]{2,1,0:T(4,128)S(1)} fusion(f32[3,256,128]{2,1,0:T(8,128)} %disp_ref.1, f32[3,128]{1,0:T(4,128)S(1)} %stack.2, f32[3,256]{0,1:T(8,128)S(1)} %copy.20), kind=kLoop, calls=%fused_computation.5 | loop fusion | flops 196608 | bytes 791040 | tf_op jit(solution)/shard_map/transpose | solution.py:191
  5.2 1.0 pad_maximum_fusion.rows_ref.m_ref
  6.3 5.8 %shard_map.77 = f32[2048,128]{1,0:T(8,128)} custom-call(s32[512]{0:T(512)} %reshape_squeeze.6.mine_ref, s32[512]{0:T(512)} %reshape_squeeze.7.their_ref, s32[16]{0:T(128)} %bitcast.15, f32[256,4,128]{2,1,0:T(4,128)} %pad_maximum_fusion.rows_ref.m_ref), custom_call_target="tpu_custom_call" | custom-call | tf_op jit(solution)/shard_map/pallas_call | solution.py:201
  12.1 0.0 copy-start
  12.1 7.2 %all-to-all-start = ((f32[16,4,32,128]{3,2,1,0:T(8,128)}), f32[16,4,32,128]{3,2,1,0:T(8,128)S(1)}, u32[]{:S(2)}, u32[]{:S(2)}) async-start(f32[16,4,32,128]{3,2,1,0:T(8,128)} %bitcast.10), calls=%async_computation | async-start | bytes 2097152 | tf_op jit(solution)/shard_map/all_to_all | solution.py:207
  19.3 0.0 copy-done
  19.3 0.2 fusion.10
  19.5 1.9 %collective-permute-start = (f32[3,256,2]{2,1,0:T(8,128)S(1)}, f32[3,256,2]{2,1,0:T(8,128)S(1)}, u32[]{:S(2)}, u32[]{:S(2)}) collective-permute-start(f32[3,256,2]{2,1,0:T(8,128)S(1)} %get-tuple-element.9), channel_id=1, source_target_pairs={{0,16},{16,32},{32,48},{48,64},{64,80},{80,96},{96,112},{112,128},... | collective-permute-start | bytes 18440 | tf_op jit(solution)/shard_map/ppermute | solution.py:25
  21.4 3.6 %collective-permute-start.1 = (f32[3,256,2]{2,1,0:T(8,128)S(1)}, f32[3,256,2]{2,1,0:T(8,128)S(1)}, u32[]{:S(2)}, u32[]{:S(2)}) collective-permute-start(f32[3,256,2]{2,1,0:T(8,128)S(1)} %get-tuple-element.8), channel_id=1, source_target_pairs={{16,0},{32,16},{48,32},{64,48},{80,64},{96,80},{112,96},{128,112},... | collective-permute-start | bytes 18440 | tf_op jit(solution)/shard_map/ppermute | solution.py:28
  25.0 11.7 %all-to-all-done = f32[16,4,32,128]{3,2,1,0:T(8,128)S(1)} async-done(((f32[16,4,32,128]{3,2,1,0:T(8,128)}), f32[16,4,32,128]{3,2,1,0:T(8,128)S(1)}, u32[]{:S(2)}, u32[]{:S(2)}) %all-to-all-start) | async-done | bytes 1048608 | tf_op jit(solution)/shard_map/all_to_all | solution.py:207
  36.8 0.0 copy-start.1
  36.8 0.5 fusion.8
  37.2 0.9 fusion.9.cnt_ref
  38.2 0.7 convert_element_type.34.req_ref
  38.8 0.0 collective-permute-done.low_ref
  38.9 0.0 copy-start.5
  38.9 0.0 collective-permute-done.1.high_ref
  38.9 0.0 copy-start.3
  38.9 0.0 copy-done.1
  38.9 0.7 copy-done.5
  39.6 0.1 copy-done.3
  39.7 34.6 %shard_map.78 = (f32[256,8,128]{2,1,0:T(8,128)}, f32[1536,128]{1,0:T(8,128)}) custom-call(s32[16]{0:T(128)} %fusion.9.cnt_ref, s32[512]{0:T(512)} %convert_element_type.34.req_ref, f32[256,4,128]{2,1,0:T(4,128)} %pad_maximum_fusion.rows_ref.m_ref, f32[2048,128]{1,0:T(8,128)} %bitcast.9, f32[3,256,2]{2,1,0:T(8,128)} %copy-done.5, f32[3,256,2]{2,1,0:T(8,128)} %copy-done.3), custom_call_target="tpu_custom_call" | custom-call | tf_op jit(solution)/shard_map/pallas_call | solution.py:213
  74.4 12.6 %all-to-all-start.1 = ((f32[16,3,32,128]{3,2,1,0:T(8,128)}), f32[16,3,32,128]{3,2,1,0:T(8,128)S(1)}, u32[]{:S(2)}, u32[]{:S(2)}) async-start(f32[16,3,32,128]{3,2,1,0:T(8,128)} %bitcast.13), calls=%async_computation.1 | async-start | bytes 1572864 | tf_op jit(solution)/shard_map/all_to_all | solution.py:224
  87.0 0.0 copy-start.4
  87.0 1.0 copy-done.4
  88.0 0.0 copy-start.6
  88.0 1.0 copy-done.6
  89.0 1.3 %fusion.5.beam_ref = f32[3,256,128]{2,1,0:T(8,128)} fusion(f32[3,256,128]{2,1,0:T(8,128)S(1)} %copy-done, f32[3,256,2]{2,1,0:T(8,128)S(1)} %copy-done.6, f32[3,256,130]{2,1,0:T(8,128)S(1)} %constant_dynamic-update-slice_fusion), kind=kLoop, calls=%fused_computation.10 | loop fusion | flops 1376256 | bytes 1579008 | tf_op jit(solution)/shard_map/sub | solution.py:40
  90.3 8.2 %all-to-all-done.1 = f32[16,3,32,128]{3,2,1,0:T(8,128)S(1)} async-done(((f32[16,3,32,128]{3,2,1,0:T(8,128)}), f32[16,3,32,128]{3,2,1,0:T(8,128)S(1)}, u32[]{:S(2)}, u32[]{:S(2)}) %all-to-all-start.1) | async-done | bytes 786464 | tf_op jit(solution)/shard_map/all_to_all | solution.py:224
  98.6 0.0 copy-start.2
  98.6 0.9 copy-done.2
  99.5 6.1 %shard_map.79 = (f32[3,256,128]{2,1,0:T(8,128)}, f32[3,256,128]{2,1,0:T(8,128)}) custom-call(s32[512]{0:T(512)} %reshape_squeeze.6.mine_ref, s32[16]{0:T(128)} %bitcast.16, f32[2048,128]{1,0:T(8,128)} %bitcast.12, f32[1536,128]{1,0:T(8,128)} %bitcast.11, f32[3,256,128]{2,1,0:T(8,128)} %vel_ref.1, f32[3,256,128]{2,1,0:T(8,128)} %disp_ref.1, ...), custom_call_target="tpu_custom_call" | custom-call | tf_op jit(solution)/shard_map/pallas_call | solution.py:227
  (6 shorter events, 0.1 us)
Async XLA Ops:
  1.5 0.7 copy-start.7
  2.2 0.7 copy-start.8
  12.1 7.2 %copy-start = (f32[3,256,128]{2,1,0:T(8,128)S(1)}, f32[3,256,128]{2,1,0:T(8,128)}, u32[]{:S(2)}) copy-start(f32[3,256,128]{2,1,0:T(8,128)} %disp_ref.1) | copy-start | bytes 1179652
  12.1 24.7 %all-to-all-start = ((f32[16,4,32,128]{3,2,1,0:T(8,128)}), f32[16,4,32,128]{3,2,1,0:T(8,128)S(1)}, u32[]{:S(2)}, u32[]{:S(2)}) async-start(f32[16,4,32,128]{3,2,1,0:T(8,128)} %bitcast.10), calls=%async_computation | async-start | bytes 2097152 | tf_op jit(solution)/shard_map/all_to_all | solution.py:207
  19.5 19.4 %collective-permute-start = (f32[3,256,2]{2,1,0:T(8,128)S(1)}, f32[3,256,2]{2,1,0:T(8,128)S(1)}, u32[]{:S(2)}, u32[]{:S(2)}) collective-permute-start(f32[3,256,2]{2,1,0:T(8,128)S(1)} %get-tuple-element.9), channel_id=1, source_target_pairs={{0,16},{16,32},{32,48},{48,64},{64,80},{80,96},{96,112},{112,128},... | collective-permute-start | bytes 18440 | tf_op jit(solution)/shard_map/ppermute | solution.py:25
  21.4 17.5 %collective-permute-start.1 = (f32[3,256,2]{2,1,0:T(8,128)S(1)}, f32[3,256,2]{2,1,0:T(8,128)S(1)}, u32[]{:S(2)}, u32[]{:S(2)}) collective-permute-start(f32[3,256,2]{2,1,0:T(8,128)S(1)} %get-tuple-element.8), channel_id=1, source_target_pairs={{16,0},{32,16},{48,32},{64,48},{80,64},{96,80},{112,96},{128,112},... | collective-permute-start | bytes 18440 | tf_op jit(solution)/shard_map/ppermute | solution.py:28
  36.8 2.1 %copy-start.1 = (f32[16,4,32,128]{3,2,1,0:T(8,128)}, f32[16,4,32,128]{3,2,1,0:T(8,128)S(1)}, u32[]{:S(2)}) copy-start(f32[16,4,32,128]{3,2,1,0:T(8,128)S(1)} %all-to-all-done) | copy-start | bytes 3145732
  38.9 0.7 copy-start.5
  38.9 0.9 copy-start.3
  74.4 24.2 %all-to-all-start.1 = ((f32[16,3,32,128]{3,2,1,0:T(8,128)}), f32[16,3,32,128]{3,2,1,0:T(8,128)S(1)}, u32[]{:S(2)}, u32[]{:S(2)}) async-start(f32[16,3,32,128]{3,2,1,0:T(8,128)} %bitcast.13), calls=%async_computation.1 | async-start | bytes 1572864 | tf_op jit(solution)/shard_map/all_to_all | solution.py:224
  87.0 1.0 copy-start.4
  88.0 1.0 copy-start.6
  98.6 0.9 copy-start.2

commit v8 on v7

--- a/solution.py
+++ b/solution.py
@@ -15,7 +15,8 @@
 damping = 0.9
 masked_far = 1.0e4
 HIGH = lax.Precision.HIGH
-tile_group = 8
+tile_group = 16
+slot_step = 4
 
 
 def halos(block, axis, dim, width):
@@ -98,15 +99,19 @@
     def peer(d, carry):
         live = cnt_ref[d]
 
-        def one(c, carry):
-            s = d * cap + c
-            x = rows_ref[jnp.clip(mine_ref[s], 0, blocks - 1)]
-            x = jnp.where((row == 3) & (lane == 1), their_ref[s].astype(jnp.float32), x)
-            x = jnp.where((row == 3) & (lane == 2), live.astype(jnp.float32), x)
-            lent_ref[pl.ds(d * 4 * cap + c, 4, stride=cap), :] = x
+        sent = jnp.clip(live, 1, cap)
+
+        def step(g, carry):
+            for k in range(slot_step):
+                c = jnp.minimum(g * slot_step + k, sent - 1)
+                s = d * cap + c
+                x = rows_ref[jnp.clip(mine_ref[s], 0, blocks - 1)]
+                x = jnp.where((row == 3) & (lane == 1), their_ref[s].astype(jnp.float32), x)
+                x = jnp.where((row == 3) & (lane == 2), live.astype(jnp.float32), x)
+                lent_ref[pl.ds(d * 4 * cap + c, 4, stride=cap), :] = x
             return carry
 
-        return lax.fori_loop(0, jnp.clip(live, 1, cap), one, carry)
+        return lax.fori_loop(0, (sent + slot_step - 1) // slot_step, step, carry)
 
     lax.fori_loop(0, peers, peer, 0)
 
@@ -155,16 +160,19 @@
     blocks = vel_ref.shape[1]
 
     def peer(d, carry):
-        def one(c, carry):
-            s = d * cap + c
-            b = jnp.clip(mine_ref[s], 0, blocks - 1)
-            start = pl.multiple_of(b * 8, 8)
-            acc_ref[pl.ds(start, 3), :] = (
-                acc_ref[pl.ds(start, 3), :] + ret_ref[pl.ds(d * 3 * cap + c, 3, stride=cap), :]
-            )
+        live = jnp.clip(cnt_ref[d], 0, cap)
+
+        def step(g, carry):
+            for k in range(slot_step):
+                c = g * slot_step + k
+                at = jnp.minimum(c, live - 1)
+                b = jnp.clip(mine_ref[d * cap + at], 0, blocks - 1)
+                start = pl.multiple_of(b * 8, 8)
+                got = ret_ref[pl.ds(d * 3 * cap + at, 3, stride=cap), :]
+                acc_ref[pl.ds(start, 3), :] = acc_ref[pl.ds(start, 3), :] + jnp.where(c < live, got, 0.0)
             return carry
 
-        return lax.fori_loop(0, jnp.clip(cnt_ref[d], 0, cap), one, carry)
+        return lax.fori_loop(0, (live + slot_step - 1) // slot_step, step, carry)
 
     lax.fori_loop(0, cnt_ref.shape[0], peer, 0)
     for c in range(3):

time: 106 us -> 97.2 us (0.917)
  the two profiles are of different devices: /device:TPU:96 before, /device:TPU:355 now
where the time goes in v8:
time: 97.2 us; the launch traced here: 96.6 us
  Pallas kernels  36 us (37%)
  starting transfers between devices  30.4 us (31%)
  waiting for transfers between devices  16.5 us (17%)
  local copies, waits for them, and re-layouts  7.44 us (8%)
  other arithmetic  5.5 us (6%)
    pallas_call x1, Pallas kernels, local(): pl.pallas_call(pair_kernel, out_shape=(jax.ShapeDtypeStruct((block_total,...  27.5 us
    all_to_all x1, starting transfers between devices, local(): lax.all_to_all(f2.reshape(peer_total, 3, slot_cap, 128), ('xa', 'xb'), sp...  17.7 us
    all_to_all x1, waiting for transfers between devices, local(): lax.all_to_all(lent.reshape(peer_total, 4, slot_cap, 128), ('xa', 'xb'),...  10.4 us
    all_to_all x1, starting transfers between devices, local(): lax.all_to_all(lent.reshape(peer_total, 4, slot_cap, 128), ('xa', 'xb'),...  7.36 us
    all_to_all x1, waiting for transfers between devices, local(): lax.all_to_all(f2.reshape(peer_total, 3, slot_cap, 128), ('xa', 'xb'), sp...  6.1 us
    pallas_call x1, Pallas kernels, local(): pl.pallas_call(functools.partial(back_kernel, slot_cap), out_shape=(jax.S...  4.81 us
    unnamed x20, local copies, waits for them, and re-layouts  4.41 us
    pallas_call x1, Pallas kernels, local(): pl.pallas_call(pack_kernel, out_shape=jax.ShapeDtypeStruct((peer_total *...  3.75 us
  transfers between devices with their start and end apart: 4, of which 2 were waited for; matrix products, arithmetic and copies ran while one was open for 4% of the time, Pallas kernels for 0%

profile of v8, /device:TPU:355, one launch (start us, length us, event | category | flops | bytes accessed | tf_op | source)
XLA Modules:
  0.0 96.6 jit_solution(16048437243733145163)
XLA Ops:
  0.7 0.8 slice_reduce_fusion
  1.5 0.0 copy-start.7
  1.5 0.7 reshape_squeeze.6.mine_ref
  2.2 0.0 copy-done.7
  2.2 0.0 copy-start.8
  2.2 0.1 copy.20
  2.3 0.5 copy-done.8
  2.9 0.7 reshape_squeeze.7.their_ref
  3.5 0.3 broadcast_select_fusion
  3.9 1.4 %fusion.1 = f32[256,3,128]{2,1,0:T(4,128)S(1)} fusion(f32[3,256,128]{2,1,0:T(8,128)} %disp_ref.1, f32[3,128]{1,0:T(4,128)S(1)} %stack.2, f32[3,256]{0,1:T(8,128)S(1)} %copy.20), kind=kLoop, calls=%fused_computation.5 | loop fusion | flops 196608 | bytes 791040 | tf_op jit(solution)/shard_map/transpose | solution.py:199
  5.2 1.0 %pad_maximum_fusion.rows_ref.m_ref = f32[256,4,128]{2,1,0:T(4,128)} fusion(f32[256,1,128]{2,1,0:T(1,128)S(1)} %broadcast_select_fusion, f32[256,3,128]{2,1,0:T(4,128)S(1)} %fusion.1), kind=kLoop, calls=%fused_computation.2 | loop fusion | flops 131072 | bytes 1048576 | tf_op jit(solution)/shard_map/concatenate | solution.py:203
  6.3 3.8 %shard_map.77 = f32[2048,128]{1,0:T(8,128)} custom-call(s32[512]{0:T(512)} %reshape_squeeze.6.mine_ref, s32[512]{0:T(512)} %reshape_squeeze.7.their_ref, s32[16]{0:T(128)} %bitcast.15, f32[256,4,128]{2,1,0:T(4,128)} %pad_maximum_fusion.rows_ref.m_ref), custom_call_target="tpu_custom_call" | custom-call | tf_op jit(solution)/shard_map/pallas_call | solution.py:209
  10.0 0.0 copy-start
  10.0 7.4 %all-to-all-start = ((f32[16,4,32,128]{3,2,1,0:T(8,128)}), f32[16,4,32,128]{3,2,1,0:T(8,128)S(1)}, u32[]{:S(2)}, u32[]{:S(2)}) async-start(f32[16,4,32,128]{3,2,1,0:T(8,128)} %bitcast.10), calls=%async_computation | async-start | bytes 2097152 | tf_op jit(solution)/shard_map/all_to_all | solution.py:215
  17.4 0.0 copy-done
  17.4 0.2 fusion.10
  17.6 3.4 %collective-permute-start = (f32[3,256,2]{2,1,0:T(8,128)S(1)}, f32[3,256,2]{2,1,0:T(8,128)S(1)}, u32[]{:S(2)}, u32[]{:S(2)}) collective-permute-start(f32[3,256,2]{2,1,0:T(8,128)S(1)} %get-tuple-element.9), channel_id=1, source_target_pairs={{0,16},{16,32},{32,48},{48,64},{64,80},{80,96},{96,112},{112,128},... | collective-permute-start | bytes 18440 | tf_op jit(solution)/shard_map/ppermute | solution.py:26
  21.0 1.9 %collective-permute-start.1 = (f32[3,256,2]{2,1,0:T(8,128)S(1)}, f32[3,256,2]{2,1,0:T(8,128)S(1)}, u32[]{:S(2)}, u32[]{:S(2)}) collective-permute-start(f32[3,256,2]{2,1,0:T(8,128)S(1)} %get-tuple-element.8), channel_id=1, source_target_pairs={{16,0},{32,16},{48,32},{64,48},{80,64},{96,80},{112,96},{128,112},... | collective-permute-start | bytes 18440 | tf_op jit(solution)/shard_map/ppermute | solution.py:29
  22.9 10.4 %all-to-all-done = f32[16,4,32,128]{3,2,1,0:T(8,128)S(1)} async-done(((f32[16,4,32,128]{3,2,1,0:T(8,128)}), f32[16,4,32,128]{3,2,1,0:T(8,128)S(1)}, u32[]{:S(2)}, u32[]{:S(2)}) %all-to-all-start) | async-done | bytes 1048608 | tf_op jit(solution)/shard_map/all_to_all | solution.py:215
  33.4 0.0 copy-start.1
  33.4 0.5 fusion.8
  33.8 0.9 fusion.9.cnt_ref
  34.8 0.7 convert_element_type.34.req_ref
  35.4 0.0 collective-permute-done.low_ref
  35.4 0.0 copy-start.5
  35.4 0.0 collective-permute-done.1.high_ref
  35.4 0.0 copy-start.3
  35.5 0.0 copy-done.1
  35.5 0.7 copy-done.5
  36.2 0.1 copy-done.3
  36.3 27.5 %shard_map.78 = (f32[256,8,128]{2,1,0:T(8,128)}, f32[1536,128]{1,0:T(8,128)}) custom-call(s32[16]{0:T(128)} %fusion.9.cnt_ref, s32[512]{0:T(512)} %convert_element_type.34.req_ref, f32[256,4,128]{2,1,0:T(4,128)} %pad_maximum_fusion.rows_ref.m_ref, f32[2048,128]{1,0:T(8,128)} %bitcast.9, f32[3,256,2]{2,1,0:T(8,128)} %copy-done.5, f32[3,256,2]{2,1,0:T(8,128)} %copy-done.3), custom_call_target="tpu_custom_call" | custom-call | tf_op jit(solution)/shard_map/pallas_call | solution.py:221
  63.8 17.7 %all-to-all-start.1 = ((f32[16,3,32,128]{3,2,1,0:T(8,128)}), f32[16,3,32,128]{3,2,1,0:T(8,128)S(1)}, u32[]{:S(2)}, u32[]{:S(2)}) async-start(f32[16,3,32,128]{3,2,1,0:T(8,128)} %bitcast.13), calls=%async_computation.1 | async-start | bytes 1572864 | tf_op jit(solution)/shard_map/all_to_all | solution.py:232
  81.5 0.0 copy-start.4
  81.5 1.0 copy-done.4
  82.5 0.0 copy-start.6
  82.5 1.0 copy-done.6
  83.5 1.3 %fusion.5.beam_ref = f32[3,256,128]{2,1,0:T(8,128)} fusion(f32[3,256,128]{2,1,0:T(8,128)S(1)} %copy-done, f32[3,256,2]{2,1,0:T(8,128)S(1)} %copy-done.6, f32[3,256,130]{2,1,0:T(8,128)S(1)} %constant_dynamic-update-slice_fusion), kind=kLoop, calls=%fused_computation.10 | loop fusion | flops 1376256 | bytes 1579008 | tf_op jit(solution)/shard_map/sub | solution.py:41
  84.8 6.1 %all-to-all-done.1 = f32[16,3,32,128]{3,2,1,0:T(8,128)S(1)} async-done(((f32[16,3,32,128]{3,2,1,0:T(8,128)}), f32[16,3,32,128]{3,2,1,0:T(8,128)S(1)}, u32[]{:S(2)}, u32[]{:S(2)}) %all-to-all-start.1) | async-done | bytes 786464 | tf_op jit(solution)/shard_map/all_to_all | solution.py:232
  90.9 0.0 copy-start.2
  90.9 0.9 copy-done.2
  91.8 4.8 %shard_map.79 = (f32[3,256,128]{2,1,0:T(8,128)}, f32[3,256,128]{2,1,0:T(8,128)}) custom-call(s32[512]{0:T(512)} %reshape_squeeze.6.mine_ref, s32[16]{0:T(128)} %bitcast.16, f32[2048,128]{1,0:T(8,128)} %bitcast.12, f32[1536,128]{1,0:T(8,128)} %bitcast.11, f32[3,256,128]{2,1,0:T(8,128)} %vel_ref.1, f32[3,256,128]{2,1,0:T(8,128)} %disp_ref.1, ...), custom_call_target="tpu_custom_call" | custom-call | tf_op jit(solution)/shard_map/pallas_call | solution.py:235
  (6 shorter events, 0.1 us)
Async XLA Ops:
  1.5 0.7 copy-start.7
  2.2 0.7 copy-start.8
  10.0 7.4 %copy-start = (f32[3,256,128]{2,1,0:T(8,128)S(1)}, f32[3,256,128]{2,1,0:T(8,128)}, u32[]{:S(2)}) copy-start(f32[3,256,128]{2,1,0:T(8,128)} %disp_ref.1) | copy-start | bytes 1179652
  10.0 23.3 %all-to-all-start = ((f32[16,4,32,128]{3,2,1,0:T(8,128)}), f32[16,4,32,128]{3,2,1,0:T(8,128)S(1)}, u32[]{:S(2)}, u32[]{:S(2)}) async-start(f32[16,4,32,128]{3,2,1,0:T(8,128)} %bitcast.10), calls=%async_computation | async-start | bytes 2097152 | tf_op jit(solution)/shard_map/all_to_all | solution.py:215
  17.6 17.8 %collective-permute-start = (f32[3,256,2]{2,1,0:T(8,128)S(1)}, f32[3,256,2]{2,1,0:T(8,128)S(1)}, u32[]{:S(2)}, u32[]{:S(2)}) collective-permute-start(f32[3,256,2]{2,1,0:T(8,128)S(1)} %get-tuple-element.9), channel_id=1, source_target_pairs={{0,16},{16,32},{32,48},{48,64},{64,80},{80,96},{96,112},{112,128},... | collective-permute-start | bytes 18440 | tf_op jit(solution)/shard_map/ppermute | solution.py:26
  21.0 14.4 %collective-permute-start.1 = (f32[3,256,2]{2,1,0:T(8,128)S(1)}, f32[3,256,2]{2,1,0:T(8,128)S(1)}, u32[]{:S(2)}, u32[]{:S(2)}) collective-permute-start(f32[3,256,2]{2,1,0:T(8,128)S(1)} %get-tuple-element.8), channel_id=1, source_target_pairs={{16,0},{32,16},{48,32},{64,48},{80,64},{96,80},{112,96},{128,112},... | collective-permute-start | bytes 18440 | tf_op jit(solution)/shard_map/ppermute | solution.py:29
  33.4 2.1 %copy-start.1 = (f32[16,4,32,128]{3,2,1,0:T(8,128)}, f32[16,4,32,128]{3,2,1,0:T(8,128)S(1)}, u32[]{:S(2)}) copy-start(f32[16,4,32,128]{3,2,1,0:T(8,128)S(1)} %all-to-all-done) | copy-start | bytes 3145732
  35.4 0.7 copy-start.5
  35.4 0.9 copy-start.3
  63.8 27.1 %all-to-all-start.1 = ((f32[16,3,32,128]{3,2,1,0:T(8,128)}), f32[16,3,32,128]{3,2,1,0:T(8,128)S(1)}, u32[]{:S(2)}, u32[]{:S(2)}) async-start(f32[16,3,32,128]{3,2,1,0:T(8,128)} %bitcast.13), calls=%async_computation.1 | async-start | bytes 1572864 | tf_op jit(solution)/shard_map/all_to_all | solution.py:232
  81.5 1.0 %copy-start.4 = (f32[3,256,2]{2,1,0:T(8,128)S(1)}, f32[3,256,2]{2,1,0:T(8,128)}, u32[]{:S(2)}) copy-start(f32[3,256,2]{2,1,0:T(8,128)} %copy-done.3) | copy-start | bytes 18436
  82.5 1.0 %copy-start.6 = (f32[3,256,2]{2,1,0:T(8,128)S(1)}, f32[3,256,2]{2,1,0:T(8,128)}, u32[]{:S(2)}) copy-start(f32[3,256,2]{2,1,0:T(8,128)} %copy-done.5) | copy-start | bytes 18436
  90.9 0.9 copy-start.2

commit v9 on v8

--- a/solution.py
+++ b/solution.py
@@ -87,12 +87,27 @@
     return (slot // cap) * rows * cap + slot % cap
 
 
-def pack_kernel(mine_ref, their_ref, cnt_ref, rows_ref, lent_ref):
+def pack_kernel(anc_ref, seg_ref, mine_ref, their_ref, cnt_ref, disp_ref, rows_ref, lent_ref):
     peers = cnt_ref.shape[0]
     cap = mine_ref.shape[0] // peers
     blocks = rows_ref.shape[0]
     row = lax.broadcasted_iota(jnp.int32, (4, 128), 0)
     lane = lax.broadcasted_iota(jnp.int32, (4, 128), 1)
+    height = lax.broadcasted_iota(jnp.int32, (1, 128), 1).astype(jnp.float32) * spacing
+
+    def block(g, carry):
+        for k in range(slot_step):
+            b = g * slot_step + k
+            x = jnp.where((row == 3) & (lane == 0), seg_ref[b].astype(jnp.float32), 0.0)
+            for c in range(3):
+                v = disp_ref[c, pl.ds(b, 1), :] + anc_ref[c * blocks + b]
+                if c == 2:
+                    v = v + height
+                x = jnp.where(row == c, jnp.broadcast_to(v, (4, 128)), x)
+            rows_ref[b] = x
+        return carry
+
+    lax.fori_loop(0, blocks // slot_step, block, 0)
 
     lent_ref[...] = jnp.zeros(lent_ref.shape, lent_ref.dtype)
 
@@ -124,12 +139,16 @@
     blocks = m_ref.shape[0]
 
     def listed(d, n):
-        def held(c, n):
-            lb_ref[n] = jnp.clip(req_ref[d * cap + c], 0, blocks - 1)
-            ls_ref[n] = d * cap + c
-            return n + 1
-
-        return lax.fori_loop(0, jnp.clip(cnt_ref[d], 0, cap), held, n)
+        live = jnp.clip(cnt_ref[d], 0, cap)
+
+        def held(g, n):
+            for k in range(slot_step):
+                c = jnp.minimum(g * slot_step + k, cap - 1)
+                lb_ref[n + k] = jnp.clip(req_ref[d * cap + c], 0, blocks - 1)
+                ls_ref[n + k] = d * cap + c
+            return n + jnp.minimum(slot_step, live - g * slot_step)
+
+        return lax.fori_loop(0, (live + slot_step - 1) // slot_step, held, n)
 
     total = lax.fori_loop(0, peers, listed, 0)
     last = jnp.maximum(total - 1, 0)
@@ -193,25 +212,20 @@
     halo_low, halo_high = halos(displacement, "len", 2, 2)
     beam = chain_force(jnp.concatenate([halo_low, displacement, halo_high], axis=2))
 
-    height = jnp.arange(seg_len, dtype=jnp.int32).astype(jnp.float32) * spacing
-    lift = jnp.stack([jnp.zeros_like(height), jnp.zeros_like(height), height])
-    positions = displacement + anchors[:, :, None] + lift[:, None, :]
-    blocks = positions.reshape(3, block_total, 128).transpose(1, 0, 2)
-    lanes = jnp.arange(128, dtype=jnp.int32)
-    seg_count = seg_live.reshape(block_total).astype(jnp.float32)
-    meta = jnp.where(lanes[None, :] == 0, seg_count[:, None], 0.0)
-    my_rows = jnp.concatenate([blocks, meta[:, None, :]], axis=1)
-
     mine_flat = pair_blocks[0, 0, :, :, 0].reshape(slot_total)
     their_flat = pair_blocks[0, 0, :, :, 1].reshape(slot_total)
     smem = pl.BlockSpec(memory_space=pltpu.SMEM)
     vmem = pl.BlockSpec(memory_space=pltpu.VMEM)
-    lent = pl.pallas_call(
+    my_rows, lent = pl.pallas_call(
         pack_kernel,
-        out_shape=jax.ShapeDtypeStruct((peer_total * 4 * slot_cap, 128), jnp.float32),
-        in_specs=[smem, smem, smem, vmem],
-        out_specs=vmem,
-    )(mine_flat, their_flat, pair_count[0, 0], my_rows)
+        out_shape=(
+            jax.ShapeDtypeStruct((block_total, 4, 128), jnp.float32),
+            jax.ShapeDtypeStruct((peer_total * 4 * slot_cap, 128), jnp.float32),
+        ),
+        in_specs=[smem, smem, smem, smem, smem, vmem],
+        out_specs=(vmem, vmem),
+    )(anchors.reshape(3 * block_total), seg_live.reshape(block_total), mine_flat, their_flat,
+      pair_count[0, 0], displacement)
     remote = lax.all_to_all(
         lent.reshape(peer_total, 4, slot_cap, 128), ("xa", "xb"), split_axis=0, concat_axis=0, tiled=True
     )
@@ -226,7 +240,7 @@
         ),
         in_specs=[smem, smem, vmem, vmem, vmem, vmem],
         out_specs=(vmem, vmem),
-        scratch_shapes=[pltpu.SMEM((slot_total,), jnp.int32), pltpu.SMEM((slot_total,), jnp.int32)],
+        scratch_shapes=[pltpu.SMEM((slot_total + slot_step,), jnp.int32)] * 2,
     )(live_from, req_ids, my_rows, remote.reshape(peer_total * 4 * slot_cap, 128), halo_low, halo_high)
 
     returned = lax.all_to_all(

time: 97.2 us -> 95.1 us (0.978)
  the two profiles are of different devices: /device:TPU:355 before, /device:TPU:288 now
where the time goes in v9:
time: 95.1 us; the launch traced here: 94.5 us
  Pallas kernels  42 us (44%)
  starting transfers between devices  22.6 us (24%)
  waiting for transfers between devices  19 us (20%)
  local copies, waits for them, and re-layouts  7.37 us (8%)
  other arithmetic  2.74 us (3%)
    pallas_call x1, Pallas kernels, local(): pl.pallas_call(pair_kernel, out_shape=(jax.ShapeDtypeStruct((block_total,...  32 us
    all_to_all x1, waiting for transfers between devices, local(): lax.all_to_all(lent.reshape(peer_total, 4, slot_cap, 128), ('xa', 'xb'),...  10.8 us
    all_to_all x1, starting transfers between devices, local(): lax.all_to_all(f2.reshape(peer_total, 3, slot_cap, 128), ('xa', 'xb'), sp...  9.93 us
    all_to_all x1, waiting for transfers between devices, local(): lax.all_to_all(f2.reshape(peer_total, 3, slot_cap, 128), ('xa', 'xb'), sp...  8.25 us
    all_to_all x1, starting transfers between devices, local(): lax.all_to_all(lent.reshape(peer_total, 4, slot_cap, 128), ('xa', 'xb'),...  7.13 us
    pallas_call x1, Pallas kernels, local(): pl.pallas_call(pack_kernel, out_shape=(jax.ShapeDtypeStruct((block_total,...  5.1 us
    pallas_call x1, Pallas kernels, local(): pl.pallas_call(functools.partial(back_kernel, slot_cap), out_shape=(jax.S...  4.92 us
    unnamed x17, local copies, waits for them, and re-layouts  3.74 us
  transfers between devices with their start and end apart: 4, of which 2 were waited for; matrix products, arithmetic and copies ran while one was open for 4% of the time, Pallas kernels for 0%

profile of v9, /device:TPU:288, one launch (start us, length us, event | category | flops | bytes accessed | tf_op | source)
XLA Modules:
  0.0 94.5 jit_solution(16643948946634872142)
XLA Ops:
  0.6 0.8 slice_reduce_fusion
  1.5 0.7 reshape_squeeze.6.mine_ref
  2.1 0.0 copy-start.7
  2.1 0.7 reshape_squeeze.7.their_ref
  2.8 0.0 copy-done.7
  2.8 0.6 reshape.29.anc_ref
  3.4 5.1 %shard_map.77 = (f32[256,4,128]{2,1,0:T(4,128)}, f32[2048,128]{1,0:T(8,128)}) custom-call(f32[768]{0:T(1024)} %reshape.29.anc_ref, s32[256]{0:T(256)} %bitcast.14, s32[512]{0:T(512)} %reshape_squeeze.6.mine_ref, s32[512]{0:T(512)} %reshape_squeeze.7.their_ref, s32[16]{0:T(128)} %bitcast.12, f32[3,256,128]{2,1,0:T(8,128)} %disp_ref.3), custom_call_target="tpu_custom_call" | custom-call | tf_op jit(solution)/shard_map/pallas_call | solution.py:219
  8.5 0.0 copy-start
  8.5 7.1 %all-to-all-start = ((f32[16,4,32,128]{3,2,1,0:T(8,128)}), f32[16,4,32,128]{3,2,1,0:T(8,128)S(1)}, u32[]{:S(2)}, u32[]{:S(2)}) async-start(f32[16,4,32,128]{3,2,1,0:T(8,128)} %bitcast.9), calls=%async_computation | async-start | bytes 2097152 | tf_op jit(solution)/shard_map/all_to_all | solution.py:229
  15.7 0.0 copy-done
  15.7 0.2 fusion.8
  15.8 1.9 %collective-permute-start = (f32[3,256,2]{2,1,0:T(8,128)S(1)}, f32[3,256,2]{2,1,0:T(8,128)S(1)}, u32[]{:S(2)}, u32[]{:S(2)}) collective-permute-start(f32[3,256,2]{2,1,0:T(8,128)S(1)} %get-tuple-element.13), channel_id=1, source_target_pairs={{0,16},{16,32},{32,48},{48,64},{64,80},{80,96},{96,112},{112,128},... | collective-permute-start | bytes 18440 | tf_op jit(solution)/shard_map/ppermute | solution.py:26
  17.8 3.6 %collective-permute-start.1 = (f32[3,256,2]{2,1,0:T(8,128)S(1)}, f32[3,256,2]{2,1,0:T(8,128)S(1)}, u32[]{:S(2)}, u32[]{:S(2)}) collective-permute-start(f32[3,256,2]{2,1,0:T(8,128)S(1)} %get-tuple-element.12), channel_id=1, source_target_pairs={{16,0},{32,16},{48,32},{64,48},{80,64},{96,80},{112,96},{128,112},... | collective-permute-start | bytes 18440 | tf_op jit(solution)/shard_map/ppermute | solution.py:29
  21.4 10.8 %all-to-all-done = f32[16,4,32,128]{3,2,1,0:T(8,128)S(1)} async-done(((f32[16,4,32,128]{3,2,1,0:T(8,128)}), f32[16,4,32,128]{3,2,1,0:T(8,128)S(1)}, u32[]{:S(2)}, u32[]{:S(2)}) %all-to-all-start) | async-done | bytes 1048608 | tf_op jit(solution)/shard_map/all_to_all | solution.py:229
  32.2 0.0 copy-start.1
  32.2 0.5 fusion.6
  32.7 0.9 fusion.7.cnt_ref
  33.6 0.7 convert_element_type.15.req_ref
  34.3 0.0 collective-permute-done.low_ref
  34.3 0.0 copy-start.5
  34.3 0.0 collective-permute-done.1.high_ref
  34.3 0.0 copy-start.3
  34.3 0.0 copy-done.1
  34.3 0.7 copy-done.5
  35.0 0.1 copy-done.3
  35.2 32.0 %shard_map.78 = (f32[256,8,128]{2,1,0:T(8,128)}, f32[1536,128]{1,0:T(8,128)}) custom-call(s32[16]{0:T(128)} %fusion.7.cnt_ref, s32[512]{0:T(512)} %convert_element_type.15.req_ref, f32[256,4,128]{2,1,0:T(4,128)} %get-tuple-element.7.m_ref, f32[2048,128]{1,0:T(8,128)} %bitcast.7, f32[3,256,2]{2,1,0:T(8,128)} %copy-done.5, f32[3,256,2]{2,1,0:T(8,128)} %copy-done.3), custom_call_target="tpu_custom_call" | custom-call | tf_op jit(solution)/shard_map/pallas_call | solution.py:235
  67.2 9.9 %all-to-all-start.1 = ((f32[16,3,32,128]{3,2,1,0:T(8,128)}), f32[16,3,32,128]{3,2,1,0:T(8,128)S(1)}, u32[]{:S(2)}, u32[]{:S(2)}) async-start(f32[16,3,32,128]{3,2,1,0:T(8,128)} %bitcast.11), calls=%async_computation.1 | async-start | bytes 1572864 | tf_op jit(solution)/shard_map/all_to_all | solution.py:246
  77.1 0.0 copy-start.4
  77.2 1.0 %copy-done.4 = f32[3,256,2]{2,1,0:T(8,128)S(1)} copy-done((f32[3,256,2]{2,1,0:T(8,128)S(1)}, f32[3,256,2]{2,1,0:T(8,128)}, u32[]{:S(2)}) %copy-start.4) | copy-done | bytes 6168
  78.1 0.0 copy-start.6
  78.1 1.0 %copy-done.6 = f32[3,256,2]{2,1,0:T(8,128)S(1)} copy-done((f32[3,256,2]{2,1,0:T(8,128)S(1)}, f32[3,256,2]{2,1,0:T(8,128)}, u32[]{:S(2)}) %copy-start.6) | copy-done | bytes 6168
  79.1 1.3 %fusion.3.beam_ref = f32[3,256,128]{2,1,0:T(8,128)} fusion(f32[3,256,128]{2,1,0:T(8,128)S(1)} %copy-done, f32[3,256,2]{2,1,0:T(8,128)S(1)} %copy-done.6, f32[3,256,130]{2,1,0:T(8,128)S(1)} %constant_dynamic-update-slice_fusion), kind=kLoop, calls=%fused_computation.6 | loop fusion | flops 1376256 | bytes 1579008 | tf_op jit(solution)/shard_map/sub | solution.py:41
  80.4 8.2 %all-to-all-done.1 = f32[16,3,32,128]{3,2,1,0:T(8,128)S(1)} async-done(((f32[16,3,32,128]{3,2,1,0:T(8,128)}), f32[16,3,32,128]{3,2,1,0:T(8,128)S(1)}, u32[]{:S(2)}, u32[]{:S(2)}) %all-to-all-start.1) | async-done | bytes 786464 | tf_op jit(solution)/shard_map/all_to_all | solution.py:246
  88.7 0.0 copy-start.2
  88.7 0.9 copy-done.2
  89.6 4.9 %shard_map.79 = (f32[3,256,128]{2,1,0:T(8,128)}, f32[3,256,128]{2,1,0:T(8,128)}) custom-call(s32[512]{0:T(512)} %reshape_squeeze.6.mine_ref, s32[16]{0:T(128)} %bitcast.13, f32[2048,128]{1,0:T(8,128)} %bitcast.10, f32[1536,128]{1,0:T(8,128)} %bitcast.8, f32[3,256,128]{2,1,0:T(8,128)} %vel_ref.1, f32[3,256,128]{2,1,0:T(8,128)} %disp_ref.3, ...), custom_call_target="tpu_custom_call" | custom-call | tf_op jit(solution)/shard_map/pallas_call | solution.py:249
  (2 shorter events, 0.1 us)
Async XLA Ops:
  2.1 0.7 copy-start.7
  8.5 7.1 %copy-start = (f32[3,256,128]{2,1,0:T(8,128)S(1)}, f32[3,256,128]{2,1,0:T(8,128)}, u32[]{:S(2)}) copy-start(f32[3,256,128]{2,1,0:T(8,128)} %disp_ref.3) | copy-start | bytes 1179652
  8.5 23.7 %all-to-all-start = ((f32[16,4,32,128]{3,2,1,0:T(8,128)}), f32[16,4,32,128]{3,2,1,0:T(8,128)S(1)}, u32[]{:S(2)}, u32[]{:S(2)}) async-start(f32[16,4,32,128]{3,2,1,0:T(8,128)} %bitcast.9), calls=%async_computation | async-start | bytes 2097152 | tf_op jit(solution)/shard_map/all_to_all | solution.py:229
  15.8 18.4 %collective-permute-start = (f32[3,256,2]{2,1,0:T(8,128)S(1)}, f32[3,256,2]{2,1,0:T(8,128)S(1)}, u32[]{:S(2)}, u32[]{:S(2)}) collective-permute-start(f32[3,256,2]{2,1,0:T(8,128)S(1)} %get-tuple-element.13), channel_id=1, source_target_pairs={{0,16},{16,32},{32,48},{48,64},{64,80},{80,96},{96,112},{112,128},... | collective-permute-start | bytes 18440 | tf_op jit(solution)/shard_map/ppermute | solution.py:26
  17.8 16.5 %collective-permute-start.1 = (f32[3,256,2]{2,1,0:T(8,128)S(1)}, f32[3,256,2]{2,1,0:T(8,128)S(1)}, u32[]{:S(2)}, u32[]{:S(2)}) collective-permute-start(f32[3,256,2]{2,1,0:T(8,128)S(1)} %get-tuple-element.12), channel_id=1, source_target_pairs={{16,0},{32,16},{48,32},{64,48},{80,64},{96,80},{112,96},{128,112},... | collective-permute-start | bytes 18440 | tf_op jit(solution)/shard_map/ppermute | solution.py:29
  32.2 2.1 %copy-start.1 = (f32[16,4,32,128]{3,2,1,0:T(8,128)}, f32[16,4,32,128]{3,2,1,0:T(8,128)S(1)}, u32[]{:S(2)}) copy-start(f32[16,4,32,128]{3,2,1,0:T(8,128)S(1)} %all-to-all-done) | copy-start | bytes 3145732
  34.3 0.7 copy-start.5
  34.3 0.9 copy-start.3
  67.2 21.5 %all-to-all-start.1 = ((f32[16,3,32,128]{3,2,1,0:T(8,128)}), f32[16,3,32,128]{3,2,1,0:T(8,128)S(1)}, u32[]{:S(2)}, u32[]{:S(2)}) async-start(f32[16,3,32,128]{3,2,1,0:T(8,128)} %bitcast.11), calls=%async_computation.1 | async-start | bytes 1572864 | tf_op jit(solution)/shard_map/all_to_all | solution.py:246
  77.1 1.0 %copy-start.4 = (f32[3,256,2]{2,1,0:T(8,128)S(1)}, f32[3,256,2]{2,1,0:T(8,128)}, u32[]{:S(2)}) copy-start(f32[3,256,2]{2,1,0:T(8,128)} %copy-done.3) | copy-start | bytes 18436
  78.1 1.0 %copy-start.6 = (f32[3,256,2]{2,1,0:T(8,128)S(1)}, f32[3,256,2]{2,1,0:T(8,128)}, u32[]{:S(2)}) copy-start(f32[3,256,2]{2,1,0:T(8,128)} %copy-done.5) | copy-start | bytes 18436
  88.7 0.9 copy-start.2

commit v10 on v9

--- a/solution.py
+++ b/solution.py
@@ -41,44 +41,82 @@
     return axial_stiff * axial - bend_stiff * bending
 
 
+def split3(v):
+    hi = v.astype(jnp.bfloat16).astype(jnp.float32)
+    rest = v - hi
+    mid = rest.astype(jnp.bfloat16).astype(jnp.float32)
+    lo = (rest - mid).astype(jnp.bfloat16).astype(jnp.float32)
+    return hi, mid, lo
+
+
+def stack_rows(rows):
+    row = lax.broadcasted_iota(jnp.int32, (8, 128), 0)
+    groups = []
+    for g in range(4):
+        acc = jnp.zeros((8, 128), jnp.float32)
+        for r, v in enumerate(rows[8 * g:8 * g + 8]):
+            acc = acc + jnp.where(row == r, jnp.broadcast_to(v, (8, 128)), 0.0)
+        groups.append(acc)
+    return jnp.concatenate(groups, axis=0)
+
+
 def rows_of(x, near):
+    lane = lax.broadcasted_iota(jnp.int32, (1, 128), 1).astype(jnp.float32)
+    v = [x[0:1], x[1:2], x[2:3]]
+    on = jnp.where(lane < x[3:4, 0:1], 1.0, 0.0)
+    norm = v[0] * v[0] + v[1] * v[1] + v[2] * v[2]
+    far = masked_far * (1.0 - on)
+    one = jnp.ones((1, 128), jnp.float32)
+    rows = []
+    if near:
+        for c in range(3):
+            hi, mid, lo = split3(v[c])
+            rows += [hi, mid, hi, mid, lo, hi]
+        rows += [one, one, one] + list(split3(norm)) + [one, far]
+        return stack_rows(rows), None
+    for c in range(3):
+        hi, mid, lo = split3(-2.0 * v[c])
+        rows += [hi, hi, mid, mid, hi, lo]
+    rows += list(split3(norm)) + [one, one, one] + [far, one]
     row = lax.broadcasted_iota(jnp.int32, (8, 128), 0)
-    lane = lax.broadcasted_iota(jnp.int32, (1, 128), 1).astype(jnp.float32)
-    v0, v1, v2 = x[0:1], x[1:2], x[2:3]
-    on = jnp.where(lane < x[3:4, 0:1], 1.0, 0.0)
-    norm = v0 * v0 + v1 * v1 + v2 * v2
-    far = masked_far * (1.0 - on)
-    pick = lambda r, v: jnp.where(row == r, jnp.broadcast_to(v, (8, 128)), 0.0)
-    if near:
-        return (pick(0, v0) + pick(1, v1) + pick(2, v2) + jnp.where((row == 3) | (row == 6), 1.0, 0.0)
-                + pick(4, norm) + pick(5, far))
-    rd = (pick(0, -2.0 * v0) + pick(1, -2.0 * v1) + pick(2, -2.0 * v2) + pick(3, norm)
-          + jnp.where((row == 4) | (row == 5), 1.0, 0.0) + pick(6, far))
-    rq = pick(0, v0) + pick(1, v1) + pick(2, v2) + jnp.where(row == 3, 1.0, 0.0)
-    return rd, rq
-
-
-def tile_two(m_a, m_b, rd_a, rd_b, rq_a, rq_b):
-    zero = jnp.zeros((8, 128), jnp.float32)
+    rq = (jnp.where(row == 0, jnp.broadcast_to(v[0], (8, 128)), 0.0)
+          + jnp.where(row == 1, jnp.broadcast_to(v[1], (8, 128)), 0.0)
+          + jnp.where(row == 2, jnp.broadcast_to(v[2], (8, 128)), 0.0) + jnp.where(row == 3, 1.0, 0.0))
+    return stack_rows(rows), rq
+
+
+def side_rows(x):
+    row = lax.broadcasted_iota(jnp.int32, (8, 128), 0)
+    return (jnp.where(row == 0, jnp.broadcast_to(x[0:1], (8, 128)), 0.0)
+            + jnp.where(row == 1, jnp.broadcast_to(x[1:2], (8, 128)), 0.0)
+            + jnp.where(row == 2, jnp.broadcast_to(x[2:3], (8, 128)), 0.0) + jnp.where(row == 3, 1.0, 0.0))
+
+
+def tile_two(m_a, m_b, s_a, s_b, rd_a, rd_b, rq_a, rq_b):
+    zero = jnp.zeros(m_a.shape, jnp.float32)
     mine = jnp.concatenate(
         [jnp.concatenate([m_a, zero], axis=1), jnp.concatenate([zero, m_b], axis=1)], axis=0
     )
     dist = lax.dot_general(
-        jnp.concatenate([rd_a, rd_b], axis=0), mine, (((0,), (0,)), ((), ())), precision=HIGH,
+        jnp.concatenate([rd_a, rd_b], axis=0), mine, (((0,), (0,)), ((), ())),
         preferred_element_type=jnp.float32,
     )
     w = jnp.exp(-dist)
+    zero = jnp.zeros((8, 128), jnp.float32)
+    side = jnp.concatenate(
+        [jnp.concatenate([s_a, zero], axis=1), jnp.concatenate([zero, s_b], axis=1)], axis=0
+    )
     f1 = lax.dot_general(
         jnp.concatenate([rq_a, rq_b], axis=0), w, (((1,), (0,)), ((), ())), precision=HIGH,
         preferred_element_type=jnp.float32,
     )
     f2 = lax.dot_general(
-        mine, w, (((1,), (1,)), ((), ())), precision=HIGH, preferred_element_type=jnp.float32
+        side, w, (((1,), (1,)), ((), ())), precision=HIGH, preferred_element_type=jnp.float32
     )
     f1 = f1 * contact_stiff
     f2 = f2 * contact_stiff
     out = []
-    for m, rq, g1, g2 in ((m_a, rq_a, f1[0:8, 0:128], f2[0:8]), (m_b, rq_b, f1[8:16, 128:256], f2[8:16])):
+    for m, rq, g1, g2 in ((s_a, rq_a, f1[0:8, 0:128], f2[0:8]), (s_b, rq_b, f1[8:16, 128:256], f2[8:16])):
         out.append((m * g1[3:4, :] - g1, (rq * g2[3:4, :] - g2)[0:3, :]))
     return out
 
@@ -163,7 +201,12 @@
             (t_a, b_a, s_a), (t_b, b_b, s_b) = picked
             rd_a, rq_a = rows_of(rem_ref[pl.ds(peer_row(s_a, 4, cap), 4, stride=cap), :], False)
             rd_b, rq_b = rows_of(rem_ref[pl.ds(peer_row(s_b, 4, cap), 4, stride=cap), :], False)
-            pair = tile_two(rows_of(m_ref[b_a], True), rows_of(m_ref[b_b], True), rd_a, rd_b, rq_a, rq_b)
+            x_a = m_ref[b_a]
+            x_b = m_ref[b_b]
+            pair = tile_two(
+                rows_of(x_a, True)[0], rows_of(x_b, True)[0], side_rows(x_a), side_rows(x_b),
+                rd_a, rd_b, rq_a, rq_b,
+            )
             for (t, b, slot), (on_first, on_second) in zip(picked, pair):
                 done.append((b, slot, jnp.where(t < total, on_first, 0.0), on_second))
         for b, slot, on_first, on_second in done:

time: 95.1 us -> 88.7 us (0.933)
  the two profiles are of different devices: /device:TPU:288 before, /device:TPU:34 now
where the time goes in v10:
time: 88.7 us; the launch traced here: 88.2 us
  Pallas kernels  41.4 us (47%)
  starting transfers between devices  19.5 us (22%)
  waiting for transfers between devices  16.5 us (19%)
  local copies, waits for them, and re-layouts  7.36 us (8%)
  other arithmetic  2.74 us (3%)
    pallas_call x1, Pallas kernels, local(): pl.pallas_call(pair_kernel, out_shape=(jax.ShapeDtypeStruct((block_total,...  30.9 us
    all_to_all x1, waiting for transfers between devices, local(): lax.all_to_all(lent.reshape(peer_total, 4, slot_cap, 128), ('xa', 'xb'),...  9.59 us
    all_to_all x1, starting transfers between devices, local(): lax.all_to_all(lent.reshape(peer_total, 4, slot_cap, 128), ('xa', 'xb'),...  7.73 us
    all_to_all x1, waiting for transfers between devices, local(): lax.all_to_all(f2.reshape(peer_total, 3, slot_cap, 128), ('xa', 'xb'), sp...  6.89 us
    all_to_all x1, starting transfers between devices, local(): lax.all_to_all(f2.reshape(peer_total, 3, slot_cap, 128), ('xa', 'xb'), sp...  6.18 us
    pallas_call x1, Pallas kernels, local(): pl.pallas_call(pack_kernel, out_shape=(jax.ShapeDtypeStruct((block_total,...  5.33 us
    pallas_call x1, Pallas kernels, local(): pl.pallas_call(functools.partial(back_kernel, slot_cap), out_shape=(jax.S...  5.19 us
    unnamed x17, local copies, waits for them, and re-layouts  3.74 us
  transfers between devices with their start and end apart: 4, of which 2 were waited for; matrix products, arithmetic and copies ran while one was open for 4% of the time, Pallas kernels for 0%

profile of v10, /device:TPU:34, one launch (start us, length us, event | category | flops | bytes accessed | tf_op | source)
XLA Modules:
  0.0 88.2 jit_solution(8380624466144972751)
XLA Ops:
  0.6 0.8 slice_reduce_fusion
  1.5 0.7 reshape_squeeze.6.mine_ref
  2.1 0.0 copy-start.7
  2.1 0.7 reshape_squeeze.7.their_ref
  2.8 0.0 copy-done.7
  2.8 0.6 reshape.29.anc_ref
  3.4 5.3 %shard_map.77 = (f32[256,4,128]{2,1,0:T(4,128)}, f32[2048,128]{1,0:T(8,128)}) custom-call(f32[768]{0:T(1024)} %reshape.29.anc_ref, s32[256]{0:T(256)} %bitcast.14, s32[512]{0:T(512)} %reshape_squeeze.6.mine_ref, s32[512]{0:T(512)} %reshape_squeeze.7.their_ref, s32[16]{0:T(128)} %bitcast.12, f32[3,256,128]{2,1,0:T(8,128)} %disp_ref.3), custom_call_target="tpu_custom_call" | custom-call | tf_op jit(solution)/shard_map/pallas_call | solution.py:262
  8.7 0.0 copy-start
  8.7 7.7 %all-to-all-start = ((f32[16,4,32,128]{3,2,1,0:T(8,128)}), f32[16,4,32,128]{3,2,1,0:T(8,128)S(1)}, u32[]{:S(2)}, u32[]{:S(2)}) async-start(f32[16,4,32,128]{3,2,1,0:T(8,128)} %bitcast.9), calls=%async_computation | async-start | bytes 2097152 | tf_op jit(solution)/shard_map/all_to_all | solution.py:272
  16.5 0.0 copy-done
  16.5 0.2 fusion.8
  16.7 1.9 %collective-permute-start = (f32[3,256,2]{2,1,0:T(8,128)S(1)}, f32[3,256,2]{2,1,0:T(8,128)S(1)}, u32[]{:S(2)}, u32[]{:S(2)}) collective-permute-start(f32[3,256,2]{2,1,0:T(8,128)S(1)} %get-tuple-element.13), channel_id=1, source_target_pairs={{0,16},{16,32},{32,48},{48,64},{64,80},{80,96},{96,112},{112,128},... | collective-permute-start | bytes 18440 | tf_op jit(solution)/shard_map/ppermute | solution.py:26
  18.6 3.6 %collective-permute-start.1 = (f32[3,256,2]{2,1,0:T(8,128)S(1)}, f32[3,256,2]{2,1,0:T(8,128)S(1)}, u32[]{:S(2)}, u32[]{:S(2)}) collective-permute-start(f32[3,256,2]{2,1,0:T(8,128)S(1)} %get-tuple-element.12), channel_id=1, source_target_pairs={{16,0},{32,16},{48,32},{64,48},{80,64},{96,80},{112,96},{128,112},... | collective-permute-start | bytes 18440 | tf_op jit(solution)/shard_map/ppermute | solution.py:29
  22.2 9.6 %all-to-all-done = f32[16,4,32,128]{3,2,1,0:T(8,128)S(1)} async-done(((f32[16,4,32,128]{3,2,1,0:T(8,128)}), f32[16,4,32,128]{3,2,1,0:T(8,128)S(1)}, u32[]{:S(2)}, u32[]{:S(2)}) %all-to-all-start) | async-done | bytes 1048608 | tf_op jit(solution)/shard_map/all_to_all | solution.py:272
  31.8 0.0 copy-start.1
  31.8 0.5 fusion.6
  32.3 0.9 %fusion.7.cnt_ref = s32[16]{0:T(128)} fusion(f32[16,4,32,128]{3,2,1,0:T(8,128)S(1)} %all-to-all-done), kind=kLoop, calls=%fused_computation.13 | loop fusion | flops 16 | bytes 128 | tf_op jit(solution)/shard_map/convert_element_type | solution.py:276
  33.2 0.7 convert_element_type.15.req_ref
  33.9 0.0 collective-permute-done.low_ref
  33.9 0.0 copy-start.5
  33.9 0.0 collective-permute-done.1.high_ref
  33.9 0.0 copy-start.3
  33.9 0.0 copy-done.1
  33.9 0.7 copy-done.5
  34.7 0.1 copy-done.3
  34.8 30.9 %shard_map.78 = (f32[256,8,128]{2,1,0:T(8,128)}, f32[1536,128]{1,0:T(8,128)}) custom-call(s32[16]{0:T(128)} %fusion.7.cnt_ref, s32[512]{0:T(512)} %convert_element_type.15.req_ref, f32[256,4,128]{2,1,0:T(4,128)} %get-tuple-element.7.m_ref, f32[2048,128]{1,0:T(8,128)} %bitcast.7, f32[3,256,2]{2,1,0:T(8,128)} %copy-done.5, f32[3,256,2]{2,1,0:T(8,128)} %copy-done.3), custom_call_target="tpu_custom_call" | custom-call | tf_op jit(solution)/shard_map/pallas_call | solution.py:278
  65.7 6.2 %all-to-all-start.1 = ((f32[16,3,32,128]{3,2,1,0:T(8,128)}), f32[16,3,32,128]{3,2,1,0:T(8,128)S(1)}, u32[]{:S(2)}, u32[]{:S(2)}) async-start(f32[16,3,32,128]{3,2,1,0:T(8,128)} %bitcast.11), calls=%async_computation.1 | async-start | bytes 1572864 | tf_op jit(solution)/shard_map/all_to_all | solution.py:289
  71.8 0.0 copy-start.4
  71.9 1.0 %copy-done.4 = f32[3,256,2]{2,1,0:T(8,128)S(1)} copy-done((f32[3,256,2]{2,1,0:T(8,128)S(1)}, f32[3,256,2]{2,1,0:T(8,128)}, u32[]{:S(2)}) %copy-start.4) | copy-done | bytes 6168
  72.8 0.0 copy-start.6
  72.9 1.0 %copy-done.6 = f32[3,256,2]{2,1,0:T(8,128)S(1)} copy-done((f32[3,256,2]{2,1,0:T(8,128)S(1)}, f32[3,256,2]{2,1,0:T(8,128)}, u32[]{:S(2)}) %copy-start.6) | copy-done | bytes 6168
  73.8 1.3 %fusion.3.beam_ref = f32[3,256,128]{2,1,0:T(8,128)} fusion(f32[3,256,128]{2,1,0:T(8,128)S(1)} %copy-done, f32[3,256,2]{2,1,0:T(8,128)S(1)} %copy-done.6, f32[3,256,130]{2,1,0:T(8,128)S(1)} %constant_dynamic-update-slice_fusion), kind=kLoop, calls=%fused_computation.6 | loop fusion | flops 1376256 | bytes 1579008 | tf_op jit(solution)/shard_map/sub | solution.py:41
  75.2 6.9 %all-to-all-done.1 = f32[16,3,32,128]{3,2,1,0:T(8,128)S(1)} async-done(((f32[16,3,32,128]{3,2,1,0:T(8,128)}), f32[16,3,32,128]{3,2,1,0:T(8,128)S(1)}, u32[]{:S(2)}, u32[]{:S(2)}) %all-to-all-start.1) | async-done | bytes 786464 | tf_op jit(solution)/shard_map/all_to_all | solution.py:289
  82.1 0.0 copy-start.2
  82.1 0.9 %copy-done.2 = f32[16,3,32,128]{3,2,1,0:T(8,128)} copy-done((f32[16,3,32,128]{3,2,1,0:T(8,128)}, f32[16,3,32,128]{3,2,1,0:T(8,128)S(1)}, u32[]{:S(2)}) %copy-start.2) | copy-done | bytes 786456
  83.0 5.2 %shard_map.79 = (f32[3,256,128]{2,1,0:T(8,128)}, f32[3,256,128]{2,1,0:T(8,128)}) custom-call(s32[512]{0:T(512)} %reshape_squeeze.6.mine_ref, s32[16]{0:T(128)} %bitcast.13, f32[2048,128]{1,0:T(8,128)} %bitcast.10, f32[1536,128]{1,0:T(8,128)} %bitcast.8, f32[3,256,128]{2,1,0:T(8,128)} %vel_ref.1, f32[3,256,128]{2,1,0:T(8,128)} %disp_ref.3, ...), custom_call_target="tpu_custom_call" | custom-call | tf_op jit(solution)/shard_map/pallas_call | solution.py:292
  (2 shorter events, 0.1 us)
Async XLA Ops:
  2.1 0.7 copy-start.7
  8.7 7.7 %copy-start = (f32[3,256,128]{2,1,0:T(8,128)S(1)}, f32[3,256,128]{2,1,0:T(8,128)}, u32[]{:S(2)}) copy-start(f32[3,256,128]{2,1,0:T(8,128)} %disp_ref.3) | copy-start | bytes 1179652
  8.7 23.1 %all-to-all-start = ((f32[16,4,32,128]{3,2,1,0:T(8,128)}), f32[16,4,32,128]{3,2,1,0:T(8,128)S(1)}, u32[]{:S(2)}, u32[]{:S(2)}) async-start(f32[16,4,32,128]{3,2,1,0:T(8,128)} %bitcast.9), calls=%async_computation | async-start | bytes 2097152 | tf_op jit(solution)/shard_map/all_to_all | solution.py:272
  16.7 17.3 %collective-permute-start = (f32[3,256,2]{2,1,0:T(8,128)S(1)}, f32[3,256,2]{2,1,0:T(8,128)S(1)}, u32[]{:S(2)}, u32[]{:S(2)}) collective-permute-start(f32[3,256,2]{2,1,0:T(8,128)S(1)} %get-tuple-element.13), channel_id=1, source_target_pairs={{0,16},{16,32},{32,48},{48,64},{64,80},{80,96},{96,112},{112,128},... | collective-permute-start | bytes 18440 | tf_op jit(solution)/shard_map/ppermute | solution.py:26
  18.6 15.3 %collective-permute-start.1 = (f32[3,256,2]{2,1,0:T(8,128)S(1)}, f32[3,256,2]{2,1,0:T(8,128)S(1)}, u32[]{:S(2)}, u32[]{:S(2)}) collective-permute-start(f32[3,256,2]{2,1,0:T(8,128)S(1)} %get-tuple-element.12), channel_id=1, source_target_pairs={{16,0},{32,16},{48,32},{64,48},{80,64},{96,80},{112,96},{128,112},... | collective-permute-start | bytes 18440 | tf_op jit(solution)/shard_map/ppermute | solution.py:29
  31.8 2.1 %copy-start.1 = (f32[16,4,32,128]{3,2,1,0:T(8,128)}, f32[16,4,32,128]{3,2,1,0:T(8,128)S(1)}, u32[]{:S(2)}) copy-start(f32[16,4,32,128]{3,2,1,0:T(8,128)S(1)} %all-to-all-done) | copy-start | bytes 3145732
  33.9 0.7 copy-start.5
  33.9 0.9 copy-start.3
  65.7 16.4 %all-to-all-start.1 = ((f32[16,3,32,128]{3,2,1,0:T(8,128)}), f32[16,3,32,128]{3,2,1,0:T(8,128)S(1)}, u32[]{:S(2)}, u32[]{:S(2)}) async-start(f32[16,3,32,128]{3,2,1,0:T(8,128)} %bitcast.11), calls=%async_computation.1 | async-start | bytes 1572864 | tf_op jit(solution)/shard_map/all_to_all | solution.py:289
  71.8 1.0 %copy-start.4 = (f32[3,256,2]{2,1,0:T(8,128)S(1)}, f32[3,256,2]{2,1,0:T(8,128)}, u32[]{:S(2)}) copy-start(f32[3,256,2]{2,1,0:T(8,128)} %copy-done.3) | copy-start | bytes 18436
  72.8 1.0 %copy-start.6 = (f32[3,256,2]{2,1,0:T(8,128)S(1)}, f32[3,256,2]{2,1,0:T(8,128)}, u32[]{:S(2)}) copy-start(f32[3,256,2]{2,1,0:T(8,128)} %copy-done.5) | copy-start | bytes 18436
  82.1 0.9 %copy-start.2 = (f32[16,3,32,128]{3,2,1,0:T(8,128)}, f32[16,3,32,128]{3,2,1,0:T(8,128)S(1)}, u32[]{:S(2)}) copy-start(f32[16,3,32,128]{3,2,1,0:T(8,128)S(1)} %all-to-all-done.1) | copy-start | bytes 2359300

commit v11 on v10

--- a/solution.py
+++ b/solution.py
@@ -92,6 +92,21 @@
             + jnp.where(row == 2, jnp.broadcast_to(x[2:3], (8, 128)), 0.0) + jnp.where(row == 3, 1.0, 0.0))
 
 
+def piece_sums(rows, w_hi, w_lo, axis):
+    hi, mid, lo = split3(rows)
+    count = rows.shape[0]
+    dims = (((1,), (axis,)), ((), ()))
+    by_hi = lax.dot_general(
+        jnp.concatenate([hi, mid, lo], axis=0), w_hi, dims, preferred_element_type=jnp.float32
+    )
+    by_lo = lax.dot_general(
+        jnp.concatenate([hi, mid], axis=0), w_lo, dims, preferred_element_type=jnp.float32
+    )
+    return (by_hi[0:count] + by_hi[count:2 * count] + by_hi[2 * count:]) + (
+        by_lo[0:count] + by_lo[count:]
+    )
+
+
 def tile_two(m_a, m_b, s_a, s_b, rd_a, rd_b, rq_a, rq_b):
     zero = jnp.zeros(m_a.shape, jnp.float32)
     mine = jnp.concatenate(
@@ -106,13 +121,10 @@
     side = jnp.concatenate(
         [jnp.concatenate([s_a, zero], axis=1), jnp.concatenate([zero, s_b], axis=1)], axis=0
     )
-    f1 = lax.dot_general(
-        jnp.concatenate([rq_a, rq_b], axis=0), w, (((1,), (0,)), ((), ())), precision=HIGH,
-        preferred_element_type=jnp.float32,
-    )
-    f2 = lax.dot_general(
-        side, w, (((1,), (1,)), ((), ())), precision=HIGH, preferred_element_type=jnp.float32
-    )
+    w_hi = w.astype(jnp.bfloat16).astype(jnp.float32)
+    w_lo = (w - w_hi).astype(jnp.bfloat16).astype(jnp.float32)
+    f1 = piece_sums(jnp.concatenate([rq_a, rq_b], axis=0), w_hi, w_lo, 0)
+    f2 = piece_sums(side, w_hi, w_lo, 1)
     f1 = f1 * contact_stiff
     f2 = f2 * contact_stiff
     out = []

time: 88.7 us -> 85.6 us (0.965)
  the two profiles are of different devices: /device:TPU:34 before, /device:TPU:224 now
where the time goes in v11:
time: 85.6 us; the launch traced here: 85.1 us
  Pallas kernels  28.6 us (33%)
  starting transfers between devices  22.9 us (27%)
  waiting for transfers between devices  22.8 us (27%)
  local copies, waits for them, and re-layouts  7.37 us (9%)
  other arithmetic  2.74 us (3%)
    pallas_call x1, Pallas kernels, local(): pl.pallas_call(pair_kernel, out_shape=(jax.ShapeDtypeStruct((block_total,...  17.6 us
    all_to_all x1, waiting for transfers between devices, local(): lax.all_to_all(lent.reshape(peer_total, 4, slot_cap, 128), ('xa', 'xb'),...  11.8 us
    all_to_all x1, waiting for transfers between devices, local(): lax.all_to_all(f2.reshape(peer_total, 3, slot_cap, 128), ('xa', 'xb'), sp...  10.9 us
    all_to_all x1, starting transfers between devices, local(): lax.all_to_all(f2.reshape(peer_total, 3, slot_cap, 128), ('xa', 'xb'), sp...  10.3 us
    all_to_all x1, starting transfers between devices, local(): lax.all_to_all(lent.reshape(peer_total, 4, slot_cap, 128), ('xa', 'xb'),...  6.95 us
    pallas_call x1, Pallas kernels, local(): pl.pallas_call(pack_kernel, out_shape=(jax.ShapeDtypeStruct((block_total,...  5.54 us
    pallas_call x1, Pallas kernels, local(): pl.pallas_call(functools.partial(back_kernel, slot_cap), out_shape=(jax.S...  5.44 us
    unnamed x17, local copies, waits for them, and re-layouts  3.74 us
  transfers between devices with their start and end apart: 4, of which 2 were waited for; matrix products, arithmetic and copies ran while one was open for 4% of the time, Pallas kernels for 0%

profile of v11, /device:TPU:224, one launch (start us, length us, event | category | flops | bytes accessed | tf_op | source)
XLA Modules:
  0.0 85.1 jit_solution(8543243593408479686)
XLA Ops:
  0.6 0.8 slice_reduce_fusion
  1.5 0.7 reshape_squeeze.6.mine_ref
  2.1 0.0 copy-start.7
  2.1 0.7 reshape_squeeze.7.their_ref
  2.8 0.0 copy-done.7
  2.8 0.6 reshape.29.anc_ref
  3.4 5.5 %shard_map.77 = (f32[256,4,128]{2,1,0:T(4,128)}, f32[2048,128]{1,0:T(8,128)}) custom-call(f32[768]{0:T(1024)} %reshape.29.anc_ref, s32[256]{0:T(256)} %bitcast.14, s32[512]{0:T(512)} %reshape_squeeze.6.mine_ref, s32[512]{0:T(512)} %reshape_squeeze.7.their_ref, s32[16]{0:T(128)} %bitcast.12, f32[3,256,128]{2,1,0:T(8,128)} %disp_ref.3), custom_call_target="tpu_custom_call" | custom-call | tf_op jit(solution)/shard_map/pallas_call | solution.py:274
  9.0 0.0 copy-start
  9.0 6.9 %all-to-all-start = ((f32[16,4,32,128]{3,2,1,0:T(8,128)}), f32[16,4,32,128]{3,2,1,0:T(8,128)S(1)}, u32[]{:S(2)}, u32[]{:S(2)}) async-start(f32[16,4,32,128]{3,2,1,0:T(8,128)} %bitcast.9), calls=%async_computation | async-start | bytes 2097152 | tf_op jit(solution)/shard_map/all_to_all | solution.py:284
  15.9 0.0 copy-done
  15.9 0.2 fusion.8
  16.1 1.9 %collective-permute-start = (f32[3,256,2]{2,1,0:T(8,128)S(1)}, f32[3,256,2]{2,1,0:T(8,128)S(1)}, u32[]{:S(2)}, u32[]{:S(2)}) collective-permute-start(f32[3,256,2]{2,1,0:T(8,128)S(1)} %get-tuple-element.13), channel_id=1, source_target_pairs={{0,16},{16,32},{32,48},{48,64},{64,80},{80,96},{96,112},{112,128},... | collective-permute-start | bytes 18440 | tf_op jit(solution)/shard_map/ppermute | solution.py:26
  18.0 3.6 %collective-permute-start.1 = (f32[3,256,2]{2,1,0:T(8,128)S(1)}, f32[3,256,2]{2,1,0:T(8,128)S(1)}, u32[]{:S(2)}, u32[]{:S(2)}) collective-permute-start(f32[3,256,2]{2,1,0:T(8,128)S(1)} %get-tuple-element.12), channel_id=1, source_target_pairs={{16,0},{32,16},{48,32},{64,48},{80,64},{96,80},{112,96},{128,112},... | collective-permute-start | bytes 18440 | tf_op jit(solution)/shard_map/ppermute | solution.py:29
  21.7 11.8 %all-to-all-done = f32[16,4,32,128]{3,2,1,0:T(8,128)S(1)} async-done(((f32[16,4,32,128]{3,2,1,0:T(8,128)}), f32[16,4,32,128]{3,2,1,0:T(8,128)S(1)}, u32[]{:S(2)}, u32[]{:S(2)}) %all-to-all-start) | async-done | bytes 1048608 | tf_op jit(solution)/shard_map/all_to_all | solution.py:284
  33.5 0.0 copy-start.1
  33.5 0.5 fusion.6
  34.0 0.9 %fusion.7.cnt_ref = s32[16]{0:T(128)} fusion(f32[16,4,32,128]{3,2,1,0:T(8,128)S(1)} %all-to-all-done), kind=kLoop, calls=%fused_computation.13 | loop fusion | flops 16 | bytes 128 | tf_op jit(solution)/shard_map/convert_element_type | solution.py:288
  34.9 0.7 convert_element_type.15.req_ref
  35.6 0.0 collective-permute-done.low_ref
  35.6 0.0 copy-start.5
  35.6 0.0 collective-permute-done.1.high_ref
  35.6 0.0 copy-start.3
  35.6 0.0 copy-done.1
  35.6 0.7 copy-done.5
  36.3 0.1 copy-done.3
  36.5 17.6 %shard_map.78 = (f32[256,8,128]{2,1,0:T(8,128)}, f32[1536,128]{1,0:T(8,128)}) custom-call(s32[16]{0:T(128)} %fusion.7.cnt_ref, s32[512]{0:T(512)} %convert_element_type.15.req_ref, f32[256,4,128]{2,1,0:T(4,128)} %get-tuple-element.7.m_ref, f32[2048,128]{1,0:T(8,128)} %bitcast.7, f32[3,256,2]{2,1,0:T(8,128)} %copy-done.5, f32[3,256,2]{2,1,0:T(8,128)} %copy-done.3), custom_call_target="tpu_custom_call" | custom-call | tf_op jit(solution)/shard_map/pallas_call | solution.py:290
  54.1 10.3 %all-to-all-start.1 = ((f32[16,3,32,128]{3,2,1,0:T(8,128)}), f32[16,3,32,128]{3,2,1,0:T(8,128)S(1)}, u32[]{:S(2)}, u32[]{:S(2)}) async-start(f32[16,3,32,128]{3,2,1,0:T(8,128)} %bitcast.11), calls=%async_computation.1 | async-start | bytes 1572864 | tf_op jit(solution)/shard_map/all_to_all | solution.py:301
  64.5 0.0 copy-start.4
  64.5 1.0 %copy-done.4 = f32[3,256,2]{2,1,0:T(8,128)S(1)} copy-done((f32[3,256,2]{2,1,0:T(8,128)S(1)}, f32[3,256,2]{2,1,0:T(8,128)}, u32[]{:S(2)}) %copy-start.4) | copy-done | bytes 6168
  65.5 0.0 copy-start.6
  65.5 1.0 %copy-done.6 = f32[3,256,2]{2,1,0:T(8,128)S(1)} copy-done((f32[3,256,2]{2,1,0:T(8,128)S(1)}, f32[3,256,2]{2,1,0:T(8,128)}, u32[]{:S(2)}) %copy-start.6) | copy-done | bytes 6168
  66.5 1.3 %fusion.3.beam_ref = f32[3,256,128]{2,1,0:T(8,128)} fusion(f32[3,256,128]{2,1,0:T(8,128)S(1)} %copy-done, f32[3,256,2]{2,1,0:T(8,128)S(1)} %copy-done.6, f32[3,256,130]{2,1,0:T(8,128)S(1)} %constant_dynamic-update-slice_fusion), kind=kLoop, calls=%fused_computation.6 | loop fusion | flops 1376256 | bytes 1579008 | tf_op jit(solution)/shard_map/sub | solution.py:41
  67.8 10.9 %all-to-all-done.1 = f32[16,3,32,128]{3,2,1,0:T(8,128)S(1)} async-done(((f32[16,3,32,128]{3,2,1,0:T(8,128)}), f32[16,3,32,128]{3,2,1,0:T(8,128)S(1)}, u32[]{:S(2)}, u32[]{:S(2)}) %all-to-all-start.1) | async-done | bytes 786464 | tf_op jit(solution)/shard_map/all_to_all | solution.py:301
  78.7 0.0 copy-start.2
  78.7 0.9 %copy-done.2 = f32[16,3,32,128]{3,2,1,0:T(8,128)} copy-done((f32[16,3,32,128]{3,2,1,0:T(8,128)}, f32[16,3,32,128]{3,2,1,0:T(8,128)S(1)}, u32[]{:S(2)}) %copy-start.2) | copy-done | bytes 786456
  79.6 5.4 %shard_map.79 = (f32[3,256,128]{2,1,0:T(8,128)}, f32[3,256,128]{2,1,0:T(8,128)}) custom-call(s32[512]{0:T(512)} %reshape_squeeze.6.mine_ref, s32[16]{0:T(128)} %bitcast.13, f32[2048,128]{1,0:T(8,128)} %bitcast.10, f32[1536,128]{1,0:T(8,128)} %bitcast.8, f32[3,256,128]{2,1,0:T(8,128)} %vel_ref.1, f32[3,256,128]{2,1,0:T(8,128)} %disp_ref.3, ...), custom_call_target="tpu_custom_call" | custom-call | tf_op jit(solution)/shard_map/pallas_call | solution.py:304
  (2 shorter events, 0.1 us)
Async XLA Ops:
  2.1 0.7 copy-start.7
  9.0 7.0 %copy-start = (f32[3,256,128]{2,1,0:T(8,128)S(1)}, f32[3,256,128]{2,1,0:T(8,128)}, u32[]{:S(2)}) copy-start(f32[3,256,128]{2,1,0:T(8,128)} %disp_ref.3) | copy-start | bytes 1179652
  9.0 24.6 %all-to-all-start = ((f32[16,4,32,128]{3,2,1,0:T(8,128)}), f32[16,4,32,128]{3,2,1,0:T(8,128)S(1)}, u32[]{:S(2)}, u32[]{:S(2)}) async-start(f32[16,4,32,128]{3,2,1,0:T(8,128)} %bitcast.9), calls=%async_computation | async-start | bytes 2097152 | tf_op jit(solution)/shard_map/all_to_all | solution.py:284
  16.1 19.5 %collective-permute-start = (f32[3,256,2]{2,1,0:T(8,128)S(1)}, f32[3,256,2]{2,1,0:T(8,128)S(1)}, u32[]{:S(2)}, u32[]{:S(2)}) collective-permute-start(f32[3,256,2]{2,1,0:T(8,128)S(1)} %get-tuple-element.13), channel_id=1, source_target_pairs={{0,16},{16,32},{32,48},{48,64},{64,80},{80,96},{96,112},{112,128},... | collective-permute-start | bytes 18440 | tf_op jit(solution)/shard_map/ppermute | solution.py:26
  18.0 17.6 %collective-permute-start.1 = (f32[3,256,2]{2,1,0:T(8,128)S(1)}, f32[3,256,2]{2,1,0:T(8,128)S(1)}, u32[]{:S(2)}, u32[]{:S(2)}) collective-permute-start(f32[3,256,2]{2,1,0:T(8,128)S(1)} %get-tuple-element.12), channel_id=1, source_target_pairs={{16,0},{32,16},{48,32},{64,48},{80,64},{96,80},{112,96},{128,112},... | collective-permute-start | bytes 18440 | tf_op jit(solution)/shard_map/ppermute | solution.py:29
  33.5 2.1 %copy-start.1 = (f32[16,4,32,128]{3,2,1,0:T(8,128)}, f32[16,4,32,128]{3,2,1,0:T(8,128)S(1)}, u32[]{:S(2)}) copy-start(f32[16,4,32,128]{3,2,1,0:T(8,128)S(1)} %all-to-all-done) | copy-start | bytes 3145732
  35.6 0.7 copy-start.5
  35.6 0.9 %copy-start.3 = (f32[3,256,2]{2,1,0:T(8,128)}, f32[3,256,2]{2,1,0:T(8,128)S(1)}, u32[]{:S(2)}) copy-start(f32[3,256,2]{2,1,0:T(8,128)S(1)} %collective-permute-done.1.high_ref) | copy-start | bytes 18436
  54.1 24.6 %all-to-all-start.1 = ((f32[16,3,32,128]{3,2,1,0:T(8,128)}), f32[16,3,32,128]{3,2,1,0:T(8,128)S(1)}, u32[]{:S(2)}, u32[]{:S(2)}) async-start(f32[16,3,32,128]{3,2,1,0:T(8,128)} %bitcast.11), calls=%async_computation.1 | async-start | bytes 1572864 | tf_op jit(solution)/shard_map/all_to_all | solution.py:301
  64.5 1.0 %copy-start.4 = (f32[3,256,2]{2,1,0:T(8,128)S(1)}, f32[3,256,2]{2,1,0:T(8,128)}, u32[]{:S(2)}) copy-start(f32[3,256,2]{2,1,0:T(8,128)} %copy-done.3) | copy-start | bytes 18436
  65.5 1.0 %copy-start.6 = (f32[3,256,2]{2,1,0:T(8,128)S(1)}, f32[3,256,2]{2,1,0:T(8,128)}, u32[]{:S(2)}) copy-start(f32[3,256,2]{2,1,0:T(8,128)} %copy-done.5) | copy-start | bytes 18436
  78.7 0.9 %copy-start.2 = (f32[16,3,32,128]{3,2,1,0:T(8,128)}, f32[16,3,32,128]{3,2,1,0:T(8,128)S(1)}, u32[]{:S(2)}) copy-start(f32[16,3,32,128]{3,2,1,0:T(8,128)S(1)} %all-to-all-done.1) | copy-start | bytes 2359300

commit v12 on v11

--- a/solution.py
+++ b/solution.py
@@ -15,7 +15,7 @@
 damping = 0.9
 masked_far = 1.0e4
 HIGH = lax.Precision.HIGH
-tile_group = 16
+tile_group = 32
 slot_step = 4
 
 

time: 85.6 us -> 84.7 us (0.989)
  the two profiles are of different devices: /device:TPU:224 before, /device:TPU:321 now
where the time goes in v12:
time: 84.7 us; the launch traced here: 84.1 us
  Pallas kernels  26.6 us (31%)
  starting transfers between devices  25 us (30%)
  waiting for transfers between devices  21.7 us (26%)
  local copies, waits for them, and re-layouts  7.37 us (9%)
  other arithmetic  2.74 us (3%)
    pallas_call x1, Pallas kernels, local(): pl.pallas_call(pair_kernel, out_shape=(jax.ShapeDtypeStruct((block_total,...  18.5 us
    all_to_all x1, waiting for transfers between devices, local(): lax.all_to_all(lent.reshape(peer_total, 4, slot_cap, 128), ('xa', 'xb'),...  14.6 us
    all_to_all x1, starting transfers between devices, local(): lax.all_to_all(f2.reshape(peer_total, 3, slot_cap, 128), ('xa', 'xb'), sp...  11.6 us
    all_to_all x1, starting transfers between devices, local(): lax.all_to_all(lent.reshape(peer_total, 4, slot_cap, 128), ('xa', 'xb'),...  8.28 us
    all_to_all x1, waiting for transfers between devices, local(): lax.all_to_all(f2.reshape(peer_total, 3, slot_cap, 128), ('xa', 'xb'), sp...  7.1 us
    pallas_call x1, Pallas kernels, local(): pl.pallas_call(pack_kernel, out_shape=(jax.ShapeDtypeStruct((block_total,...  4.2 us
    pallas_call x1, Pallas kernels, local(): pl.pallas_call(functools.partial(back_kernel, slot_cap), out_shape=(jax.S...  3.85 us
    unnamed x17, local copies, waits for them, and re-layouts  3.74 us
  transfers between devices with their start and end apart: 4, of which 2 were waited for; matrix products, arithmetic and copies ran while one was open for 4% of the time, Pallas kernels for 0%

profile of v12, /device:TPU:321, one launch (start us, length us, event | category | flops | bytes accessed | tf_op | source)
XLA Modules:
  0.0 84.1 jit_solution(3518281325998999507)
XLA Ops:
  0.6 0.8 slice_reduce_fusion
  1.5 0.7 reshape_squeeze.6.mine_ref
  2.1 0.0 copy-start.7
  2.1 0.7 reshape_squeeze.7.their_ref
  2.8 0.0 copy-done.7
  2.8 0.6 reshape.29.anc_ref
  3.4 4.2 %shard_map.77 = (f32[256,4,128]{2,1,0:T(4,128)}, f32[2048,128]{1,0:T(8,128)}) custom-call(f32[768]{0:T(1024)} %reshape.29.anc_ref, s32[256]{0:T(256)} %bitcast.14, s32[512]{0:T(512)} %reshape_squeeze.6.mine_ref, s32[512]{0:T(512)} %reshape_squeeze.7.their_ref, s32[16]{0:T(128)} %bitcast.12, f32[3,256,128]{2,1,0:T(8,128)} %disp_ref.3), custom_call_target="tpu_custom_call" | custom-call | tf_op jit(solution)/shard_map/pallas_call | solution.py:274
  7.6 0.0 copy-start
  7.6 8.3 %all-to-all-start = ((f32[16,4,32,128]{3,2,1,0:T(8,128)}), f32[16,4,32,128]{3,2,1,0:T(8,128)S(1)}, u32[]{:S(2)}, u32[]{:S(2)}) async-start(f32[16,4,32,128]{3,2,1,0:T(8,128)} %bitcast.9), calls=%async_computation | async-start | bytes 2097152 | tf_op jit(solution)/shard_map/all_to_all | solution.py:284
  15.9 0.0 copy-done
  15.9 0.2 fusion.8
  16.1 3.2 %collective-permute-start = (f32[3,256,2]{2,1,0:T(8,128)S(1)}, f32[3,256,2]{2,1,0:T(8,128)S(1)}, u32[]{:S(2)}, u32[]{:S(2)}) collective-permute-start(f32[3,256,2]{2,1,0:T(8,128)S(1)} %get-tuple-element.13), channel_id=1, source_target_pairs={{0,16},{16,32},{32,48},{48,64},{64,80},{80,96},{96,112},{112,128},... | collective-permute-start | bytes 18440 | tf_op jit(solution)/shard_map/ppermute | solution.py:26
  19.3 1.9 %collective-permute-start.1 = (f32[3,256,2]{2,1,0:T(8,128)S(1)}, f32[3,256,2]{2,1,0:T(8,128)S(1)}, u32[]{:S(2)}, u32[]{:S(2)}) collective-permute-start(f32[3,256,2]{2,1,0:T(8,128)S(1)} %get-tuple-element.12), channel_id=1, source_target_pairs={{16,0},{32,16},{48,32},{64,48},{80,64},{96,80},{112,96},{128,112},... | collective-permute-start | bytes 18440 | tf_op jit(solution)/shard_map/ppermute | solution.py:29
  21.2 14.6 %all-to-all-done = f32[16,4,32,128]{3,2,1,0:T(8,128)S(1)} async-done(((f32[16,4,32,128]{3,2,1,0:T(8,128)}), f32[16,4,32,128]{3,2,1,0:T(8,128)S(1)}, u32[]{:S(2)}, u32[]{:S(2)}) %all-to-all-start) | async-done | bytes 1048608 | tf_op jit(solution)/shard_map/all_to_all | solution.py:284
  35.8 0.0 copy-start.1
  35.8 0.5 fusion.6
  36.3 0.9 %fusion.7.cnt_ref = s32[16]{0:T(128)} fusion(f32[16,4,32,128]{3,2,1,0:T(8,128)S(1)} %all-to-all-done), kind=kLoop, calls=%fused_computation.13 | loop fusion | flops 16 | bytes 128 | tf_op jit(solution)/shard_map/convert_element_type | solution.py:288
  37.2 0.7 convert_element_type.15.req_ref
  37.9 0.0 collective-permute-done.low_ref
  37.9 0.0 copy-start.5
  37.9 0.0 collective-permute-done.1.high_ref
  37.9 0.0 copy-start.3
  37.9 0.0 copy-done.1
  37.9 0.7 copy-done.5
  38.6 0.1 copy-done.3
  38.8 18.5 %shard_map.78 = (f32[256,8,128]{2,1,0:T(8,128)}, f32[1536,128]{1,0:T(8,128)}) custom-call(s32[16]{0:T(128)} %fusion.7.cnt_ref, s32[512]{0:T(512)} %convert_element_type.15.req_ref, f32[256,4,128]{2,1,0:T(4,128)} %get-tuple-element.7.m_ref, f32[2048,128]{1,0:T(8,128)} %bitcast.7, f32[3,256,2]{2,1,0:T(8,128)} %copy-done.5, f32[3,256,2]{2,1,0:T(8,128)} %copy-done.3), custom_call_target="tpu_custom_call" | custom-call | tf_op jit(solution)/shard_map/pallas_call | solution.py:290
  57.3 11.6 %all-to-all-start.1 = ((f32[16,3,32,128]{3,2,1,0:T(8,128)}), f32[16,3,32,128]{3,2,1,0:T(8,128)S(1)}, u32[]{:S(2)}, u32[]{:S(2)}) async-start(f32[16,3,32,128]{3,2,1,0:T(8,128)} %bitcast.11), calls=%async_computation.1 | async-start | bytes 1572864 | tf_op jit(solution)/shard_map/all_to_all | solution.py:301
  68.9 0.0 copy-start.4
  69.0 1.0 %copy-done.4 = f32[3,256,2]{2,1,0:T(8,128)S(1)} copy-done((f32[3,256,2]{2,1,0:T(8,128)S(1)}, f32[3,256,2]{2,1,0:T(8,128)}, u32[]{:S(2)}) %copy-start.4) | copy-done | bytes 6168
  69.9 0.0 copy-start.6
  70.0 1.0 %copy-done.6 = f32[3,256,2]{2,1,0:T(8,128)S(1)} copy-done((f32[3,256,2]{2,1,0:T(8,128)S(1)}, f32[3,256,2]{2,1,0:T(8,128)}, u32[]{:S(2)}) %copy-start.6) | copy-done | bytes 6168
  70.9 1.3 %fusion.3.beam_ref = f32[3,256,128]{2,1,0:T(8,128)} fusion(f32[3,256,128]{2,1,0:T(8,128)S(1)} %copy-done, f32[3,256,2]{2,1,0:T(8,128)S(1)} %copy-done.6, f32[3,256,130]{2,1,0:T(8,128)S(1)} %constant_dynamic-update-slice_fusion), kind=kLoop, calls=%fused_computation.6 | loop fusion | flops 1376256 | bytes 1579008 | tf_op jit(solution)/shard_map/sub | solution.py:41
  72.3 7.1 %all-to-all-done.1 = f32[16,3,32,128]{3,2,1,0:T(8,128)S(1)} async-done(((f32[16,3,32,128]{3,2,1,0:T(8,128)}), f32[16,3,32,128]{3,2,1,0:T(8,128)S(1)}, u32[]{:S(2)}, u32[]{:S(2)}) %all-to-all-start.1) | async-done | bytes 786464 | tf_op jit(solution)/shard_map/all_to_all | solution.py:301
  79.4 0.0 copy-start.2
  79.4 0.9 %copy-done.2 = f32[16,3,32,128]{3,2,1,0:T(8,128)} copy-done((f32[16,3,32,128]{3,2,1,0:T(8,128)}, f32[16,3,32,128]{3,2,1,0:T(8,128)S(1)}, u32[]{:S(2)}) %copy-start.2) | copy-done | bytes 786456
  80.3 3.9 %shard_map.79 = (f32[3,256,128]{2,1,0:T(8,128)}, f32[3,256,128]{2,1,0:T(8,128)}) custom-call(s32[512]{0:T(512)} %reshape_squeeze.6.mine_ref, s32[16]{0:T(128)} %bitcast.13, f32[2048,128]{1,0:T(8,128)} %bitcast.10, f32[1536,128]{1,0:T(8,128)} %bitcast.8, f32[3,256,128]{2,1,0:T(8,128)} %vel_ref.1, f32[3,256,128]{2,1,0:T(8,128)} %disp_ref.3, ...), custom_call_target="tpu_custom_call" | custom-call | tf_op jit(solution)/shard_map/pallas_call | solution.py:304
  (2 shorter events, 0.1 us)
Async XLA Ops:
  2.1 0.7 copy-start.7
  7.6 8.3 %copy-start = (f32[3,256,128]{2,1,0:T(8,128)S(1)}, f32[3,256,128]{2,1,0:T(8,128)}, u32[]{:S(2)}) copy-start(f32[3,256,128]{2,1,0:T(8,128)} %disp_ref.3) | copy-start | bytes 1179652
  7.6 28.2 %all-to-all-start = ((f32[16,4,32,128]{3,2,1,0:T(8,128)}), f32[16,4,32,128]{3,2,1,0:T(8,128)S(1)}, u32[]{:S(2)}, u32[]{:S(2)}) async-start(f32[16,4,32,128]{3,2,1,0:T(8,128)} %bitcast.9), calls=%async_computation | async-start | bytes 2097152 | tf_op jit(solution)/shard_map/all_to_all | solution.py:284
  16.1 21.8 %collective-permute-start = (f32[3,256,2]{2,1,0:T(8,128)S(1)}, f32[3,256,2]{2,1,0:T(8,128)S(1)}, u32[]{:S(2)}, u32[]{:S(2)}) collective-permute-start(f32[3,256,2]{2,1,0:T(8,128)S(1)} %get-tuple-element.13), channel_id=1, source_target_pairs={{0,16},{16,32},{32,48},{48,64},{64,80},{80,96},{96,112},{112,128},... | collective-permute-start | bytes 18440 | tf_op jit(solution)/shard_map/ppermute | solution.py:26
  19.3 18.6 %collective-permute-start.1 = (f32[3,256,2]{2,1,0:T(8,128)S(1)}, f32[3,256,2]{2,1,0:T(8,128)S(1)}, u32[]{:S(2)}, u32[]{:S(2)}) collective-permute-start(f32[3,256,2]{2,1,0:T(8,128)S(1)} %get-tuple-element.12), channel_id=1, source_target_pairs={{16,0},{32,16},{48,32},{64,48},{80,64},{96,80},{112,96},{128,112},... | collective-permute-start | bytes 18440 | tf_op jit(solution)/shard_map/ppermute | solution.py:29
  35.8 2.1 %copy-start.1 = (f32[16,4,32,128]{3,2,1,0:T(8,128)}, f32[16,4,32,128]{3,2,1,0:T(8,128)S(1)}, u32[]{:S(2)}) copy-start(f32[16,4,32,128]{3,2,1,0:T(8,128)S(1)} %all-to-all-done) | copy-start | bytes 3145732
  37.9 0.7 copy-start.5
  37.9 0.9 %copy-start.3 = (f32[3,256,2]{2,1,0:T(8,128)}, f32[3,256,2]{2,1,0:T(8,128)S(1)}, u32[]{:S(2)}) copy-start(f32[3,256,2]{2,1,0:T(8,128)S(1)} %collective-permute-done.1.high_ref) | copy-start | bytes 18436
  57.3 22.1 %all-to-all-start.1 = ((f32[16,3,32,128]{3,2,1,0:T(8,128)}), f32[16,3,32,128]{3,2,1,0:T(8,128)S(1)}, u32[]{:S(2)}, u32[]{:S(2)}) async-start(f32[16,3,32,128]{3,2,1,0:T(8,128)} %bitcast.11), calls=%async_computation.1 | async-start | bytes 1572864 | tf_op jit(solution)/shard_map/all_to_all | solution.py:301
  68.9 1.0 %copy-start.4 = (f32[3,256,2]{2,1,0:T(8,128)S(1)}, f32[3,256,2]{2,1,0:T(8,128)}, u32[]{:S(2)}) copy-start(f32[3,256,2]{2,1,0:T(8,128)} %copy-done.3) | copy-start | bytes 18436
  69.9 1.0 %copy-start.6 = (f32[3,256,2]{2,1,0:T(8,128)S(1)}, f32[3,256,2]{2,1,0:T(8,128)}, u32[]{:S(2)}) copy-start(f32[3,256,2]{2,1,0:T(8,128)} %copy-done.5) | copy-start | bytes 18436
  79.4 0.9 %copy-start.2 = (f32[16,3,32,128]{3,2,1,0:T(8,128)}, f32[16,3,32,128]{3,2,1,0:T(8,128)S(1)}, u32[]{:S(2)}) copy-start(f32[16,3,32,128]{3,2,1,0:T(8,128)S(1)} %all-to-all-done.1) | copy-start | bytes 2359300

commit v13 on v12

--- a/solution.py
+++ b/solution.py
@@ -16,7 +16,7 @@
 masked_far = 1.0e4
 HIGH = lax.Precision.HIGH
 tile_group = 32
-slot_step = 4
+slot_step = 8
 
 
 def halos(block, axis, dim, width):

time: 84.7 us -> 81 us (0.956)
  the two profiles are of different devices: /device:TPU:321 before, /device:TPU:64 now
where the time goes in v13:
time: 81 us; the launch traced here: 79.5 us
  Pallas kernels  26.7 us (33%)
  waiting for transfers between devices  22.9 us (28%)
  starting transfers between devices  19.1 us (24%)
  local copies, waits for them, and re-layouts  7.37 us (9%)
  other arithmetic  2.74 us (3%)
    pallas_call x1, Pallas kernels, local(): pl.pallas_call(pair_kernel, out_shape=(jax.ShapeDtypeStruct((block_total,...  18.6 us
    all_to_all x1, waiting for transfers between devices, local(): lax.all_to_all(lent.reshape(peer_total, 4, slot_cap, 128), ('xa', 'xb'),...  11.8 us
    all_to_all x1, waiting for transfers between devices, local(): lax.all_to_all(f2.reshape(peer_total, 3, slot_cap, 128), ('xa', 'xb'), sp...  11 us
    all_to_all x1, starting transfers between devices, local(): lax.all_to_all(lent.reshape(peer_total, 4, slot_cap, 128), ('xa', 'xb'),...  8.04 us
    all_to_all x1, starting transfers between devices, local(): lax.all_to_all(f2.reshape(peer_total, 3, slot_cap, 128), ('xa', 'xb'), sp...  5.49 us
    pallas_call x1, Pallas kernels, local(): pl.pallas_call(pack_kernel, out_shape=(jax.ShapeDtypeStruct((block_total,...  4.12 us
    pallas_call x1, Pallas kernels, local(): pl.pallas_call(functools.partial(back_kernel, slot_cap), out_shape=(jax.S...  3.94 us
    unnamed x17, local copies, waits for them, and re-layouts  3.74 us
  transfers between devices with their start and end apart: 4, of which 2 were waited for; matrix products, arithmetic and copies ran while one was open for 5% of the time, Pallas kernels for 0%

profile of v13, /device:TPU:64, one launch (start us, length us, event | category | flops | bytes accessed | tf_op | source)
XLA Modules:
  0.0 79.5 jit_solution(7041079594170306228)
XLA Ops:
  0.6 0.8 %slice_reduce_fusion = (s32[16,32]{1,0:T(8,128)S(1)}, s32[16,32]{1,0:T(8,128)S(1)}) fusion(s32[1,1,16,32,2]{3,4,2,1,0:T(2,128)} %param.10), kind=kLoop, calls=%fused_computation.14 | loop fusion | bytes 8192 | tf_op jit(solution)/shard_map/slice | solution.py:271
  1.5 0.7 reshape_squeeze.6.mine_ref
  2.1 0.0 copy-start.7
  2.1 0.7 reshape_squeeze.7.their_ref
  2.8 0.0 copy-done.7
  2.8 0.6 reshape.29.anc_ref
  3.4 4.1 %shard_map.77 = (f32[256,4,128]{2,1,0:T(4,128)}, f32[2048,128]{1,0:T(8,128)}) custom-call(f32[768]{0:T(1024)} %reshape.29.anc_ref, s32[256]{0:T(256)} %bitcast.14, s32[512]{0:T(512)} %reshape_squeeze.6.mine_ref, s32[512]{0:T(512)} %reshape_squeeze.7.their_ref, s32[16]{0:T(128)} %bitcast.12, f32[3,256,128]{2,1,0:T(8,128)} %disp_ref.3), custom_call_target="tpu_custom_call" | custom-call | tf_op jit(solution)/shard_map/pallas_call | solution.py:274
  7.5 0.0 copy-start
  7.5 8.0 %all-to-all-start = ((f32[16,4,32,128]{3,2,1,0:T(8,128)}), f32[16,4,32,128]{3,2,1,0:T(8,128)S(1)}, u32[]{:S(2)}, u32[]{:S(2)}) async-start(f32[16,4,32,128]{3,2,1,0:T(8,128)} %bitcast.9), calls=%async_computation | async-start | bytes 2097152 | tf_op jit(solution)/shard_map/all_to_all | solution.py:284
  15.6 0.0 copy-done
  15.6 0.2 fusion.8
  15.8 1.9 %collective-permute-start = (f32[3,256,2]{2,1,0:T(8,128)S(1)}, f32[3,256,2]{2,1,0:T(8,128)S(1)}, u32[]{:S(2)}, u32[]{:S(2)}) collective-permute-start(f32[3,256,2]{2,1,0:T(8,128)S(1)} %get-tuple-element.13), channel_id=1, source_target_pairs={{0,16},{16,32},{32,48},{48,64},{64,80},{80,96},{96,112},{112,128},... | collective-permute-start | bytes 18440 | tf_op jit(solution)/shard_map/ppermute | solution.py:26
  17.7 3.6 %collective-permute-start.1 = (f32[3,256,2]{2,1,0:T(8,128)S(1)}, f32[3,256,2]{2,1,0:T(8,128)S(1)}, u32[]{:S(2)}, u32[]{:S(2)}) collective-permute-start(f32[3,256,2]{2,1,0:T(8,128)S(1)} %get-tuple-element.12), channel_id=1, source_target_pairs={{16,0},{32,16},{48,32},{64,48},{80,64},{96,80},{112,96},{128,112},... | collective-permute-start | bytes 18440 | tf_op jit(solution)/shard_map/ppermute | solution.py:29
  21.4 11.8 %all-to-all-done = f32[16,4,32,128]{3,2,1,0:T(8,128)S(1)} async-done(((f32[16,4,32,128]{3,2,1,0:T(8,128)}), f32[16,4,32,128]{3,2,1,0:T(8,128)S(1)}, u32[]{:S(2)}, u32[]{:S(2)}) %all-to-all-start) | async-done | bytes 1048608 | tf_op jit(solution)/shard_map/all_to_all | solution.py:284
  33.2 0.0 copy-start.1
  33.2 0.5 fusion.6
  33.6 0.9 %fusion.7.cnt_ref = s32[16]{0:T(128)} fusion(f32[16,4,32,128]{3,2,1,0:T(8,128)S(1)} %all-to-all-done), kind=kLoop, calls=%fused_computation.13 | loop fusion | flops 16 | bytes 128 | tf_op jit(solution)/shard_map/convert_element_type | solution.py:288
  34.6 0.7 convert_element_type.15.req_ref
  35.3 0.0 collective-permute-done.low_ref
  35.3 0.0 copy-start.5
  35.3 0.0 collective-permute-done.1.high_ref
  35.3 0.0 copy-start.3
  35.3 0.0 copy-done.1
  35.3 0.7 copy-done.5
  36.0 0.1 copy-done.3
  36.1 18.6 %shard_map.78 = (f32[256,8,128]{2,1,0:T(8,128)}, f32[1536,128]{1,0:T(8,128)}) custom-call(s32[16]{0:T(128)} %fusion.7.cnt_ref, s32[512]{0:T(512)} %convert_element_type.15.req_ref, f32[256,4,128]{2,1,0:T(4,128)} %get-tuple-element.7.m_ref, f32[2048,128]{1,0:T(8,128)} %bitcast.7, f32[3,256,2]{2,1,0:T(8,128)} %copy-done.5, f32[3,256,2]{2,1,0:T(8,128)} %copy-done.3), custom_call_target="tpu_custom_call" | custom-call | tf_op jit(solution)/shard_map/pallas_call | solution.py:290
  54.7 5.5 %all-to-all-start.1 = ((f32[16,3,32,128]{3,2,1,0:T(8,128)}), f32[16,3,32,128]{3,2,1,0:T(8,128)S(1)}, u32[]{:S(2)}, u32[]{:S(2)}) async-start(f32[16,3,32,128]{3,2,1,0:T(8,128)} %bitcast.11), calls=%async_computation.1 | async-start | bytes 1572864 | tf_op jit(solution)/shard_map/all_to_all | solution.py:301
  60.2 0.0 copy-start.4
  60.3 1.0 %copy-done.4 = f32[3,256,2]{2,1,0:T(8,128)S(1)} copy-done((f32[3,256,2]{2,1,0:T(8,128)S(1)}, f32[3,256,2]{2,1,0:T(8,128)}, u32[]{:S(2)}) %copy-start.4) | copy-done | bytes 6168
  61.2 0.0 copy-start.6
  61.3 1.0 %copy-done.6 = f32[3,256,2]{2,1,0:T(8,128)S(1)} copy-done((f32[3,256,2]{2,1,0:T(8,128)S(1)}, f32[3,256,2]{2,1,0:T(8,128)}, u32[]{:S(2)}) %copy-start.6) | copy-done | bytes 6168
  62.2 1.3 %fusion.3.beam_ref = f32[3,256,128]{2,1,0:T(8,128)} fusion(f32[3,256,128]{2,1,0:T(8,128)S(1)} %copy-done, f32[3,256,2]{2,1,0:T(8,128)S(1)} %copy-done.6, f32[3,256,130]{2,1,0:T(8,128)S(1)} %constant_dynamic-update-slice_fusion), kind=kLoop, calls=%fused_computation.6 | loop fusion | flops 1376256 | bytes 1579008 | tf_op jit(solution)/shard_map/sub | solution.py:41
  63.6 11.0 %all-to-all-done.1 = f32[16,3,32,128]{3,2,1,0:T(8,128)S(1)} async-done(((f32[16,3,32,128]{3,2,1,0:T(8,128)}), f32[16,3,32,128]{3,2,1,0:T(8,128)S(1)}, u32[]{:S(2)}, u32[]{:S(2)}) %all-to-all-start.1) | async-done | bytes 786464 | tf_op jit(solution)/shard_map/all_to_all | solution.py:301
  74.6 0.0 copy-start.2
  74.6 0.9 %copy-done.2 = f32[16,3,32,128]{3,2,1,0:T(8,128)} copy-done((f32[16,3,32,128]{3,2,1,0:T(8,128)}, f32[16,3,32,128]{3,2,1,0:T(8,128)S(1)}, u32[]{:S(2)}) %copy-start.2) | copy-done | bytes 786456
  75.5 3.9 %shard_map.79 = (f32[3,256,128]{2,1,0:T(8,128)}, f32[3,256,128]{2,1,0:T(8,128)}) custom-call(s32[512]{0:T(512)} %reshape_squeeze.6.mine_ref, s32[16]{0:T(128)} %bitcast.13, f32[2048,128]{1,0:T(8,128)} %bitcast.10, f32[1536,128]{1,0:T(8,128)} %bitcast.8, f32[3,256,128]{2,1,0:T(8,128)} %vel_ref.1, f32[3,256,128]{2,1,0:T(8,128)} %disp_ref.3, ...), custom_call_target="tpu_custom_call" | custom-call | tf_op jit(solution)/shard_map/pallas_call | solution.py:304
  (2 shorter events, 0.1 us)
Async XLA Ops:
  2.1 0.7 copy-start.7
  7.5 8.1 %copy-start = (f32[3,256,128]{2,1,0:T(8,128)S(1)}, f32[3,256,128]{2,1,0:T(8,128)}, u32[]{:S(2)}) copy-start(f32[3,256,128]{2,1,0:T(8,128)} %disp_ref.3) | copy-start | bytes 1179652
  7.5 25.6 %all-to-all-start = ((f32[16,4,32,128]{3,2,1,0:T(8,128)}), f32[16,4,32,128]{3,2,1,0:T(8,128)S(1)}, u32[]{:S(2)}, u32[]{:S(2)}) async-start(f32[16,4,32,128]{3,2,1,0:T(8,128)} %bitcast.9), calls=%async_computation | async-start | bytes 2097152 | tf_op jit(solution)/shard_map/all_to_all | solution.py:284
  15.8 19.5 %collective-permute-start = (f32[3,256,2]{2,1,0:T(8,128)S(1)}, f32[3,256,2]{2,1,0:T(8,128)S(1)}, u32[]{:S(2)}, u32[]{:S(2)}) collective-permute-start(f32[3,256,2]{2,1,0:T(8,128)S(1)} %get-tuple-element.13), channel_id=1, source_target_pairs={{0,16},{16,32},{32,48},{48,64},{64,80},{80,96},{96,112},{112,128},... | collective-permute-start | bytes 18440 | tf_op jit(solution)/shard_map/ppermute | solution.py:26
  17.7 17.6 %collective-permute-start.1 = (f32[3,256,2]{2,1,0:T(8,128)S(1)}, f32[3,256,2]{2,1,0:T(8,128)S(1)}, u32[]{:S(2)}, u32[]{:S(2)}) collective-permute-start(f32[3,256,2]{2,1,0:T(8,128)S(1)} %get-tuple-element.12), channel_id=1, source_target_pairs={{16,0},{32,16},{48,32},{64,48},{80,64},{96,80},{112,96},{128,112},... | collective-permute-start | bytes 18440 | tf_op jit(solution)/shard_map/ppermute | solution.py:29
  33.2 2.1 %copy-start.1 = (f32[16,4,32,128]{3,2,1,0:T(8,128)}, f32[16,4,32,128]{3,2,1,0:T(8,128)S(1)}, u32[]{:S(2)}) copy-start(f32[16,4,32,128]{3,2,1,0:T(8,128)S(1)} %all-to-all-done) | copy-start | bytes 3145732
  35.3 0.7 copy-start.5
  35.3 0.9 %copy-start.3 = (f32[3,256,2]{2,1,0:T(8,128)}, f32[3,256,2]{2,1,0:T(8,128)S(1)}, u32[]{:S(2)}) copy-start(f32[3,256,2]{2,1,0:T(8,128)S(1)} %collective-permute-done.1.high_ref) | copy-start | bytes 18436
  54.7 19.9 %all-to-all-start.1 = ((f32[16,3,32,128]{3,2,1,0:T(8,128)}), f32[16,3,32,128]{3,2,1,0:T(8,128)S(1)}, u32[]{:S(2)}, u32[]{:S(2)}) async-start(f32[16,3,32,128]{3,2,1,0:T(8,128)} %bitcast.11), calls=%async_computation.1 | async-start | bytes 1572864 | tf_op jit(solution)/shard_map/all_to_all | solution.py:301
  60.2 1.0 %copy-start.4 = (f32[3,256,2]{2,1,0:T(8,128)S(1)}, f32[3,256,2]{2,1,0:T(8,128)}, u32[]{:S(2)}) copy-start(f32[3,256,2]{2,1,0:T(8,128)} %copy-done.3) | copy-start | bytes 18436
  61.2 1.0 %copy-start.6 = (f32[3,256,2]{2,1,0:T(8,128)S(1)}, f32[3,256,2]{2,1,0:T(8,128)}, u32[]{:S(2)}) copy-start(f32[3,256,2]{2,1,0:T(8,128)} %copy-done.5) | copy-start | bytes 18436
  74.6 0.9 %copy-start.2 = (f32[16,3,32,128]{3,2,1,0:T(8,128)}, f32[16,3,32,128]{3,2,1,0:T(8,128)S(1)}, u32[]{:S(2)}) copy-start(f32[16,3,32,128]{3,2,1,0:T(8,128)S(1)} %all-to-all-done.1) | copy-start | bytes 2359300

commit v14 on v13

--- a/solution.py
+++ b/solution.py
@@ -15,7 +15,7 @@
 damping = 0.9
 masked_far = 1.0e4
 HIGH = lax.Precision.HIGH
-tile_group = 32
+tile_group = 64
 slot_step = 8
 
 

time: 81 us -> 82.2 us (1.015)
  the two profiles are of different devices: /device:TPU:64 before, /device:TPU:33 now
where the time goes in v14:
time: 82.2 us; the launch traced here: 81.7 us
  Pallas kernels  28 us (34%)
  starting transfers between devices  21.4 us (26%)
  waiting for transfers between devices  21.4 us (26%)
  local copies, waits for them, and re-layouts  7.37 us (9%)
  other arithmetic  2.74 us (3%)
    pallas_call x1, Pallas kernels, local(): pl.pallas_call(pair_kernel, out_shape=(jax.ShapeDtypeStruct((block_total,...  19.9 us
    all_to_all x1, waiting for transfers between devices, local(): lax.all_to_all(lent.reshape(peer_total, 4, slot_cap, 128), ('xa', 'xb'),...  13.3 us
    all_to_all x1, starting transfers between devices, local(): lax.all_to_all(f2.reshape(peer_total, 3, slot_cap, 128), ('xa', 'xb'), sp...  8.23 us
    all_to_all x1, waiting for transfers between devices, local(): lax.all_to_all(f2.reshape(peer_total, 3, slot_cap, 128), ('xa', 'xb'), sp...  8.07 us
    all_to_all x1, starting transfers between devices, local(): lax.all_to_all(lent.reshape(peer_total, 4, slot_cap, 128), ('xa', 'xb'),...  7.79 us
    pallas_call x1, Pallas kernels, local(): pl.pallas_call(pack_kernel, out_shape=(jax.ShapeDtypeStruct((block_total,...  4.12 us
    pallas_call x1, Pallas kernels, local(): pl.pallas_call(functools.partial(back_kernel, slot_cap), out_shape=(jax.S...  3.95 us
    unnamed x17, local copies, waits for them, and re-layouts  3.74 us
  transfers between devices with their start and end apart: 4, of which 2 were waited for; matrix products, arithmetic and copies ran while one was open for 4% of the time, Pallas kernels for 0%

profile of v14, /device:TPU:33, one launch (start us, length us, event | category | flops | bytes accessed | tf_op | source)
XLA Modules:
  0.0 81.7 jit_solution(18240199125861829729)
XLA Ops:
  0.6 0.8 %slice_reduce_fusion = (s32[16,32]{1,0:T(8,128)S(1)}, s32[16,32]{1,0:T(8,128)S(1)}) fusion(s32[1,1,16,32,2]{3,4,2,1,0:T(2,128)} %param.10), kind=kLoop, calls=%fused_computation.14 | loop fusion | bytes 8192 | tf_op jit(solution)/shard_map/slice | solution.py:271
  1.5 0.7 reshape_squeeze.6.mine_ref
  2.1 0.0 copy-start.7
  2.1 0.7 reshape_squeeze.7.their_ref
  2.8 0.0 copy-done.7
  2.8 0.6 reshape.29.anc_ref
  3.4 4.1 %shard_map.77 = (f32[256,4,128]{2,1,0:T(4,128)}, f32[2048,128]{1,0:T(8,128)}) custom-call(f32[768]{0:T(1024)} %reshape.29.anc_ref, s32[256]{0:T(256)} %bitcast.14, s32[512]{0:T(512)} %reshape_squeeze.6.mine_ref, s32[512]{0:T(512)} %reshape_squeeze.7.their_ref, s32[16]{0:T(128)} %bitcast.12, f32[3,256,128]{2,1,0:T(8,128)} %disp_ref.3), custom_call_target="tpu_custom_call" | custom-call | tf_op jit(solution)/shard_map/pallas_call | solution.py:274
  7.5 0.0 copy-start
  7.5 7.8 %all-to-all-start = ((f32[16,4,32,128]{3,2,1,0:T(8,128)}), f32[16,4,32,128]{3,2,1,0:T(8,128)S(1)}, u32[]{:S(2)}, u32[]{:S(2)}) async-start(f32[16,4,32,128]{3,2,1,0:T(8,128)} %bitcast.9), calls=%async_computation | async-start | bytes 2097152 | tf_op jit(solution)/shard_map/all_to_all | solution.py:284
  15.3 0.0 copy-done
  15.3 0.2 fusion.8
  15.5 3.5 %collective-permute-start = (f32[3,256,2]{2,1,0:T(8,128)S(1)}, f32[3,256,2]{2,1,0:T(8,128)S(1)}, u32[]{:S(2)}, u32[]{:S(2)}) collective-permute-start(f32[3,256,2]{2,1,0:T(8,128)S(1)} %get-tuple-element.13), channel_id=1, source_target_pairs={{0,16},{16,32},{32,48},{48,64},{64,80},{80,96},{96,112},{112,128},... | collective-permute-start | bytes 18440 | tf_op jit(solution)/shard_map/ppermute | solution.py:26
  19.0 1.9 %collective-permute-start.1 = (f32[3,256,2]{2,1,0:T(8,128)S(1)}, f32[3,256,2]{2,1,0:T(8,128)S(1)}, u32[]{:S(2)}, u32[]{:S(2)}) collective-permute-start(f32[3,256,2]{2,1,0:T(8,128)S(1)} %get-tuple-element.12), channel_id=1, source_target_pairs={{16,0},{32,16},{48,32},{64,48},{80,64},{96,80},{112,96},{128,112},... | collective-permute-start | bytes 18440 | tf_op jit(solution)/shard_map/ppermute | solution.py:29
  20.9 13.3 %all-to-all-done = f32[16,4,32,128]{3,2,1,0:T(8,128)S(1)} async-done(((f32[16,4,32,128]{3,2,1,0:T(8,128)}), f32[16,4,32,128]{3,2,1,0:T(8,128)S(1)}, u32[]{:S(2)}, u32[]{:S(2)}) %all-to-all-start) | async-done | bytes 1048608 | tf_op jit(solution)/shard_map/all_to_all | solution.py:284
  34.3 0.0 copy-start.1
  34.3 0.5 fusion.6
  34.7 0.9 %fusion.7.cnt_ref = s32[16]{0:T(128)} fusion(f32[16,4,32,128]{3,2,1,0:T(8,128)S(1)} %all-to-all-done), kind=kLoop, calls=%fused_computation.13 | loop fusion | flops 16 | bytes 128 | tf_op jit(solution)/shard_map/convert_element_type | solution.py:288
  35.7 0.7 convert_element_type.15.req_ref
  36.3 0.0 collective-permute-done.low_ref
  36.3 0.0 copy-start.5
  36.3 0.0 collective-permute-done.1.high_ref
  36.3 0.0 copy-start.3
  36.4 0.0 copy-done.1
  36.4 0.7 copy-done.5
  37.1 0.1 copy-done.3
  37.2 19.9 %shard_map.78 = (f32[256,8,128]{2,1,0:T(8,128)}, f32[1536,128]{1,0:T(8,128)}) custom-call(s32[16]{0:T(128)} %fusion.7.cnt_ref, s32[512]{0:T(512)} %convert_element_type.15.req_ref, f32[256,4,128]{2,1,0:T(4,128)} %get-tuple-element.7.m_ref, f32[2048,128]{1,0:T(8,128)} %bitcast.7, f32[3,256,2]{2,1,0:T(8,128)} %copy-done.5, f32[3,256,2]{2,1,0:T(8,128)} %copy-done.3), custom_call_target="tpu_custom_call" | custom-call | tf_op jit(solution)/shard_map/pallas_call | solution.py:290
  57.1 8.2 %all-to-all-start.1 = ((f32[16,3,32,128]{3,2,1,0:T(8,128)}), f32[16,3,32,128]{3,2,1,0:T(8,128)S(1)}, u32[]{:S(2)}, u32[]{:S(2)}) async-start(f32[16,3,32,128]{3,2,1,0:T(8,128)} %bitcast.11), calls=%async_computation.1 | async-start | bytes 1572864 | tf_op jit(solution)/shard_map/all_to_all | solution.py:301
  65.4 0.0 copy-start.4
  65.4 1.0 %copy-done.4 = f32[3,256,2]{2,1,0:T(8,128)S(1)} copy-done((f32[3,256,2]{2,1,0:T(8,128)S(1)}, f32[3,256,2]{2,1,0:T(8,128)}, u32[]{:S(2)}) %copy-start.4) | copy-done | bytes 6168
  66.4 0.0 copy-start.6
  66.4 1.0 %copy-done.6 = f32[3,256,2]{2,1,0:T(8,128)S(1)} copy-done((f32[3,256,2]{2,1,0:T(8,128)S(1)}, f32[3,256,2]{2,1,0:T(8,128)}, u32[]{:S(2)}) %copy-start.6) | copy-done | bytes 6168
  67.4 1.3 %fusion.3.beam_ref = f32[3,256,128]{2,1,0:T(8,128)} fusion(f32[3,256,128]{2,1,0:T(8,128)S(1)} %copy-done, f32[3,256,2]{2,1,0:T(8,128)S(1)} %copy-done.6, f32[3,256,130]{2,1,0:T(8,128)S(1)} %constant_dynamic-update-slice_fusion), kind=kLoop, calls=%fused_computation.6 | loop fusion | flops 1376256 | bytes 1579008 | tf_op jit(solution)/shard_map/sub | solution.py:41
  68.7 8.1 %all-to-all-done.1 = f32[16,3,32,128]{3,2,1,0:T(8,128)S(1)} async-done(((f32[16,3,32,128]{3,2,1,0:T(8,128)}), f32[16,3,32,128]{3,2,1,0:T(8,128)S(1)}, u32[]{:S(2)}, u32[]{:S(2)}) %all-to-all-start.1) | async-done | bytes 786464 | tf_op jit(solution)/shard_map/all_to_all | solution.py:301
  76.8 0.0 copy-start.2
  76.8 0.9 %copy-done.2 = f32[16,3,32,128]{3,2,1,0:T(8,128)} copy-done((f32[16,3,32,128]{3,2,1,0:T(8,128)}, f32[16,3,32,128]{3,2,1,0:T(8,128)S(1)}, u32[]{:S(2)}) %copy-start.2) | copy-done | bytes 786456
  77.7 3.9 %shard_map.79 = (f32[3,256,128]{2,1,0:T(8,128)}, f32[3,256,128]{2,1,0:T(8,128)}) custom-call(s32[512]{0:T(512)} %reshape_squeeze.6.mine_ref, s32[16]{0:T(128)} %bitcast.13, f32[2048,128]{1,0:T(8,128)} %bitcast.10, f32[1536,128]{1,0:T(8,128)} %bitcast.8, f32[3,256,128]{2,1,0:T(8,128)} %vel_ref.1, f32[3,256,128]{2,1,0:T(8,128)} %disp_ref.3, ...), custom_call_target="tpu_custom_call" | custom-call | tf_op jit(solution)/shard_map/pallas_call | solution.py:304
  (2 shorter events, 0.1 us)
Async XLA Ops:
  2.1 0.7 copy-start.7
  7.5 7.8 %copy-start = (f32[3,256,128]{2,1,0:T(8,128)S(1)}, f32[3,256,128]{2,1,0:T(8,128)}, u32[]{:S(2)}) copy-start(f32[3,256,128]{2,1,0:T(8,128)} %disp_ref.3) | copy-start | bytes 1179652
  7.5 26.7 %all-to-all-start = ((f32[16,4,32,128]{3,2,1,0:T(8,128)}), f32[16,4,32,128]{3,2,1,0:T(8,128)S(1)}, u32[]{:S(2)}, u32[]{:S(2)}) async-start(f32[16,4,32,128]{3,2,1,0:T(8,128)} %bitcast.9), calls=%async_computation | async-start | bytes 2097152 | tf_op jit(solution)/shard_map/all_to_all | solution.py:284
  15.5 20.8 %collective-permute-start = (f32[3,256,2]{2,1,0:T(8,128)S(1)}, f32[3,256,2]{2,1,0:T(8,128)S(1)}, u32[]{:S(2)}, u32[]{:S(2)}) collective-permute-start(f32[3,256,2]{2,1,0:T(8,128)S(1)} %get-tuple-element.13), channel_id=1, source_target_pairs={{0,16},{16,32},{32,48},{48,64},{64,80},{80,96},{96,112},{112,128},... | collective-permute-start | bytes 18440 | tf_op jit(solution)/shard_map/ppermute | solution.py:26
  19.0 17.3 %collective-permute-start.1 = (f32[3,256,2]{2,1,0:T(8,128)S(1)}, f32[3,256,2]{2,1,0:T(8,128)S(1)}, u32[]{:S(2)}, u32[]{:S(2)}) collective-permute-start(f32[3,256,2]{2,1,0:T(8,128)S(1)} %get-tuple-element.12), channel_id=1, source_target_pairs={{16,0},{32,16},{48,32},{64,48},{80,64},{96,80},{112,96},{128,112},... | collective-permute-start | bytes 18440 | tf_op jit(solution)/shard_map/ppermute | solution.py:29
  34.3 2.1 %copy-start.1 = (f32[16,4,32,128]{3,2,1,0:T(8,128)}, f32[16,4,32,128]{3,2,1,0:T(8,128)S(1)}, u32[]{:S(2)}) copy-start(f32[16,4,32,128]{3,2,1,0:T(8,128)S(1)} %all-to-all-done) | copy-start | bytes 3145732
  36.3 0.7 copy-start.5
  36.3 0.9 %copy-start.3 = (f32[3,256,2]{2,1,0:T(8,128)}, f32[3,256,2]{2,1,0:T(8,128)S(1)}, u32[]{:S(2)}) copy-start(f32[3,256,2]{2,1,0:T(8,128)S(1)} %collective-permute-done.1.high_ref) | copy-start | bytes 18436
  57.1 19.7 %all-to-all-start.1 = ((f32[16,3,32,128]{3,2,1,0:T(8,128)}), f32[16,3,32,128]{3,2,1,0:T(8,128)S(1)}, u32[]{:S(2)}, u32[]{:S(2)}) async-start(f32[16,3,32,128]{3,2,1,0:T(8,128)} %bitcast.11), calls=%async_computation.1 | async-start | bytes 1572864 | tf_op jit(solution)/shard_map/all_to_all | solution.py:301
  65.4 1.0 %copy-start.4 = (f32[3,256,2]{2,1,0:T(8,128)S(1)}, f32[3,256,2]{2,1,0:T(8,128)}, u32[]{:S(2)}) copy-start(f32[3,256,2]{2,1,0:T(8,128)} %copy-done.3) | copy-start | bytes 18436
  66.4 1.0 %copy-start.6 = (f32[3,256,2]{2,1,0:T(8,128)S(1)}, f32[3,256,2]{2,1,0:T(8,128)}, u32[]{:S(2)}) copy-start(f32[3,256,2]{2,1,0:T(8,128)} %copy-done.5) | copy-start | bytes 18436
  76.8 0.9 %copy-start.2 = (f32[16,3,32,128]{3,2,1,0:T(8,128)}, f32[16,3,32,128]{3,2,1,0:T(8,128)S(1)}, u32[]{:S(2)}) copy-start(f32[16,3,32,128]{3,2,1,0:T(8,128)S(1)} %all-to-all-done.1) | copy-start | bytes 2359300

commit v15 on v13

--- a/solution.py
+++ b/solution.py
@@ -159,8 +159,6 @@
 
     lax.fori_loop(0, blocks // slot_step, block, 0)
 
-    lent_ref[...] = jnp.zeros(lent_ref.shape, lent_ref.dtype)
-
     def peer(d, carry):
         live = cnt_ref[d]
 
@@ -183,7 +181,6 @@
 
 def pair_kernel(cnt_ref, req_ref, m_ref, rem_ref, low_ref, high_ref, f1_ref, f2_ref, lb_ref, ls_ref):
     f1_ref[...] = jnp.zeros(f1_ref.shape, f1_ref.dtype)
-    f2_ref[...] = jnp.zeros(f2_ref.shape, f2_ref.dtype)
     peers = cnt_ref.shape[0]
     cap = req_ref.shape[0] // peers
     blocks = m_ref.shape[0]

time: 81 us -> 82.9 us (1.023)
  the two profiles are of different devices: /device:TPU:64 before, /device:TPU:256 now
where the time goes in v15:
time: 82.9 us; the launch traced here: 82.4 us
  Pallas kernels  28.2 us (34%)
  starting transfers between devices  22.7 us (27%)
  waiting for transfers between devices  20.6 us (25%)
  local copies, waits for them, and re-layouts  7.37 us (9%)
  other arithmetic  2.74 us (3%)
    pallas_call x1, Pallas kernels, local(): pl.pallas_call(pair_kernel, out_shape=(jax.ShapeDtypeStruct((block_total,...  18.5 us
    all_to_all x1, waiting for transfers between devices, local(): lax.all_to_all(lent.reshape(peer_total, 4, slot_cap, 128), ('xa', 'xb'),...  10.4 us
    all_to_all x1, waiting for transfers between devices, local(): lax.all_to_all(f2.reshape(peer_total, 3, slot_cap, 128), ('xa', 'xb'), sp...  10.2 us
    all_to_all x1, starting transfers between devices, local(): lax.all_to_all(f2.reshape(peer_total, 3, slot_cap, 128), ('xa', 'xb'), sp...  8.57 us
    all_to_all x1, starting transfers between devices, local(): lax.all_to_all(lent.reshape(peer_total, 4, slot_cap, 128), ('xa', 'xb'),...  7.32 us
    pallas_call x1, Pallas kernels, local(): pl.pallas_call(pack_kernel, out_shape=(jax.ShapeDtypeStruct((block_total,...  4.89 us
    ppermute x1, starting transfers between devices, halos(): lax.ppermute(lax.slice_in_dim(block, 0, width, axis=dim), axis, backward)  4.85 us
    pallas_call x1, Pallas kernels, local(): pl.pallas_call(functools.partial(back_kernel, slot_cap), out_shape=(jax.S...  4.83 us
  transfers between devices with their start and end apart: 4, of which 2 were waited for; matrix products, arithmetic and copies ran while one was open for 4% of the time, Pallas kernels for 0%

profile of v15, /device:TPU:256, one launch (start us, length us, event | category | flops | bytes accessed | tf_op | source)
XLA Modules:
  0.0 82.4 jit_solution(12980660042444135157)
XLA Ops:
  0.6 0.8 %slice_reduce_fusion = (s32[16,32]{1,0:T(8,128)S(1)}, s32[16,32]{1,0:T(8,128)S(1)}) fusion(s32[1,1,16,32,2]{3,4,2,1,0:T(2,128)} %param.10), kind=kLoop, calls=%fused_computation.14 | loop fusion | bytes 8192 | tf_op jit(solution)/shard_map/slice | solution.py:268
  1.5 0.7 reshape_squeeze.6.mine_ref
  2.1 0.0 copy-start.7
  2.1 0.7 reshape_squeeze.7.their_ref
  2.8 0.0 copy-done.7
  2.8 0.6 reshape.29.anc_ref
  3.4 4.9 %shard_map.77 = (f32[256,4,128]{2,1,0:T(4,128)}, f32[2048,128]{1,0:T(8,128)}) custom-call(f32[768]{0:T(1024)} %reshape.29.anc_ref, s32[256]{0:T(256)} %bitcast.14, s32[512]{0:T(512)} %reshape_squeeze.6.mine_ref, s32[512]{0:T(512)} %reshape_squeeze.7.their_ref, s32[16]{0:T(128)} %bitcast.12, f32[3,256,128]{2,1,0:T(8,128)} %disp_ref.3), custom_call_target="tpu_custom_call" | custom-call | tf_op jit(solution)/shard_map/pallas_call | solution.py:271
  8.3 0.0 copy-start
  8.3 7.3 %all-to-all-start = ((f32[16,4,32,128]{3,2,1,0:T(8,128)}), f32[16,4,32,128]{3,2,1,0:T(8,128)S(1)}, u32[]{:S(2)}, u32[]{:S(2)}) async-start(f32[16,4,32,128]{3,2,1,0:T(8,128)} %bitcast.9), calls=%async_computation | async-start | bytes 2097152 | tf_op jit(solution)/shard_map/all_to_all | solution.py:281
  15.6 0.0 copy-done
  15.6 0.2 fusion.8
  15.8 1.9 %collective-permute-start = (f32[3,256,2]{2,1,0:T(8,128)S(1)}, f32[3,256,2]{2,1,0:T(8,128)S(1)}, u32[]{:S(2)}, u32[]{:S(2)}) collective-permute-start(f32[3,256,2]{2,1,0:T(8,128)S(1)} %get-tuple-element.13), channel_id=1, source_target_pairs={{0,16},{16,32},{32,48},{48,64},{64,80},{80,96},{96,112},{112,128},... | collective-permute-start | bytes 18440 | tf_op jit(solution)/shard_map/ppermute | solution.py:26
  17.8 4.9 %collective-permute-start.1 = (f32[3,256,2]{2,1,0:T(8,128)S(1)}, f32[3,256,2]{2,1,0:T(8,128)S(1)}, u32[]{:S(2)}, u32[]{:S(2)}) collective-permute-start(f32[3,256,2]{2,1,0:T(8,128)S(1)} %get-tuple-element.12), channel_id=1, source_target_pairs={{16,0},{32,16},{48,32},{64,48},{80,64},{96,80},{112,96},{128,112},... | collective-permute-start | bytes 18440 | tf_op jit(solution)/shard_map/ppermute | solution.py:29
  22.6 10.4 %all-to-all-done = f32[16,4,32,128]{3,2,1,0:T(8,128)S(1)} async-done(((f32[16,4,32,128]{3,2,1,0:T(8,128)}), f32[16,4,32,128]{3,2,1,0:T(8,128)S(1)}, u32[]{:S(2)}, u32[]{:S(2)}) %all-to-all-start) | async-done | bytes 1048608 | tf_op jit(solution)/shard_map/all_to_all | solution.py:281
  33.0 0.0 copy-start.1
  33.0 0.5 fusion.6
  33.5 0.9 %fusion.7.cnt_ref = s32[16]{0:T(128)} fusion(f32[16,4,32,128]{3,2,1,0:T(8,128)S(1)} %all-to-all-done), kind=kLoop, calls=%fused_computation.13 | loop fusion | flops 16 | bytes 128 | tf_op jit(solution)/shard_map/convert_element_type | solution.py:285
  34.4 0.7 convert_element_type.15.req_ref
  35.1 0.0 collective-permute-done.low_ref
  35.1 0.0 copy-start.5
  35.1 0.0 collective-permute-done.1.high_ref
  35.1 0.0 copy-start.3
  35.1 0.0 copy-done.1
  35.1 0.7 copy-done.5
  35.8 0.1 copy-done.3
  36.0 18.5 %shard_map.78 = (f32[256,8,128]{2,1,0:T(8,128)}, f32[1536,128]{1,0:T(8,128)}) custom-call(s32[16]{0:T(128)} %fusion.7.cnt_ref, s32[512]{0:T(512)} %convert_element_type.15.req_ref, f32[256,4,128]{2,1,0:T(4,128)} %get-tuple-element.7.m_ref, f32[2048,128]{1,0:T(8,128)} %bitcast.7, f32[3,256,2]{2,1,0:T(8,128)} %copy-done.5, f32[3,256,2]{2,1,0:T(8,128)} %copy-done.3), custom_call_target="tpu_custom_call" | custom-call | tf_op jit(solution)/shard_map/pallas_call | solution.py:287
  54.5 8.6 %all-to-all-start.1 = ((f32[16,3,32,128]{3,2,1,0:T(8,128)}), f32[16,3,32,128]{3,2,1,0:T(8,128)S(1)}, u32[]{:S(2)}, u32[]{:S(2)}) async-start(f32[16,3,32,128]{3,2,1,0:T(8,128)} %bitcast.11), calls=%async_computation.1 | async-start | bytes 1572864 | tf_op jit(solution)/shard_map/all_to_all | solution.py:298
  63.0 0.0 copy-start.4
  63.1 1.0 %copy-done.4 = f32[3,256,2]{2,1,0:T(8,128)S(1)} copy-done((f32[3,256,2]{2,1,0:T(8,128)S(1)}, f32[3,256,2]{2,1,0:T(8,128)}, u32[]{:S(2)}) %copy-start.4) | copy-done | bytes 6168
  64.0 0.0 copy-start.6
  64.1 1.0 %copy-done.6 = f32[3,256,2]{2,1,0:T(8,128)S(1)} copy-done((f32[3,256,2]{2,1,0:T(8,128)S(1)}, f32[3,256,2]{2,1,0:T(8,128)}, u32[]{:S(2)}) %copy-start.6) | copy-done | bytes 6168
  65.0 1.3 %fusion.3.beam_ref = f32[3,256,128]{2,1,0:T(8,128)} fusion(f32[3,256,128]{2,1,0:T(8,128)S(1)} %copy-done, f32[3,256,2]{2,1,0:T(8,128)S(1)} %copy-done.6, f32[3,256,130]{2,1,0:T(8,128)S(1)} %constant_dynamic-update-slice_fusion), kind=kLoop, calls=%fused_computation.6 | loop fusion | flops 1376256 | bytes 1579008 | tf_op jit(solution)/shard_map/sub | solution.py:41
  66.4 10.2 %all-to-all-done.1 = f32[16,3,32,128]{3,2,1,0:T(8,128)S(1)} async-done(((f32[16,3,32,128]{3,2,1,0:T(8,128)}), f32[16,3,32,128]{3,2,1,0:T(8,128)S(1)}, u32[]{:S(2)}, u32[]{:S(2)}) %all-to-all-start.1) | async-done | bytes 786464 | tf_op jit(solution)/shard_map/all_to_all | solution.py:298
  76.6 0.0 copy-start.2
  76.6 0.9 %copy-done.2 = f32[16,3,32,128]{3,2,1,0:T(8,128)} copy-done((f32[16,3,32,128]{3,2,1,0:T(8,128)}, f32[16,3,32,128]{3,2,1,0:T(8,128)S(1)}, u32[]{:S(2)}) %copy-start.2) | copy-done | bytes 786456
  77.5 4.8 %shard_map.79 = (f32[3,256,128]{2,1,0:T(8,128)}, f32[3,256,128]{2,1,0:T(8,128)}) custom-call(s32[512]{0:T(512)} %reshape_squeeze.6.mine_ref, s32[16]{0:T(128)} %bitcast.13, f32[2048,128]{1,0:T(8,128)} %bitcast.10, f32[1536,128]{1,0:T(8,128)} %bitcast.8, f32[3,256,128]{2,1,0:T(8,128)} %vel_ref.1, f32[3,256,128]{2,1,0:T(8,128)} %disp_ref.3, ...), custom_call_target="tpu_custom_call" | custom-call | tf_op jit(solution)/shard_map/pallas_call | solution.py:301
  (2 shorter events, 0.1 us)
Async XLA Ops:
  2.1 0.7 copy-start.7
  8.3 7.3 %copy-start = (f32[3,256,128]{2,1,0:T(8,128)S(1)}, f32[3,256,128]{2,1,0:T(8,128)}, u32[]{:S(2)}) copy-start(f32[3,256,128]{2,1,0:T(8,128)} %disp_ref.3) | copy-start | bytes 1179652
  8.3 24.7 %all-to-all-start = ((f32[16,4,32,128]{3,2,1,0:T(8,128)}), f32[16,4,32,128]{3,2,1,0:T(8,128)S(1)}, u32[]{:S(2)}, u32[]{:S(2)}) async-start(f32[16,4,32,128]{3,2,1,0:T(8,128)} %bitcast.9), calls=%async_computation | async-start | bytes 2097152 | tf_op jit(solution)/shard_map/all_to_all | solution.py:281
  15.8 19.3 %collective-permute-start = (f32[3,256,2]{2,1,0:T(8,128)S(1)}, f32[3,256,2]{2,1,0:T(8,128)S(1)}, u32[]{:S(2)}, u32[]{:S(2)}) collective-permute-start(f32[3,256,2]{2,1,0:T(8,128)S(1)} %get-tuple-element.13), channel_id=1, source_target_pairs={{0,16},{16,32},{32,48},{48,64},{64,80},{80,96},{96,112},{112,128},... | collective-permute-start | bytes 18440 | tf_op jit(solution)/shard_map/ppermute | solution.py:26
  17.8 17.3 %collective-permute-start.1 = (f32[3,256,2]{2,1,0:T(8,128)S(1)}, f32[3,256,2]{2,1,0:T(8,128)S(1)}, u32[]{:S(2)}, u32[]{:S(2)}) collective-permute-start(f32[3,256,2]{2,1,0:T(8,128)S(1)} %get-tuple-element.12), channel_id=1, source_target_pairs={{16,0},{32,16},{48,32},{64,48},{80,64},{96,80},{112,96},{128,112},... | collective-permute-start | bytes 18440 | tf_op jit(solution)/shard_map/ppermute | solution.py:29
  33.0 2.1 %copy-start.1 = (f32[16,4,32,128]{3,2,1,0:T(8,128)}, f32[16,4,32,128]{3,2,1,0:T(8,128)S(1)}, u32[]{:S(2)}) copy-start(f32[16,4,32,128]{3,2,1,0:T(8,128)S(1)} %all-to-all-done) | copy-start | bytes 3145732
  35.1 0.7 copy-start.5
  35.1 0.9 %copy-start.3 = (f32[3,256,2]{2,1,0:T(8,128)}, f32[3,256,2]{2,1,0:T(8,128)S(1)}, u32[]{:S(2)}) copy-start(f32[3,256,2]{2,1,0:T(8,128)S(1)} %collective-permute-done.1.high_ref) | copy-start | bytes 18436
  54.5 22.2 %all-to-all-start.1 = ((f32[16,3,32,128]{3,2,1,0:T(8,128)}), f32[16,3,32,128]{3,2,1,0:T(8,128)S(1)}, u32[]{:S(2)}, u32[]{:S(2)}) async-start(f32[16,3,32,128]{3,2,1,0:T(8,128)} %bitcast.11), calls=%async_computation.1 | async-start | bytes 1572864 | tf_op jit(solution)/shard_map/all_to_all | solution.py:298
  63.0 1.0 %copy-start.4 = (f32[3,256,2]{2,1,0:T(8,128)S(1)}, f32[3,256,2]{2,1,0:T(8,128)}, u32[]{:S(2)}) copy-start(f32[3,256,2]{2,1,0:T(8,128)} %copy-done.3) | copy-start | bytes 18436
  64.0 1.0 %copy-start.6 = (f32[3,256,2]{2,1,0:T(8,128)S(1)}, f32[3,256,2]{2,1,0:T(8,128)}, u32[]{:S(2)}) copy-start(f32[3,256,2]{2,1,0:T(8,128)} %copy-done.5) | copy-start | bytes 18436
  76.6 0.9 %copy-start.2 = (f32[16,3,32,128]{3,2,1,0:T(8,128)}, f32[16,3,32,128]{3,2,1,0:T(8,128)S(1)}, u32[]{:S(2)}) copy-start(f32[16,3,32,128]{3,2,1,0:T(8,128)S(1)} %all-to-all-done.1) | copy-start | bytes 2359300

commit v16 on v13

--- a/solution.py
+++ b/solution.py
@@ -16,7 +16,7 @@
 masked_far = 1.0e4
 HIGH = lax.Precision.HIGH
 tile_group = 32
-slot_step = 8
+slot_step = 16
 
 
 def halos(block, axis, dim, width):

time: 81 us -> 83.8 us (1.035)
  the two profiles are of different devices: /device:TPU:64 before, /device:TPU:129 now
where the time goes in v16:
time: 83.8 us; the launch traced here: 83.1 us
  Pallas kernels  25.4 us (30%)
  starting transfers between devices  24.8 us (30%)
  waiting for transfers between devices  22 us (26%)
  local copies, waits for them, and re-layouts  7.37 us (9%)
  other arithmetic  2.74 us (3%)
    pallas_call x1, Pallas kernels, local(): pl.pallas_call(pair_kernel, out_shape=(jax.ShapeDtypeStruct((block_total,...  16 us
    all_to_all x1, waiting for transfers between devices, local(): lax.all_to_all(lent.reshape(peer_total, 4, slot_cap, 128), ('xa', 'xb'),...  12.6 us
    all_to_all x1, starting transfers between devices, local(): lax.all_to_all(f2.reshape(peer_total, 3, slot_cap, 128), ('xa', 'xb'), sp...  11.2 us
    all_to_all x1, waiting for transfers between devices, local(): lax.all_to_all(f2.reshape(peer_total, 3, slot_cap, 128), ('xa', 'xb'), sp...  9.36 us
    all_to_all x1, starting transfers between devices, local(): lax.all_to_all(lent.reshape(peer_total, 4, slot_cap, 128), ('xa', 'xb'),...  7.65 us
    pallas_call x1, Pallas kernels, local(): pl.pallas_call(pack_kernel, out_shape=(jax.ShapeDtypeStruct((block_total,...  4.75 us
    pallas_call x1, Pallas kernels, local(): pl.pallas_call(functools.partial(back_kernel, slot_cap), out_shape=(jax.S...  4.73 us
    ppermute x1, starting transfers between devices, halos(): lax.ppermute(lax.slice_in_dim(block, block.shape[dim] - width, None, axis...  4.05 us
  transfers between devices with their start and end apart: 4, of which 2 were waited for; matrix products, arithmetic and copies ran while one was open for 4% of the time, Pallas kernels for 0%

profile of v16, /device:TPU:129, one launch (start us, length us, event | category | flops | bytes accessed | tf_op | source)
XLA Modules:
  0.0 83.1 jit_solution(16260357747005788441)
XLA Ops:
  0.6 0.8 %slice_reduce_fusion = (s32[16,32]{1,0:T(8,128)S(1)}, s32[16,32]{1,0:T(8,128)S(1)}) fusion(s32[1,1,16,32,2]{3,4,2,1,0:T(2,128)} %param.10), kind=kLoop, calls=%fused_computation.14 | loop fusion | bytes 8192 | tf_op jit(solution)/shard_map/slice | solution.py:271
  1.5 0.7 reshape_squeeze.6.mine_ref
  2.1 0.0 copy-start.7
  2.1 0.7 reshape_squeeze.7.their_ref
  2.8 0.0 copy-done.7
  2.8 0.6 reshape.29.anc_ref
  3.4 4.7 %shard_map.77 = (f32[256,4,128]{2,1,0:T(4,128)}, f32[2048,128]{1,0:T(8,128)}) custom-call(f32[768]{0:T(1024)} %reshape.29.anc_ref, s32[256]{0:T(256)} %bitcast.14, s32[512]{0:T(512)} %reshape_squeeze.6.mine_ref, s32[512]{0:T(512)} %reshape_squeeze.7.their_ref, s32[16]{0:T(128)} %bitcast.12, f32[3,256,128]{2,1,0:T(8,128)} %disp_ref.3), custom_call_target="tpu_custom_call" | custom-call | tf_op jit(solution)/shard_map/pallas_call | solution.py:274
  8.2 0.0 copy-start
  8.2 7.6 %all-to-all-start = ((f32[16,4,32,128]{3,2,1,0:T(8,128)}), f32[16,4,32,128]{3,2,1,0:T(8,128)S(1)}, u32[]{:S(2)}, u32[]{:S(2)}) async-start(f32[16,4,32,128]{3,2,1,0:T(8,128)} %bitcast.9), calls=%async_computation | async-start | bytes 2097152 | tf_op jit(solution)/shard_map/all_to_all | solution.py:284
  15.8 0.0 copy-done
  15.8 0.2 fusion.8
  16.0 4.0 %collective-permute-start = (f32[3,256,2]{2,1,0:T(8,128)S(1)}, f32[3,256,2]{2,1,0:T(8,128)S(1)}, u32[]{:S(2)}, u32[]{:S(2)}) collective-permute-start(f32[3,256,2]{2,1,0:T(8,128)S(1)} %get-tuple-element.13), channel_id=1, source_target_pairs={{0,16},{16,32},{32,48},{48,64},{64,80},{80,96},{96,112},{112,128},... | collective-permute-start | bytes 18440 | tf_op jit(solution)/shard_map/ppermute | solution.py:26
  20.1 1.9 %collective-permute-start.1 = (f32[3,256,2]{2,1,0:T(8,128)S(1)}, f32[3,256,2]{2,1,0:T(8,128)S(1)}, u32[]{:S(2)}, u32[]{:S(2)}) collective-permute-start(f32[3,256,2]{2,1,0:T(8,128)S(1)} %get-tuple-element.12), channel_id=1, source_target_pairs={{16,0},{32,16},{48,32},{64,48},{80,64},{96,80},{112,96},{128,112},... | collective-permute-start | bytes 18440 | tf_op jit(solution)/shard_map/ppermute | solution.py:29
  22.0 12.6 %all-to-all-done = f32[16,4,32,128]{3,2,1,0:T(8,128)S(1)} async-done(((f32[16,4,32,128]{3,2,1,0:T(8,128)}), f32[16,4,32,128]{3,2,1,0:T(8,128)S(1)}, u32[]{:S(2)}, u32[]{:S(2)}) %all-to-all-start) | async-done | bytes 1048608 | tf_op jit(solution)/shard_map/all_to_all | solution.py:284
  34.6 0.0 copy-start.1
  34.6 0.5 fusion.6
  35.1 0.9 %fusion.7.cnt_ref = s32[16]{0:T(128)} fusion(f32[16,4,32,128]{3,2,1,0:T(8,128)S(1)} %all-to-all-done), kind=kLoop, calls=%fused_computation.13 | loop fusion | flops 16 | bytes 128 | tf_op jit(solution)/shard_map/convert_element_type | solution.py:288
  36.0 0.7 convert_element_type.15.req_ref
  36.7 0.0 collective-permute-done.low_ref
  36.7 0.0 copy-start.5
  36.7 0.0 collective-permute-done.1.high_ref
  36.7 0.0 copy-start.3
  36.7 0.0 copy-done.1
  36.7 0.7 copy-done.5
  37.5 0.1 copy-done.3
  37.6 16.0 %shard_map.78 = (f32[256,8,128]{2,1,0:T(8,128)}, f32[1536,128]{1,0:T(8,128)}) custom-call(s32[16]{0:T(128)} %fusion.7.cnt_ref, s32[512]{0:T(512)} %convert_element_type.15.req_ref, f32[256,4,128]{2,1,0:T(4,128)} %get-tuple-element.7.m_ref, f32[2048,128]{1,0:T(8,128)} %bitcast.7, f32[3,256,2]{2,1,0:T(8,128)} %copy-done.5, f32[3,256,2]{2,1,0:T(8,128)} %copy-done.3), custom_call_target="tpu_custom_call" | custom-call | tf_op jit(solution)/shard_map/pallas_call | solution.py:290
  53.5 11.2 %all-to-all-start.1 = ((f32[16,3,32,128]{3,2,1,0:T(8,128)}), f32[16,3,32,128]{3,2,1,0:T(8,128)S(1)}, u32[]{:S(2)}, u32[]{:S(2)}) async-start(f32[16,3,32,128]{3,2,1,0:T(8,128)} %bitcast.11), calls=%async_computation.1 | async-start | bytes 1572864 | tf_op jit(solution)/shard_map/all_to_all | solution.py:301
  64.8 0.0 copy-start.4
  64.8 1.0 %copy-done.4 = f32[3,256,2]{2,1,0:T(8,128)S(1)} copy-done((f32[3,256,2]{2,1,0:T(8,128)S(1)}, f32[3,256,2]{2,1,0:T(8,128)}, u32[]{:S(2)}) %copy-start.4) | copy-done | bytes 6168
  65.8 0.0 copy-start.6
  65.8 1.0 %copy-done.6 = f32[3,256,2]{2,1,0:T(8,128)S(1)} copy-done((f32[3,256,2]{2,1,0:T(8,128)S(1)}, f32[3,256,2]{2,1,0:T(8,128)}, u32[]{:S(2)}) %copy-start.6) | copy-done | bytes 6168
  66.8 1.3 %fusion.3.beam_ref = f32[3,256,128]{2,1,0:T(8,128)} fusion(f32[3,256,128]{2,1,0:T(8,128)S(1)} %copy-done, f32[3,256,2]{2,1,0:T(8,128)S(1)} %copy-done.6, f32[3,256,130]{2,1,0:T(8,128)S(1)} %constant_dynamic-update-slice_fusion), kind=kLoop, calls=%fused_computation.6 | loop fusion | flops 1376256 | bytes 1579008 | tf_op jit(solution)/shard_map/sub | solution.py:41
  68.1 9.4 %all-to-all-done.1 = f32[16,3,32,128]{3,2,1,0:T(8,128)S(1)} async-done(((f32[16,3,32,128]{3,2,1,0:T(8,128)}), f32[16,3,32,128]{3,2,1,0:T(8,128)S(1)}, u32[]{:S(2)}, u32[]{:S(2)}) %all-to-all-start.1) | async-done | bytes 786464 | tf_op jit(solution)/shard_map/all_to_all | solution.py:301
  77.5 0.0 copy-start.2
  77.5 0.9 %copy-done.2 = f32[16,3,32,128]{3,2,1,0:T(8,128)} copy-done((f32[16,3,32,128]{3,2,1,0:T(8,128)}, f32[16,3,32,128]{3,2,1,0:T(8,128)S(1)}, u32[]{:S(2)}) %copy-start.2) | copy-done | bytes 786456
  78.4 4.7 %shard_map.79 = (f32[3,256,128]{2,1,0:T(8,128)}, f32[3,256,128]{2,1,0:T(8,128)}) custom-call(s32[512]{0:T(512)} %reshape_squeeze.6.mine_ref, s32[16]{0:T(128)} %bitcast.13, f32[2048,128]{1,0:T(8,128)} %bitcast.10, f32[1536,128]{1,0:T(8,128)} %bitcast.8, f32[3,256,128]{2,1,0:T(8,128)} %vel_ref.1, f32[3,256,128]{2,1,0:T(8,128)} %disp_ref.3, ...), custom_call_target="tpu_custom_call" | custom-call | tf_op jit(solution)/shard_map/pallas_call | solution.py:304
  (2 shorter events, 0.1 us)
Async XLA Ops:
  2.1 0.7 copy-start.7
  8.2 7.7 %copy-start = (f32[3,256,128]{2,1,0:T(8,128)S(1)}, f32[3,256,128]{2,1,0:T(8,128)}, u32[]{:S(2)}) copy-start(f32[3,256,128]{2,1,0:T(8,128)} %disp_ref.3) | copy-start | bytes 1179652
  8.2 26.5 %all-to-all-start = ((f32[16,4,32,128]{3,2,1,0:T(8,128)}), f32[16,4,32,128]{3,2,1,0:T(8,128)S(1)}, u32[]{:S(2)}, u32[]{:S(2)}) async-start(f32[16,4,32,128]{3,2,1,0:T(8,128)} %bitcast.9), calls=%async_computation | async-start | bytes 2097152 | tf_op jit(solution)/shard_map/all_to_all | solution.py:284
  16.0 20.7 %collective-permute-start = (f32[3,256,2]{2,1,0:T(8,128)S(1)}, f32[3,256,2]{2,1,0:T(8,128)S(1)}, u32[]{:S(2)}, u32[]{:S(2)}) collective-permute-start(f32[3,256,2]{2,1,0:T(8,128)S(1)} %get-tuple-element.13), channel_id=1, source_target_pairs={{0,16},{16,32},{32,48},{48,64},{64,80},{80,96},{96,112},{112,128},... | collective-permute-start | bytes 18440 | tf_op jit(solution)/shard_map/ppermute | solution.py:26
  20.1 16.7 %collective-permute-start.1 = (f32[3,256,2]{2,1,0:T(8,128)S(1)}, f32[3,256,2]{2,1,0:T(8,128)S(1)}, u32[]{:S(2)}, u32[]{:S(2)}) collective-permute-start(f32[3,256,2]{2,1,0:T(8,128)S(1)} %get-tuple-element.12), channel_id=1, source_target_pairs={{16,0},{32,16},{48,32},{64,48},{80,64},{96,80},{112,96},{128,112},... | collective-permute-start | bytes 18440 | tf_op jit(solution)/shard_map/ppermute | solution.py:29
  34.6 2.1 %copy-start.1 = (f32[16,4,32,128]{3,2,1,0:T(8,128)}, f32[16,4,32,128]{3,2,1,0:T(8,128)S(1)}, u32[]{:S(2)}) copy-start(f32[16,4,32,128]{3,2,1,0:T(8,128)S(1)} %all-to-all-done) | copy-start | bytes 3145732
  36.7 0.7 copy-start.5
  36.7 0.9 %copy-start.3 = (f32[3,256,2]{2,1,0:T(8,128)}, f32[3,256,2]{2,1,0:T(8,128)S(1)}, u32[]{:S(2)}) copy-start(f32[3,256,2]{2,1,0:T(8,128)S(1)} %collective-permute-done.1.high_ref) | copy-start | bytes 18436
  53.5 23.9 %all-to-all-start.1 = ((f32[16,3,32,128]{3,2,1,0:T(8,128)}), f32[16,3,32,128]{3,2,1,0:T(8,128)S(1)}, u32[]{:S(2)}, u32[]{:S(2)}) async-start(f32[16,3,32,128]{3,2,1,0:T(8,128)} %bitcast.11), calls=%async_computation.1 | async-start | bytes 1572864 | tf_op jit(solution)/shard_map/all_to_all | solution.py:301
  64.8 1.0 %copy-start.4 = (f32[3,256,2]{2,1,0:T(8,128)S(1)}, f32[3,256,2]{2,1,0:T(8,128)}, u32[]{:S(2)}) copy-start(f32[3,256,2]{2,1,0:T(8,128)} %copy-done.3) | copy-start | bytes 18436
  65.8 1.0 %copy-start.6 = (f32[3,256,2]{2,1,0:T(8,128)S(1)}, f32[3,256,2]{2,1,0:T(8,128)}, u32[]{:S(2)}) copy-start(f32[3,256,2]{2,1,0:T(8,128)} %copy-done.5) | copy-start | bytes 18436
  77.5 0.9 %copy-start.2 = (f32[16,3,32,128]{3,2,1,0:T(8,128)}, f32[16,3,32,128]{3,2,1,0:T(8,128)S(1)}, u32[]{:S(2)}) copy-start(f32[16,3,32,128]{3,2,1,0:T(8,128)S(1)} %all-to-all-done.1) | copy-start | bytes 2359300
